TPU v7x, 128 devices: a whole 4x4x4 slice. The times are simulated.
128 devices in a mesh: gx: 16 (over z, y), gy: 8 (over x, core).
Axes of the slice: x: 4, y: 4, z: 4, core: 2. Of those that a mesh axis runs over, the one named last changes fastest.
Arguments:
- tile_sums: bfloat16 [16384, 5, 16384], P(('gx', 'gy')), may hold values from -180 to 180
- tile_dest: int32 [16384], P(('gx', 'gy')), may hold values from 0 to 127, as said below
- tile_place: int32 [16384], P(('gx', 'gy')), may hold values from 0 to 15
- tile_count: int32 [128], P(('gx', 'gy')), may hold values from 64 to 128, as said below
Outputs:
- smoothed: float32 [5, 16, 1024, 2048], P(None, 'gx', 'gy')
Inputs may be any that keep to these rules, and one draw needn't show every extreme that they name: `tile_dest`: each DEM device's 128 records name every filter device exactly once. Only the first tile_count[d] slots of device d are live; some device has all 128 live and some has half.
All inputs are finite; a program needn't handle non-finite values.
Results may differ from a plain program's by a relative error of at most 0.0003.
Values may be sent and summed in bfloat16 or wider, within the bound.
No kernel may reach another device: no remote copies, remote signals or barrier semaphores. Data moves between devices by JAX's collectives and lax.ppermute only.
A program may use at most 192 MiB of HBM per device.

v0:
```python
import math

import jax
import jax.numpy as jnp
import numpy as np
from jax import lax
from jax.sharding import PartitionSpec as P

TE = 32
BX = 4
BY = 4
RADIUS = 4
HIGHEST = lax.Precision.HIGHEST


def gauss_taps():
    spread = RADIUS * 5.0 / 16.0
    raw_taps = [
        math.exp(-(offset * offset) / (2.0 * spread * spread))
        for offset in range(-RADIUS, RADIUS + 1)
    ]
    total_weight = sum(raw_taps)
    return [value / total_weight for value in raw_taps]


def band(length_in, length_out, shift):
    taps = gauss_taps()
    mat = np.zeros((length_in, length_out), np.float32)
    for j in range(length_out):
        for k in range(2 * RADIUS + 1):
            i = j + shift + k - RADIUS
            if 0 <= i < length_in:
                mat[i, j] = taps[k]
    return jnp.asarray(mat)


def halo(cells, axis, dim, width):
    count = lax.axis_size(axis)
    ends = count - 1
    head = lax.slice_in_dim(cells, 0, width, axis=dim)
    tail = lax.slice_in_dim(cells, cells.shape[dim] - width, cells.shape[dim], axis=dim)
    return jnp.concatenate(
        [
            lax.ppermute(tail, axis, [(i, (i + 1) % count) for i in range(ends)]),
            cells,
            lax.ppermute(head, axis, [((i + 1) % count, i) for i in range(ends)]),
        ],
        axis=dim,
    )


def local(tile_sums, tile_dest, tile_place, tile_count):
    slot_count, fields, cells = tile_sums.shape
    planes = cells // (TE * TE)
    across = lax.axis_size("gx")
    column_count = lax.axis_size("gy")
    peer_count = across * column_count
    targets = jnp.arange(peer_count, dtype=jnp.int32)
    pick = (tile_dest[None, :] == targets[:, None]).astype(jnp.bfloat16)
    table = jnp.stack([tile_dest, tile_place, jnp.broadcast_to(tile_count, (slot_count,))])
    every = lax.all_gather(table, ("gx", "gy"))
    every_dest, every_place, every_count = every[:, 0], every[:, 1], every[:, 2, 0]
    me = lax.axis_index("gx") * column_count + lax.axis_index("gy")
    slots = jnp.arange(slot_count, dtype=jnp.int32)
    mine = (every_dest == me) & (slots[None, :] < every_count[:, None])
    in_place = jnp.sum(jnp.where(mine, every_place + 1, 0), axis=1) - 1
    local_ids = jnp.arange(BX * BY, dtype=jnp.int32)
    landing = (in_place[None, :] == local_ids[:, None]).astype(jnp.bfloat16)
    height = BY * TE
    width = BX * TE
    wz = band(planes, planes, 0)
    wy = band(height + 2 * RADIUS, height, RADIUS)
    rows = cells // 128

    def send(f):
        record = tile_sums[:, f, :]
        outgoing = jnp.dot(pick, record, preferred_element_type=jnp.float32).astype(jnp.bfloat16)
        outgoing = outgoing.reshape(peer_count, rows, 128)
        return lax.all_to_all(outgoing, ("gx", "gy"), 0, 0, tiled=True)

    def proc(incoming):
        deposited = jnp.einsum("ts,src->trc", landing, incoming, preferred_element_type=jnp.float32)
        deposited = deposited.reshape(BY, BX, planes, TE, TE).transpose(2, 0, 3, 1, 4)
        deposited = deposited.reshape(planes, height, width)
        along_z = jnp.einsum("io,iyx->oyx", wz, deposited, precision=HIGHEST)
        padded = halo(along_z, "gy", 1, RADIUS)
        return jnp.einsum("iy,zix->zyx", wy, padded, precision=HIGHEST)

    def gather_x(along_y):
        return lax.all_to_all(along_y, "gx", 1, 3, tiled=True)

    def along_x(slab):
        count = slab.shape[0]
        blocks = slab.reshape(count * height, across, width)
        edge = jnp.zeros((count * height, 1, width), blocks.dtype)
        padded = jnp.concatenate([edge, blocks, edge], axis=1)
        result = jnp.einsum("rjx,xo->rjo", padded[:, 1 : across + 1], w_mid, precision=HIGHEST)
        result = result + jnp.einsum("rjx,xo->rjo", padded[:, 0:across], w_left, precision=HIGHEST)
        result = result + jnp.einsum("rjx,xo->rjo", padded[:, 2 : across + 2], w_right, precision=HIGHEST)
        return result.reshape(slab.shape)

    w_mid = band(width, width, 0)
    w_left = band(width, width, width)
    w_right = band(width, width, -width)
    smoothed = []
    incoming = send(0)
    for f in range(fields - 1):
        following = send(f + 1)
        smoothed.append(proc(incoming))
        incoming = following
    first = gather_x(jnp.stack(smoothed, axis=0))
    last = proc(incoming)
    last = gather_x(last[None])
    first = along_x(first)
    result = jnp.zeros((fields,) + first.shape[1:], first.dtype)
    result = lax.dynamic_update_slice_in_dim(result, first, 0, axis=0)
    return lax.dynamic_update_slice_in_dim(result, along_x(last), fields - 1, axis=0)


def solution(mesh):
    return jax.shard_map(
        local,
        mesh=mesh,
        in_specs=(P(("gx", "gy"), None, None), P(("gx", "gy")), P(("gx", "gy")), P(("gx", "gy"))),
        out_specs=P(None, "gx", "gy", None),
        check_vma=False,
    )
```

profile of v0, /device:TPU:4, one launch (start us, length us, event | category | flops | bytes accessed | tf_op | source)
XLA Modules:
  0.0 597.2 jit_solution(16179481397044923640)
XLA Ops:
  6.7 11.0 %all-to-all-start.2 = ((bf16[128,128,128]{2,1,0:T(8,128)(2,1)}), bf16[128,128,128]{2,1,0:T(8,128)(2,1)}, u32[]{:S(2)}, u32[]{:S(2)}) async-start(bf16[128,128,128]{2,1,0:T(8,128)(2,1)} %bitcast.163), calls=%async_computation.2 | async-start | bytes 8388608 | tf_op jit(solution)/shard_map/all_to_all | solution.py:79
  24.3 43.9 %all-to-all-done.2 = bf16[128,128,128]{2,1,0:T(8,128)(2,1)} async-done(((bf16[128,128,128]{2,1,0:T(8,128)(2,1)}), bf16[128,128,128]{2,1,0:T(8,128)(2,1)}, u32[]{:S(2)}, u32[]{:S(2)}) %all-to-all-start.2) | async-done | bytes 4194336 | tf_op jit(solution)/shard_map/all_to_all | solution.py:79
  68.3 7.5 %all-to-all-start.1 = ((bf16[128,128,128]{2,1,0:T(8,128)(2,1)}), bf16[128,128,128]{2,1,0:T(8,128)(2,1)}, u32[]{:S(2)}, u32[]{:S(2)}) async-start(bf16[128,128,128]{2,1,0:T(8,128)(2,1)} %bitcast.161), calls=%async_computation.1 | async-start | bytes 8388608 | tf_op jit(solution)/shard_map/all_to_all | solution.py:79
  82.5 44.0 %all-to-all-done.1 = bf16[128,128,128]{2,1,0:T(8,128)(2,1)} async-done(((bf16[128,128,128]{2,1,0:T(8,128)(2,1)}), bf16[128,128,128]{2,1,0:T(8,128)(2,1)}, u32[]{:S(2)}, u32[]{:S(2)}) %all-to-all-start.1) | async-done | bytes 4194336 | tf_op jit(solution)/shard_map/all_to_all | solution.py:79
  126.5 7.5 %all-to-all-start = ((bf16[128,128,128]{2,1,0:T(8,128)(2,1)}), bf16[128,128,128]{2,1,0:T(8,128)(2,1)}, u32[]{:S(2)}, u32[]{:S(2)}) async-start(bf16[128,128,128]{2,1,0:T(8,128)(2,1)} %bitcast.162), calls=%async_computation | async-start | bytes 8388608 | tf_op jit(solution)/shard_map/all_to_all | solution.py:79
  140.7 44.1 %all-to-all-done = bf16[128,128,128]{2,1,0:T(8,128)(2,1)} async-done(((bf16[128,128,128]{2,1,0:T(8,128)(2,1)}), bf16[128,128,128]{2,1,0:T(8,128)(2,1)}, u32[]{:S(2)}, u32[]{:S(2)}) %all-to-all-start) | async-done | bytes 4194336 | tf_op jit(solution)/shard_map/all_to_all | solution.py:79
  184.8 7.9 %all-to-all-start.3 = ((bf16[128,128,128]{2,1,0:T(8,128)(2,1)}), bf16[128,128,128]{2,1,0:T(8,128)(2,1)}, u32[]{:S(2)}, u32[]{:S(2)}) async-start(bf16[128,128,128]{2,1,0:T(8,128)(2,1)} %bitcast.160), calls=%async_computation.3 | async-start | bytes 8388608 | tf_op jit(solution)/shard_map/all_to_all | solution.py:79
  200.1 43.1 %all-to-all-done.3 = bf16[128,128,128]{2,1,0:T(8,128)(2,1)} async-done(((bf16[128,128,128]{2,1,0:T(8,128)(2,1)}), bf16[128,128,128]{2,1,0:T(8,128)(2,1)}, u32[]{:S(2)}, u32[]{:S(2)}) %all-to-all-start.3) | async-done | bytes 4194336 | tf_op jit(solution)/shard_map/all_to_all | solution.py:79
  243.2 7.7 %all-to-all-start.5 = ((bf16[128,128,128]{2,1,0:T(8,128)(2,1)}), bf16[128,128,128]{2,1,0:T(8,128)(2,1)}, u32[]{:S(2)}, u32[]{:S(2)}) async-start(bf16[128,128,128]{2,1,0:T(8,128)(2,1)} %bitcast.159), calls=%async_computation.5 | async-start | bytes 8388608 | tf_op jit(solution)/shard_map/all_to_all | solution.py:79
  251.0 75.6 %all-gather.1 = s32[128,3,128]{2,1,0:T(4,128)S(1)} all-gather(s32[1,3,128]{2,1,0:T(4,128)S(1)} %add_bitcast_fusion), channel_id=2, replica_groups=mesh['gx'=16,'gy'=8] {'gx','gy'}, dimensions={0}, use_global_device_ids=true | all-gather | bytes 198144 | tf_op jit(solution)/shard_map/all_gather | solution.py:61
  329.2 4.5 fusion.9
  336.6 6.9 %copy.139 = f32[16,4,32,4,32]{4,3,0,2,1:T(4,128)} copy(f32[16,4,32,4,32]{4,2,0,3,1:T(8,128)} %bitcast.154) | data formatting | bytes 2097152 | tf_op jit(solution)/shard_map/reshape | solution.py:84
  361.5 6.8 %copy.138 = f32[16,4,32,4,32]{4,3,0,2,1:T(4,128)} copy(f32[16,4,32,4,32]{4,2,0,3,1:T(8,128)} %bitcast.155) | data formatting | bytes 2097152 | tf_op jit(solution)/shard_map/reshape | solution.py:84
  382.5 6.8 %copy.137 = f32[16,4,32,4,32]{4,3,0,2,1:T(4,128)} copy(f32[16,4,32,4,32]{4,2,0,3,1:T(8,128)} %bitcast.156) | data formatting | bytes 2097152 | tf_op jit(solution)/shard_map/reshape | solution.py:84
  402.7 6.9 %copy.140 = f32[16,4,32,4,32]{4,3,0,2,1:T(4,128)} copy(f32[16,4,32,4,32]{4,2,0,3,1:T(8,128)} %bitcast.157) | data formatting | bytes 2097152 | tf_op jit(solution)/shard_map/reshape | solution.py:84
  409.6 4.9 reshape.106
  428.9 6.8 %copy.144 = f32[16,4,32,4,32]{4,3,0,2,1:T(4,128)} copy(f32[16,4,32,4,32]{4,2,0,3,1:T(8,128)} %bitcast.158) | data formatting | bytes 2097152 | tf_op jit(solution)/shard_map/reshape | solution.py:84
  435.8 4.6 reshape.107
  490.6 7.0 %all-to-all-start.4 = ((f32[4,16,128,128]{2,3,0,1:T(8,128)}), f32[4,16,128,128]{2,3,0,1:T(8,128)}, u32[]{:S(2)}, u32[]{:S(2)}) async-start(f32[4,16,128,128]{2,3,0,1:T(8,128)} %copy.116), calls=%async_computation.4 | async-start | bytes 8388608 | tf_op jit(solution)/shard_map/all_to_all | solution.py:90
  502.9 61.7 %all-to-all-done.4 = f32[4,16,128,128]{2,3,0,1:T(8,128)} async-done(((f32[4,16,128,128]{2,3,0,1:T(8,128)}), f32[4,16,128,128]{2,3,0,1:T(8,128)}, u32[]{:S(2)}, u32[]{:S(2)}) %all-to-all-start.4) | async-done | bytes 4194336 | tf_op jit(solution)/shard_map/all_to_all | solution.py:90
  564.5 5.3 copy.141
  569.9 5.6 fusion.72
  586.8 4.9 reshape.84
  591.7 5.1 maximum_bitcast_fusion
  (106 shorter events, 165.2 us)
Async XLA Ops:
  6.7 11.0 %copy-start.8 = (s32[128]{0:T(128)S(1)}, s32[128]{0:T(128)}, u32[]{:S(2)}) copy-start(s32[128]{0:T(128)} %param.10) | copy-start | bytes 1540
  6.7 61.6 %all-to-all-start.2 = ((bf16[128,128,128]{2,1,0:T(8,128)(2,1)}), bf16[128,128,128]{2,1,0:T(8,128)(2,1)}, u32[]{:S(2)}, u32[]{:S(2)}) async-start(bf16[128,128,128]{2,1,0:T(8,128)(2,1)} %bitcast.163), calls=%async_computation.2 | async-start | bytes 8388608 | tf_op jit(solution)/shard_map/all_to_all | solution.py:79
  68.3 58.2 %all-to-all-start.1 = ((bf16[128,128,128]{2,1,0:T(8,128)(2,1)}), bf16[128,128,128]{2,1,0:T(8,128)(2,1)}, u32[]{:S(2)}, u32[]{:S(2)}) async-start(bf16[128,128,128]{2,1,0:T(8,128)(2,1)} %bitcast.161), calls=%async_computation.1 | async-start | bytes 8388608 | tf_op jit(solution)/shard_map/all_to_all | solution.py:79
  126.5 58.3 %all-to-all-start = ((bf16[128,128,128]{2,1,0:T(8,128)(2,1)}), bf16[128,128,128]{2,1,0:T(8,128)(2,1)}, u32[]{:S(2)}, u32[]{:S(2)}) async-start(bf16[128,128,128]{2,1,0:T(8,128)(2,1)} %bitcast.162), calls=%async_computation | async-start | bytes 8388608 | tf_op jit(solution)/shard_map/all_to_all | solution.py:79
  184.8 58.5 %all-to-all-start.3 = ((bf16[128,128,128]{2,1,0:T(8,128)(2,1)}), bf16[128,128,128]{2,1,0:T(8,128)(2,1)}, u32[]{:S(2)}, u32[]{:S(2)}) async-start(bf16[128,128,128]{2,1,0:T(8,128)(2,1)} %bitcast.160), calls=%async_computation.3 | async-start | bytes 8388608 | tf_op jit(solution)/shard_map/all_to_all | solution.py:79
  243.2 7.7 %copy-start.9 = (s32[128]{0:T(128)S(1)}, s32[128]{0:T(128)}, u32[]{:S(2)}) copy-start(s32[128]{0:T(128)} %param.11) | copy-start | bytes 1540
  243.2 176.2 %all-to-all-start.5 = ((bf16[128,128,128]{2,1,0:T(8,128)(2,1)}), bf16[128,128,128]{2,1,0:T(8,128)(2,1)}, u32[]{:S(2)}, u32[]{:S(2)}) async-start(bf16[128,128,128]{2,1,0:T(8,128)(2,1)} %bitcast.159), calls=%async_computation.5 | async-start | bytes 8388608 | tf_op jit(solution)/shard_map/all_to_all | solution.py:79
  348.2 113.9 %collective-permute-start.4 = (f32[16,4,128]{2,0,1:T(8,128)S(1)}, f32[16,4,128]{2,0,1:T(8,128)S(1)}, u32[]{:S(2)}, u32[]{:S(2)}) collective-permute-start(f32[16,4,128]{2,0,1:T(8,128)S(1)} %get-tuple-element.9), channel_id=1, source_target_pairs={{0,1},{1,2},{2,3},{3,4},{4,5},{5,6},{6,7},{8,9},{9,10},{10,11},{11... | collective-permute-start | bytes 98312 | tf_op jit(solution)/shard_map/ppermute | solution.py:44
  350.5 115.4 %collective-permute-start.5 = (f32[16,4,128]{2,0,1:T(8,128)S(1)}, f32[16,4,128]{2,0,1:T(8,128)S(1)}, u32[]{:S(2)}, u32[]{:S(2)}) collective-permute-start(f32[16,4,128]{2,0,1:T(8,128)S(1)} %get-tuple-element.10), channel_id=1, source_target_pairs={{1,0},{2,1},{3,2},{4,3},{5,4},{6,5},{7,6},{9,8},{10,9},{11,10},{12... | collective-permute-start | bytes 98312 | tf_op jit(solution)/shard_map/ppermute | solution.py:46
  373.1 94.8 %collective-permute-start.2 = (f32[16,4,128]{2,0,1:T(8,128)S(1)}, f32[16,4,128]{2,0,1:T(8,128)S(1)}, u32[]{:S(2)}, u32[]{:S(2)}) collective-permute-start(f32[16,4,128]{2,0,1:T(8,128)S(1)} %get-tuple-element.7), channel_id=1, source_target_pairs={{0,1},{1,2},{2,3},{3,4},{4,5},{5,6},{6,7},{8,9},{9,10},{10,11},{11... | collective-permute-start | bytes 98312 | tf_op jit(solution)/shard_map/ppermute | solution.py:44
  435.8 17.4 %copy-start.3 = (f32[136,128,1]{1,0,2:T(8,128)S(1)}, f32[136,128,1]{1,0,2:T(8,128)}, u32[]{:S(2)}) copy-start(f32[136,128,1]{1,0,2:T(8,128)} %constant.48) | copy-start | bytes 208900
  442.6 6.2 %collective-permute-start.8 = (f32[16,4,128]{2,0,1:T(8,128)S(1)}, f32[16,4,128]{2,0,1:T(8,128)S(1)}, u32[]{:S(2)}, u32[]{:S(2)}) collective-permute-start(f32[16,4,128]{2,0,1:T(8,128)S(1)} %get-tuple-element.13), channel_id=1, source_target_pairs={{0,1},{1,2},{2,3},{3,4},{4,5},{5,6},{6,7},{8,9},{9,10},{10,11},{11... | collective-permute-start | bytes 98312 | tf_op jit(solution)/shard_map/ppermute | solution.py:44
  445.5 5.6 collective-permute-start.9
  448.8 23.0 %collective-permute-start.3 = (f32[16,4,128]{2,0,1:T(8,128)S(1)}, f32[16,4,128]{2,0,1:T(8,128)S(1)}, u32[]{:S(2)}, u32[]{:S(2)}) collective-permute-start(f32[16,4,128]{2,0,1:T(8,128)S(1)} %get-tuple-element.8), channel_id=1, source_target_pairs={{1,0},{2,1},{3,2},{4,3},{5,4},{6,5},{7,6},{9,8},{10,9},{11,10},{12... | collective-permute-start | bytes 98312 | tf_op jit(solution)/shard_map/ppermute | solution.py:46
  451.2 20.6 %collective-permute-start = (f32[16,4,128]{2,0,1:T(8,128)}, f32[16,4,128]{2,0,1:T(8,128)S(1)}, u32[]{:S(2)}, u32[]{:S(2)}) collective-permute-start(f32[16,4,128]{2,0,1:T(8,128)} %get-tuple-element.5), channel_id=1, source_target_pairs={{0,1},{1,2},{2,3},{3,4},{4,5},{5,6},{6,7},{8,9},{9,10},{10,11},{11... | collective-permute-start | bytes 98312 | tf_op jit(solution)/shard_map/ppermute | solution.py:44
  457.7 32.9 %all-to-all-start.6 = ((f32[1,16,128,128]{2,3,0,1:T(8,128)}), f32[1,16,128,128]{2,3,0,1:T(8,128)}, u32[]{:S(2)}, u32[]{:S(2)}) async-start(f32[1,16,128,128]{2,3,0,1:T(8,128)} %convolution_bitcast_fusion), calls=%async_computation.6 | async-start | bytes 2097152 | tf_op jit(solution)/shard_map/all_to_all | solution.py:90
  462.1 9.8 %copy-start.2 = (f32[16,128,128]{2,0,1:T(8,128)S(1)}, f32[16,128,128]{2,0,1:T(8,128)}, u32[]{:S(2)}) copy-start(f32[16,128,128]{2,0,1:T(8,128)} %copy-done.1) | copy-start | bytes 3145732
  462.1 9.7 %collective-permute-start.1 = (f32[16,4,128]{2,0,1:T(8,128)S(1)}, f32[16,4,128]{2,0,1:T(8,128)S(1)}, u32[]{:S(2)}, u32[]{:S(2)}) collective-permute-start(f32[16,4,128]{2,0,1:T(8,128)S(1)} %get-tuple-element.6), channel_id=1, source_target_pairs={{1,0},{2,1},{3,2},{4,3},{5,4},{6,5},{7,6},{9,8},{10,9},{11,10},{12... | collective-permute-start | bytes 98312 | tf_op jit(solution)/shard_map/ppermute | solution.py:46
  465.9 6.1 %collective-permute-start.6 = (f32[16,4,128]{2,0,1:T(8,128)}, f32[16,4,128]{2,0,1:T(8,128)S(1)}, u32[]{:S(2)}, u32[]{:S(2)}) collective-permute-start(f32[16,4,128]{2,0,1:T(8,128)} %get-tuple-element.11), channel_id=1, source_target_pairs={{0,1},{1,2},{2,3},{3,4},{4,5},{5,6},{6,7},{8,9},{9,10},{10,11},{11... | collective-permute-start | bytes 98312 | tf_op jit(solution)/shard_map/ppermute | solution.py:44
  467.9 5.5 collective-permute-start.7
  490.6 8.6 %copy-start.6 = (f32[128,128,1]{1,0,2:T(8,128)S(1)}, f32[128,128,1]{1,0,2:T(8,128)}, u32[]{:S(2)}) copy-start(f32[128,128,1]{1,0,2:T(8,128)} %constant.49) | copy-start | bytes 196612
  490.6 73.9 %all-to-all-start.4 = ((f32[4,16,128,128]{2,3,0,1:T(8,128)}), f32[4,16,128,128]{2,3,0,1:T(8,128)}, u32[]{:S(2)}, u32[]{:S(2)}) async-start(f32[4,16,128,128]{2,3,0,1:T(8,128)} %copy.116), calls=%async_computation.4 | async-start | bytes 8388608 | tf_op jit(solution)/shard_map/all_to_all | solution.py:90
  497.7 3.8 copy-start.4
  569.9 5.6 copy-start
  (3 other events, 7.5 us)
where the time goes:
time: 607 us; the launch traced here: 597 us
  waiting for transfers between devices  238 us (39%)
  local copies, waits for them, and re-layouts  114 us (19%)
  matrix products  81.6 us (13%)
  starting transfers between devices  80.2 us (13%)
  blocking collectives  75.6 us (12%)
  other arithmetic  6.23 us (1%)
    all_to_all x5, waiting for transfers between devices, send(): return lax.all_to_all(outgoing, ('gx', 'gy'), 0, 0, tiled=True)  175 us
    all_gather x1, blocking collectives, local(): every = lax.all_gather(table, ('gx', 'gy'))  75.6 us
    all_to_all x2, waiting for transfers between devices, gather_x(): return lax.all_to_all(along_y, 'gx', 1, 3, tiled=True)  61.7 us
    reshape x10, local copies, waits for them, and re-layouts, proc(): deposited = deposited.reshape(planes, height, width)  54.9 us
    all_to_all x5, starting transfers between devices, send(): return lax.all_to_all(outgoing, ('gx', 'gy'), 0, 0, tiled=True)  41.6 us
    dot_general x5, matrix products, proc(): jnp.einsum('ts,src->trc', landing, incoming, preferred_element_type=jnp.f...  22.5 us
    dot_general x5, matrix products, proc(): return jnp.einsum('iy,zix->zyx', wy, padded, precision=HIGHEST)  18.8 us
    unnamed x25, local copies, waits for them, and re-layouts  17.3 us
  transfers between devices with their start and end apart: 17, of which 6 were waited for; matrix products, arithmetic and copies ran while one was open for 27% of the time, Pallas kernels for 0%

commit v1 on v0

--- a/solution.py
+++ b/solution.py
@@ -55,15 +55,21 @@
     across = lax.axis_size("gx")
     column_count = lax.axis_size("gy")
     peer_count = across * column_count
+    is_live = jnp.arange(slot_count, dtype=jnp.int32) < tile_count[0]
     targets = jnp.arange(peer_count, dtype=jnp.int32)
-    pick = (tile_dest[None, :] == targets[:, None]).astype(jnp.bfloat16)
-    table = jnp.stack([tile_dest, tile_place, jnp.broadcast_to(tile_count, (slot_count,))])
-    every = lax.all_gather(table, ("gx", "gy"))
-    every_dest, every_place, every_count = every[:, 0], every[:, 1], every[:, 2, 0]
-    me = lax.axis_index("gx") * column_count + lax.axis_index("gy")
-    slots = jnp.arange(slot_count, dtype=jnp.int32)
-    mine = (every_dest == me) & (slots[None, :] < every_count[:, None])
-    in_place = jnp.sum(jnp.where(mine, every_place + 1, 0), axis=1) - 1
+    chosen = tile_dest[None, :] == targets[:, None]
+    pick = chosen.astype(jnp.bfloat16)
+    out_place = jnp.sum(jnp.where(chosen & is_live[None, :], tile_place[None, :] + 1, 0), axis=1) - 1
+    rows = cells // 128
+
+    def send(f):
+        record = tile_sums[:, f, :]
+        outgoing = jnp.dot(pick, record, preferred_element_type=jnp.float32).astype(jnp.bfloat16)
+        outgoing = outgoing.reshape(peer_count, rows, 128)
+        return lax.all_to_all(outgoing, ("gx", "gy"), 0, 0, tiled=True)
+
+    incoming = send(0)
+    in_place = lax.all_to_all(out_place[:, None], ("gx", "gy"), 0, 0, tiled=True).reshape(peer_count)
     local_ids = jnp.arange(BX * BY, dtype=jnp.int32)
     landing = (in_place[None, :] == local_ids[:, None]).astype(jnp.bfloat16)
     height = BY * TE
@@ -71,12 +77,6 @@
     wz = band(planes, planes, 0)
     wy = band(height + 2 * RADIUS, height, RADIUS)
     rows = cells // 128
-
-    def send(f):
-        record = tile_sums[:, f, :]
-        outgoing = jnp.dot(pick, record, preferred_element_type=jnp.float32).astype(jnp.bfloat16)
-        outgoing = outgoing.reshape(peer_count, rows, 128)
-        return lax.all_to_all(outgoing, ("gx", "gy"), 0, 0, tiled=True)
 
     def proc(incoming):
         deposited = jnp.einsum("ts,src->trc", landing, incoming, preferred_element_type=jnp.float32)
@@ -103,7 +103,6 @@
     w_left = band(width, width, width)
     w_right = band(width, width, -width)
     smoothed = []
-    incoming = send(0)
     for f in range(fields - 1):
         following = send(f + 1)
         smoothed.append(proc(incoming))
@@ -112,9 +111,8 @@
     last = proc(incoming)
     last = gather_x(last[None])
     first = along_x(first)
-    result = jnp.zeros((fields,) + first.shape[1:], first.dtype)
-    result = lax.dynamic_update_slice_in_dim(result, first, 0, axis=0)
-    return lax.dynamic_update_slice_in_dim(result, along_x(last), fields - 1, axis=0)
+    last = along_x(last)
+    return jnp.concatenate([first, last], axis=0)
 
 
 def solution(mesh):

time: 607 us -> 546 us (0.90)
  blocking collectives: 75.6 us -> 0 us
  starting transfers between devices: 80.2 us -> 91.4 us
    all_gather x1 -> x0, blocking collectives: 75.6 us -> none  [local(): every = lax.all_gather(table, ('gx', 'gy'))]
    all_to_all x0 -> x1, starting transfers between devices: none -> 10.5 us  [local(): lax.all_to_all(out_place[:, None], ('gx', 'gy'), 0, 0, tiled=True)]
    unnamed x25 -> x23, local copies, waits for them, and re-layouts: 17.3 us -> 17.2 us
  transfers between devices with their start and end apart: 17 -> 18, of which waited for: 6 -> 7; matrix products, arithmetic and copies ran while one was open for 27% -> 31% of each run, Pallas kernels for 0% -> 0%
where the time goes in v1:
time: 546 us; the launch traced here: 536 us
  waiting for transfers between devices  240 us (44%)
  local copies, waits for them, and re-layouts  112 us (21%)
  starting transfers between devices  91.4 us (17%)
  matrix products  81.6 us (15%)
  other arithmetic  9.76 us (2%)
    all_to_all x5, waiting for transfers between devices, send(): return lax.all_to_all(outgoing, ('gx', 'gy'), 0, 0, tiled=True)  176 us
    all_to_all x2, waiting for transfers between devices, gather_x(): return lax.all_to_all(along_y, 'gx', 1, 3, tiled=True)  60.9 us
    reshape x10, local copies, waits for them, and re-layouts, proc(): deposited = deposited.reshape(planes, height, width)  54.9 us
    all_to_all x5, starting transfers between devices, send(): return lax.all_to_all(outgoing, ('gx', 'gy'), 0, 0, tiled=True)  39.4 us
    dot_general x5, matrix products, proc(): jnp.einsum('ts,src->trc', landing, incoming, preferred_element_type=jnp.f...  22.6 us
    dot_general x5, matrix products, proc(): return jnp.einsum('iy,zix->zyx', wy, padded, precision=HIGHEST)  18.8 us
    unnamed x23, local copies, waits for them, and re-layouts  17.2 us
    dot_general x5, matrix products, send(): jnp.dot(pick, record, preferred_element_type=jnp.float32)  17.2 us
  transfers between devices with their start and end apart: 18, of which 7 were waited for; matrix products, arithmetic and copies ran while one was open for 31% of the time, Pallas kernels for 0%

profile of v1, /device:TPU:4, one launch (start us, length us, event | category | flops | bytes accessed | tf_op | source)
XLA Modules:
  0.0 535.9 jit_solution(17245537624112223934)
XLA Ops:
  2.8 10.5 %all-to-all-start = ((s32[128,1,1]{2,1,0:T(1,128)}), s32[128,1,1]{2,1,0:T(1,128)S(1)}, u32[]{:S(2)}, u32[]{:S(2)}) async-start(s32[128,1,1]{2,1,0:T(1,128)} %copy.171), calls=%async_computation | async-start | bytes 131072 | tf_op jit(solution)/shard_map/all_to_all | solution.py:72
  21.4 8.9 %all-to-all-start.3 = ((bf16[128,128,128]{2,1,0:T(8,128)(2,1)}), bf16[128,128,128]{2,1,0:T(8,128)(2,1)}, u32[]{:S(2)}, u32[]{:S(2)}) async-start(bf16[128,128,128]{2,1,0:T(8,128)(2,1)} %bitcast.151), calls=%async_computation.3 | async-start | bytes 8388608 | tf_op jit(solution)/shard_map/all_to_all | solution.py:69
  36.9 43.9 %all-to-all-done.3 = bf16[128,128,128]{2,1,0:T(8,128)(2,1)} async-done(((bf16[128,128,128]{2,1,0:T(8,128)(2,1)}), bf16[128,128,128]{2,1,0:T(8,128)(2,1)}, u32[]{:S(2)}, u32[]{:S(2)}) %all-to-all-start.3) | async-done | bytes 4194336 | tf_op jit(solution)/shard_map/all_to_all | solution.py:69
  80.9 7.5 %all-to-all-start.2 = ((bf16[128,128,128]{2,1,0:T(8,128)(2,1)}), bf16[128,128,128]{2,1,0:T(8,128)(2,1)}, u32[]{:S(2)}, u32[]{:S(2)}) async-start(bf16[128,128,128]{2,1,0:T(8,128)(2,1)} %bitcast.152), calls=%async_computation.2 | async-start | bytes 8388608 | tf_op jit(solution)/shard_map/all_to_all | solution.py:69
  95.1 44.0 %all-to-all-done.2 = bf16[128,128,128]{2,1,0:T(8,128)(2,1)} async-done(((bf16[128,128,128]{2,1,0:T(8,128)(2,1)}), bf16[128,128,128]{2,1,0:T(8,128)(2,1)}, u32[]{:S(2)}, u32[]{:S(2)}) %all-to-all-start.2) | async-done | bytes 4194336 | tf_op jit(solution)/shard_map/all_to_all | solution.py:69
  139.1 7.5 %all-to-all-start.1 = ((bf16[128,128,128]{2,1,0:T(8,128)(2,1)}), bf16[128,128,128]{2,1,0:T(8,128)(2,1)}, u32[]{:S(2)}, u32[]{:S(2)}) async-start(bf16[128,128,128]{2,1,0:T(8,128)(2,1)} %bitcast.153), calls=%async_computation.1 | async-start | bytes 8388608 | tf_op jit(solution)/shard_map/all_to_all | solution.py:69
  153.3 44.1 %all-to-all-done.1 = bf16[128,128,128]{2,1,0:T(8,128)(2,1)} async-done(((bf16[128,128,128]{2,1,0:T(8,128)(2,1)}), bf16[128,128,128]{2,1,0:T(8,128)(2,1)}, u32[]{:S(2)}, u32[]{:S(2)}) %all-to-all-start.1) | async-done | bytes 4194336 | tf_op jit(solution)/shard_map/all_to_all | solution.py:69
  197.4 7.9 %all-to-all-start.4 = ((bf16[128,128,128]{2,1,0:T(8,128)(2,1)}), bf16[128,128,128]{2,1,0:T(8,128)(2,1)}, u32[]{:S(2)}, u32[]{:S(2)}) async-start(bf16[128,128,128]{2,1,0:T(8,128)(2,1)} %bitcast.154), calls=%async_computation.4 | async-start | bytes 8388608 | tf_op jit(solution)/shard_map/all_to_all | solution.py:69
  212.0 43.8 %all-to-all-done.4 = bf16[128,128,128]{2,1,0:T(8,128)(2,1)} async-done(((bf16[128,128,128]{2,1,0:T(8,128)(2,1)}), bf16[128,128,128]{2,1,0:T(8,128)(2,1)}, u32[]{:S(2)}, u32[]{:S(2)}) %all-to-all-start.4) | async-done | bytes 4194336 | tf_op jit(solution)/shard_map/all_to_all | solution.py:69
  255.9 7.5 %all-to-all-start.6 = ((bf16[128,128,128]{2,1,0:T(8,128)(2,1)}), bf16[128,128,128]{2,1,0:T(8,128)(2,1)}, u32[]{:S(2)}, u32[]{:S(2)}) async-start(bf16[128,128,128]{2,1,0:T(8,128)(2,1)} %bitcast.150), calls=%async_computation.6 | async-start | bytes 8388608 | tf_op jit(solution)/shard_map/all_to_all | solution.py:69
  273.1 6.9 %copy.215 = f32[16,4,32,4,32]{4,3,0,2,1:T(4,128)} copy(f32[16,4,32,4,32]{4,2,0,3,1:T(8,128)} %bitcast.145) | data formatting | bytes 2097152 | tf_op jit(solution)/shard_map/reshape | solution.py:84
  298.0 6.8 %copy.214 = f32[16,4,32,4,32]{4,3,0,2,1:T(4,128)} copy(f32[16,4,32,4,32]{4,2,0,3,1:T(8,128)} %bitcast.146) | data formatting | bytes 2097152 | tf_op jit(solution)/shard_map/reshape | solution.py:84
  319.0 6.8 %copy.213 = f32[16,4,32,4,32]{4,3,0,2,1:T(4,128)} copy(f32[16,4,32,4,32]{4,2,0,3,1:T(8,128)} %bitcast.147) | data formatting | bytes 2097152 | tf_op jit(solution)/shard_map/reshape | solution.py:84
  339.2 6.9 %copy.216 = f32[16,4,32,4,32]{4,3,0,2,1:T(4,128)} copy(f32[16,4,32,4,32]{4,2,0,3,1:T(8,128)} %bitcast.148) | data formatting | bytes 2097152 | tf_op jit(solution)/shard_map/reshape | solution.py:84
  346.1 4.9 reshape.111
  365.4 6.8 %copy.220 = f32[16,4,32,4,32]{4,3,0,2,1:T(4,128)} copy(f32[16,4,32,4,32]{4,2,0,3,1:T(8,128)} %bitcast.149) | data formatting | bytes 2097152 | tf_op jit(solution)/shard_map/reshape | solution.py:84
  372.3 4.6 reshape.112
  394.2 7.5 %all-to-all-start.7 = ((f32[1,16,128,128]{2,3,0,1:T(8,128)}), f32[1,16,128,128]{2,3,0,1:T(8,128)}, u32[]{:S(2)}, u32[]{:S(2)}) async-start(f32[1,16,128,128]{2,3,0,1:T(8,128)} %convolution_bitcast_fusion), calls=%async_computation.7 | async-start | bytes 2097152 | tf_op jit(solution)/shard_map/all_to_all | solution.py:90
  430.0 7.1 %all-to-all-start.5 = ((f32[4,16,128,128]{2,3,0,1:T(8,128)}), f32[4,16,128,128]{2,3,0,1:T(8,128)}, u32[]{:S(2)}, u32[]{:S(2)}) async-start(f32[4,16,128,128]{2,3,0,1:T(8,128)} %copy.192), calls=%async_computation.5 | async-start | bytes 8388608 | tf_op jit(solution)/shard_map/all_to_all | solution.py:90
  442.3 60.9 %all-to-all-done.5 = f32[4,16,128,128]{2,3,0,1:T(8,128)} async-done(((f32[4,16,128,128]{2,3,0,1:T(8,128)}), f32[4,16,128,128]{2,3,0,1:T(8,128)}, u32[]{:S(2)}, u32[]{:S(2)}) %all-to-all-start.5) | async-done | bytes 4194336 | tf_op jit(solution)/shard_map/all_to_all | solution.py:90
  503.2 5.3 copy.217
  508.6 5.6 %fusion.70 = f32[512,16,128]{2,0,1:T(8,128)S(1)} fusion(f32[512,16,128]{2,0,1:T(8,128)} %bitcast.142, f32[128,128,1]{1,0,2:T(8,128)S(1)} %copy-done.6), kind=kOutput, calls=%fused_computation.81 | convolution fusion | flops 1610612736 | bytes 8454144 | tf_op jit(solution)/shard_map/rjx,xo->rjo/dot_general | solution.py:97
  525.5 4.9 reshape.93
  530.4 5.1 maximum_bitcast_fusion
  (105 shorter events, 168.2 us)
Async XLA Ops:
  2.8 18.6 %all-to-all-start = ((s32[128,1,1]{2,1,0:T(1,128)}), s32[128,1,1]{2,1,0:T(1,128)S(1)}, u32[]{:S(2)}, u32[]{:S(2)}) async-start(s32[128,1,1]{2,1,0:T(1,128)} %copy.171), calls=%async_computation | async-start | bytes 131072 | tf_op jit(solution)/shard_map/all_to_all | solution.py:72
  21.4 8.9 %copy-start.8 = (s32[128]{0:T(128)S(1)}, s32[128]{0:T(128)}, u32[]{:S(2)}) copy-start(s32[128]{0:T(128)} %param.10) | copy-start | bytes 1540
  21.4 59.5 %all-to-all-start.3 = ((bf16[128,128,128]{2,1,0:T(8,128)(2,1)}), bf16[128,128,128]{2,1,0:T(8,128)(2,1)}, u32[]{:S(2)}, u32[]{:S(2)}) async-start(bf16[128,128,128]{2,1,0:T(8,128)(2,1)} %bitcast.151), calls=%async_computation.3 | async-start | bytes 8388608 | tf_op jit(solution)/shard_map/all_to_all | solution.py:69
  80.9 58.2 %all-to-all-start.2 = ((bf16[128,128,128]{2,1,0:T(8,128)(2,1)}), bf16[128,128,128]{2,1,0:T(8,128)(2,1)}, u32[]{:S(2)}, u32[]{:S(2)}) async-start(bf16[128,128,128]{2,1,0:T(8,128)(2,1)} %bitcast.152), calls=%async_computation.2 | async-start | bytes 8388608 | tf_op jit(solution)/shard_map/all_to_all | solution.py:69
  139.1 58.3 %all-to-all-start.1 = ((bf16[128,128,128]{2,1,0:T(8,128)(2,1)}), bf16[128,128,128]{2,1,0:T(8,128)(2,1)}, u32[]{:S(2)}, u32[]{:S(2)}) async-start(bf16[128,128,128]{2,1,0:T(8,128)(2,1)} %bitcast.153), calls=%async_computation.1 | async-start | bytes 8388608 | tf_op jit(solution)/shard_map/all_to_all | solution.py:69
  197.4 58.5 %all-to-all-start.4 = ((bf16[128,128,128]{2,1,0:T(8,128)(2,1)}), bf16[128,128,128]{2,1,0:T(8,128)(2,1)}, u32[]{:S(2)}, u32[]{:S(2)}) async-start(bf16[128,128,128]{2,1,0:T(8,128)(2,1)} %bitcast.154), calls=%async_computation.4 | async-start | bytes 8388608 | tf_op jit(solution)/shard_map/all_to_all | solution.py:69
  255.9 100.1 %all-to-all-start.6 = ((bf16[128,128,128]{2,1,0:T(8,128)(2,1)}), bf16[128,128,128]{2,1,0:T(8,128)(2,1)}, u32[]{:S(2)}, u32[]{:S(2)}) async-start(bf16[128,128,128]{2,1,0:T(8,128)(2,1)} %bitcast.150), calls=%async_computation.6 | async-start | bytes 8388608 | tf_op jit(solution)/shard_map/all_to_all | solution.py:69
  284.7 117.0 %collective-permute-start.4 = (f32[16,4,128]{2,0,1:T(8,128)S(1)}, f32[16,4,128]{2,0,1:T(8,128)S(1)}, u32[]{:S(2)}, u32[]{:S(2)}) collective-permute-start(f32[16,4,128]{2,0,1:T(8,128)S(1)} %get-tuple-element.9), channel_id=1, source_target_pairs={{0,1},{1,2},{2,3},{3,4},{4,5},{5,6},{6,7},{8,9},{9,10},{10,11},{11... | collective-permute-start | bytes 98312 | tf_op jit(solution)/shard_map/ppermute | solution.py:44
  286.8 118.5 %collective-permute-start.5 = (f32[16,4,128]{2,0,1:T(8,128)S(1)}, f32[16,4,128]{2,0,1:T(8,128)S(1)}, u32[]{:S(2)}, u32[]{:S(2)}) collective-permute-start(f32[16,4,128]{2,0,1:T(8,128)S(1)} %get-tuple-element.10), channel_id=1, source_target_pairs={{1,0},{2,1},{3,2},{4,3},{5,4},{6,5},{7,6},{9,8},{10,9},{11,10},{12... | collective-permute-start | bytes 98312 | tf_op jit(solution)/shard_map/ppermute | solution.py:46
  309.6 97.7 %collective-permute-start.2 = (f32[16,4,128]{2,0,1:T(8,128)S(1)}, f32[16,4,128]{2,0,1:T(8,128)S(1)}, u32[]{:S(2)}, u32[]{:S(2)}) collective-permute-start(f32[16,4,128]{2,0,1:T(8,128)S(1)} %get-tuple-element.7), channel_id=1, source_target_pairs={{0,1},{1,2},{2,3},{3,4},{4,5},{5,6},{6,7},{8,9},{9,10},{10,11},{11... | collective-permute-start | bytes 98312 | tf_op jit(solution)/shard_map/ppermute | solution.py:44
  372.3 17.4 %copy-start.3 = (f32[136,128,1]{1,0,2:T(8,128)S(1)}, f32[136,128,1]{1,0,2:T(8,128)}, u32[]{:S(2)}) copy-start(f32[136,128,1]{1,0,2:T(8,128)} %constant.35) | copy-start | bytes 208900
  379.1 6.2 %collective-permute-start.8 = (f32[16,4,128]{2,0,1:T(8,128)S(1)}, f32[16,4,128]{2,0,1:T(8,128)S(1)}, u32[]{:S(2)}, u32[]{:S(2)}) collective-permute-start(f32[16,4,128]{2,0,1:T(8,128)S(1)} %get-tuple-element.13), channel_id=1, source_target_pairs={{0,1},{1,2},{2,3},{3,4},{4,5},{5,6},{6,7},{8,9},{9,10},{10,11},{11... | collective-permute-start | bytes 98312 | tf_op jit(solution)/shard_map/ppermute | solution.py:44
  382.3 5.4 %collective-permute-start.9 = (f32[16,4,128]{2,0,1:T(8,128)S(1)}, f32[16,4,128]{2,0,1:T(8,128)S(1)}, u32[]{:S(2)}, u32[]{:S(2)}) collective-permute-start(f32[16,4,128]{2,0,1:T(8,128)S(1)} %get-tuple-element.14), channel_id=1, source_target_pairs={{1,0},{2,1},{3,2},{4,3},{5,4},{6,5},{7,6},{9,8},{10,9},{11,10},{12... | collective-permute-start | bytes 98312 | tf_op jit(solution)/shard_map/ppermute | solution.py:46
  385.3 25.8 %collective-permute-start.3 = (f32[16,4,128]{2,0,1:T(8,128)S(1)}, f32[16,4,128]{2,0,1:T(8,128)S(1)}, u32[]{:S(2)}, u32[]{:S(2)}) collective-permute-start(f32[16,4,128]{2,0,1:T(8,128)S(1)} %get-tuple-element.8), channel_id=1, source_target_pairs={{1,0},{2,1},{3,2},{4,3},{5,4},{6,5},{7,6},{9,8},{10,9},{11,10},{12... | collective-permute-start | bytes 98312 | tf_op jit(solution)/shard_map/ppermute | solution.py:46
  387.7 23.5 %collective-permute-start = (f32[16,4,128]{2,0,1:T(8,128)}, f32[16,4,128]{2,0,1:T(8,128)S(1)}, u32[]{:S(2)}, u32[]{:S(2)}) collective-permute-start(f32[16,4,128]{2,0,1:T(8,128)} %get-tuple-element.5), channel_id=1, source_target_pairs={{0,1},{1,2},{2,3},{3,4},{4,5},{5,6},{6,7},{8,9},{9,10},{10,11},{11... | collective-permute-start | bytes 98312 | tf_op jit(solution)/shard_map/ppermute | solution.py:44
  394.2 35.8 %all-to-all-start.7 = ((f32[1,16,128,128]{2,3,0,1:T(8,128)}), f32[1,16,128,128]{2,3,0,1:T(8,128)}, u32[]{:S(2)}, u32[]{:S(2)}) async-start(f32[1,16,128,128]{2,3,0,1:T(8,128)} %convolution_bitcast_fusion), calls=%async_computation.7 | async-start | bytes 2097152 | tf_op jit(solution)/shard_map/all_to_all | solution.py:90
  401.7 9.5 %copy-start.2 = (f32[16,128,128]{2,0,1:T(8,128)S(1)}, f32[16,128,128]{2,0,1:T(8,128)}, u32[]{:S(2)}) copy-start(f32[16,128,128]{2,0,1:T(8,128)} %copy-done.1) | copy-start | bytes 3145732
  401.7 9.5 %collective-permute-start.1 = (f32[16,4,128]{2,0,1:T(8,128)S(1)}, f32[16,4,128]{2,0,1:T(8,128)S(1)}, u32[]{:S(2)}, u32[]{:S(2)}) collective-permute-start(f32[16,4,128]{2,0,1:T(8,128)S(1)} %get-tuple-element.6), channel_id=1, source_target_pairs={{1,0},{2,1},{3,2},{4,3},{5,4},{6,5},{7,6},{9,8},{10,9},{11,10},{12... | collective-permute-start | bytes 98312 | tf_op jit(solution)/shard_map/ppermute | solution.py:46
  405.2 6.1 %collective-permute-start.6 = (f32[16,4,128]{2,0,1:T(8,128)}, f32[16,4,128]{2,0,1:T(8,128)S(1)}, u32[]{:S(2)}, u32[]{:S(2)}) collective-permute-start(f32[16,4,128]{2,0,1:T(8,128)} %get-tuple-element.11), channel_id=1, source_target_pairs={{0,1},{1,2},{2,3},{3,4},{4,5},{5,6},{6,7},{8,9},{9,10},{10,11},{11... | collective-permute-start | bytes 98312 | tf_op jit(solution)/shard_map/ppermute | solution.py:44
  407.3 5.5 %collective-permute-start.7 = (f32[16,4,128]{2,0,1:T(8,128)}, f32[16,4,128]{2,0,1:T(8,128)S(1)}, u32[]{:S(2)}, u32[]{:S(2)}) collective-permute-start(f32[16,4,128]{2,0,1:T(8,128)} %get-tuple-element.12), channel_id=1, source_target_pairs={{1,0},{2,1},{3,2},{4,3},{5,4},{6,5},{7,6},{9,8},{10,9},{11,10},{12... | collective-permute-start | bytes 98312 | tf_op jit(solution)/shard_map/ppermute | solution.py:46
  430.0 8.7 %copy-start.6 = (f32[128,128,1]{1,0,2:T(8,128)S(1)}, f32[128,128,1]{1,0,2:T(8,128)}, u32[]{:S(2)}) copy-start(f32[128,128,1]{1,0,2:T(8,128)} %constant.36) | copy-start | bytes 196612
  430.0 73.2 %all-to-all-start.5 = ((f32[4,16,128,128]{2,3,0,1:T(8,128)}), f32[4,16,128,128]{2,3,0,1:T(8,128)}, u32[]{:S(2)}, u32[]{:S(2)}) async-start(f32[4,16,128,128]{2,3,0,1:T(8,128)} %copy.192), calls=%async_computation.5 | async-start | bytes 8388608 | tf_op jit(solution)/shard_map/all_to_all | solution.py:90
  437.1 3.8 copy-start.4
  508.6 5.6 %copy-start = (f32[4,16,128,128]{3,2,0,1:T(8,128)S(1)}, f32[4,16,128,128]{3,2,0,1:T(8,128)}, u32[]{:S(2)}) copy-start(f32[4,16,128,128]{3,2,0,1:T(8,128)} %copy.217) | copy-start | bytes 12582916
  (3 other events, 7.5 us)

commit v2 on v1

--- a/solution.py
+++ b/solution.py
@@ -60,16 +60,20 @@
     chosen = tile_dest[None, :] == targets[:, None]
     pick = chosen.astype(jnp.bfloat16)
     out_place = jnp.sum(jnp.where(chosen & is_live[None, :], tile_place[None, :] + 1, 0), axis=1) - 1
-    rows = cells // 128
 
     def send(f):
         record = tile_sums[:, f, :]
         outgoing = jnp.dot(pick, record, preferred_element_type=jnp.float32).astype(jnp.bfloat16)
         outgoing = outgoing.reshape(peer_count, rows, 128)
+        if f == 0:
+            marks = jnp.broadcast_to(out_place.astype(jnp.bfloat16)[:, None, None], (peer_count, 8, 128))
+            outgoing = jnp.concatenate([outgoing, marks], axis=1)
         return lax.all_to_all(outgoing, ("gx", "gy"), 0, 0, tiled=True)
 
+    rows = cells // 128
     incoming = send(0)
-    in_place = lax.all_to_all(out_place[:, None], ("gx", "gy"), 0, 0, tiled=True).reshape(peer_count)
+    in_place = incoming[:, rows, 0].astype(jnp.int32)
+    incoming = incoming[:, :rows]
     local_ids = jnp.arange(BX * BY, dtype=jnp.int32)
     landing = (in_place[None, :] == local_ids[:, None]).astype(jnp.bfloat16)
     height = BY * TE

time: 546 us -> 537 us (0.984)
  starting transfers between devices: 91.4 us -> 82.9 us
    all_to_all x1 -> x0, starting transfers between devices: 10.5 us -> none  [local(): lax.all_to_all(out_place[:, None], ('gx', 'gy'), 0, 0, tiled=True)]
    unnamed x23 -> x25, local copies, waits for them, and re-layouts: 17.2 us -> 15.2 us
  transfers between devices with their start and end apart: 18 -> 17, of which waited for: 7 -> 6; matrix products, arithmetic and copies ran while one was open for 31% -> 31% of each run, Pallas kernels for 0% -> 0%
where the time goes in v2:
time: 537 us; the launch traced here: 527 us
  waiting for transfers between devices  240 us (45%)
  local copies, waits for them, and re-layouts  112 us (21%)
  starting transfers between devices  82.9 us (15%)
  matrix products  79.4 us (15%)
  other arithmetic  12 us (2%)
    all_to_all x5, waiting for transfers between devices, send(): return lax.all_to_all(outgoing, ('gx', 'gy'), 0, 0, tiled=True)  177 us
    all_to_all x2, waiting for transfers between devices, gather_x(): return lax.all_to_all(along_y, 'gx', 1, 3, tiled=True)  60.9 us
    reshape x10, local copies, waits for them, and re-layouts, proc(): deposited = deposited.reshape(planes, height, width)  54.8 us
    all_to_all x5, starting transfers between devices, send(): return lax.all_to_all(outgoing, ('gx', 'gy'), 0, 0, tiled=True)  41.4 us
    dot_general x5, matrix products, proc(): jnp.einsum('ts,src->trc', landing, incoming, preferred_element_type=jnp.f...  20.4 us
    dot_general x5, matrix products, proc(): return jnp.einsum('iy,zix->zyx', wy, padded, precision=HIGHEST)  18.8 us
    dot_general x5, matrix products, send(): jnp.dot(pick, record, preferred_element_type=jnp.float32)  17.2 us
    ppermute x5, starting transfers between devices, halo(): lax.ppermute(head, axis, [((i + 1) % count, i) for i in range(ends)])  16 us
  transfers between devices with their start and end apart: 17, of which 6 were waited for; matrix products, arithmetic and copies ran while one was open for 31% of the time, Pallas kernels for 0%

profile of v2, /device:TPU:4, one launch (start us, length us, event | category | flops | bytes accessed | tf_op | source)
XLA Modules:
  0.0 527.1 jit_solution(1534795865805677097)
XLA Ops:
  6.7 11.0 %all-to-all-start.1 = ((bf16[128,128,128]{2,1,0:T(8,128)(2,1)}), bf16[128,128,128]{2,1,0:T(8,128)(2,1)}, u32[]{:S(2)}, u32[]{:S(2)}) async-start(bf16[128,128,128]{2,1,0:T(8,128)(2,1)} %bitcast.152), calls=%async_computation.1 | async-start | bytes 8388608 | tf_op jit(solution)/shard_map/all_to_all | solution.py:71
  24.3 43.9 %all-to-all-done.1 = bf16[128,128,128]{2,1,0:T(8,128)(2,1)} async-done(((bf16[128,128,128]{2,1,0:T(8,128)(2,1)}), bf16[128,128,128]{2,1,0:T(8,128)(2,1)}, u32[]{:S(2)}, u32[]{:S(2)}) %all-to-all-start.1) | async-done | bytes 4194336 | tf_op jit(solution)/shard_map/all_to_all | solution.py:71
  68.2 7.5 %all-to-all-start.2 = ((bf16[128,128,128]{2,1,0:T(8,128)(2,1)}), bf16[128,128,128]{2,1,0:T(8,128)(2,1)}, u32[]{:S(2)}, u32[]{:S(2)}) async-start(bf16[128,128,128]{2,1,0:T(8,128)(2,1)} %bitcast.150), calls=%async_computation.2 | async-start | bytes 8388608 | tf_op jit(solution)/shard_map/all_to_all | solution.py:71
  82.4 44.1 %all-to-all-done.2 = bf16[128,128,128]{2,1,0:T(8,128)(2,1)} async-done(((bf16[128,128,128]{2,1,0:T(8,128)(2,1)}), bf16[128,128,128]{2,1,0:T(8,128)(2,1)}, u32[]{:S(2)}, u32[]{:S(2)}) %all-to-all-start.2) | async-done | bytes 4194336 | tf_op jit(solution)/shard_map/all_to_all | solution.py:71
  126.4 7.5 %all-to-all-start.3 = ((bf16[128,128,128]{2,1,0:T(8,128)(2,1)}), bf16[128,128,128]{2,1,0:T(8,128)(2,1)}, u32[]{:S(2)}, u32[]{:S(2)}) async-start(bf16[128,128,128]{2,1,0:T(8,128)(2,1)} %bitcast.149), calls=%async_computation.3 | async-start | bytes 8388608 | tf_op jit(solution)/shard_map/all_to_all | solution.py:71
  142.3 42.4 %all-to-all-done.3 = bf16[128,128,128]{2,1,0:T(8,128)(2,1)} async-done(((bf16[128,128,128]{2,1,0:T(8,128)(2,1)}), bf16[128,128,128]{2,1,0:T(8,128)(2,1)}, u32[]{:S(2)}, u32[]{:S(2)}) %all-to-all-start.3) | async-done | bytes 4194336 | tf_op jit(solution)/shard_map/all_to_all | solution.py:71
  184.7 7.9 %all-to-all-start = ((bf16[128,136,128]{2,1,0:T(8,128)(2,1)}), bf16[128,136,128]{2,1,0:T(8,128)(2,1)}, u32[]{:S(2)}, u32[]{:S(2)}) async-start(bf16[128,136,128]{2,1,0:T(8,128)(2,1)} %pad_maximum_fusion), calls=%async_computation | async-start | bytes 8912896 | tf_op jit(solution)/shard_map/all_to_all | solution.py:71
  199.3 46.7 %all-to-all-done = bf16[128,136,128]{2,1,0:T(8,128)(2,1)} async-done(((bf16[128,136,128]{2,1,0:T(8,128)(2,1)}), bf16[128,136,128]{2,1,0:T(8,128)(2,1)}, u32[]{:S(2)}, u32[]{:S(2)}) %all-to-all-start) | async-done | bytes 4456480 | tf_op jit(solution)/shard_map/all_to_all | solution.py:71
  246.0 7.5 %all-to-all-start.5 = ((bf16[128,128,128]{2,1,0:T(8,128)(2,1)}), bf16[128,128,128]{2,1,0:T(8,128)(2,1)}, u32[]{:S(2)}, u32[]{:S(2)}) async-start(bf16[128,128,128]{2,1,0:T(8,128)(2,1)} %bitcast.148), calls=%async_computation.5 | async-start | bytes 8388608 | tf_op jit(solution)/shard_map/all_to_all | solution.py:71
  264.5 6.8 %copy.172 = f32[16,4,32,4,32]{4,3,0,2,1:T(4,128)} copy(f32[16,4,32,4,32]{4,2,0,3,1:T(8,128)} %bitcast.143) | data formatting | bytes 2097152 | tf_op jit(solution)/shard_map/reshape | solution.py:88
  289.4 6.8 %copy.173 = f32[16,4,32,4,32]{4,3,0,2,1:T(4,128)} copy(f32[16,4,32,4,32]{4,2,0,3,1:T(8,128)} %bitcast.144) | data formatting | bytes 2097152 | tf_op jit(solution)/shard_map/reshape | solution.py:88
  310.5 6.8 %copy.174 = f32[16,4,32,4,32]{4,3,0,2,1:T(4,128)} copy(f32[16,4,32,4,32]{4,2,0,3,1:T(8,128)} %bitcast.145) | data formatting | bytes 2097152 | tf_op jit(solution)/shard_map/reshape | solution.py:88
  321.0 4.5 fusion.9
  330.5 6.8 %copy.175 = f32[16,4,32,4,32]{4,3,0,2,1:T(4,128)} copy(f32[16,4,32,4,32]{4,2,0,3,1:T(8,128)} %bitcast.146) | data formatting | bytes 2097152 | tf_op jit(solution)/shard_map/reshape | solution.py:88
  337.4 4.9 reshape.109
  356.6 6.8 %copy.179 = f32[16,4,32,4,32]{4,3,0,2,1:T(4,128)} copy(f32[16,4,32,4,32]{4,2,0,3,1:T(8,128)} %bitcast.147) | data formatting | bytes 2097152 | tf_op jit(solution)/shard_map/reshape | solution.py:88
  363.5 4.6 reshape.110
  385.4 7.5 %all-to-all-start.6 = ((f32[1,16,128,128]{2,3,0,1:T(8,128)}), f32[1,16,128,128]{2,3,0,1:T(8,128)}, u32[]{:S(2)}, u32[]{:S(2)}) async-start(f32[1,16,128,128]{2,3,0,1:T(8,128)} %convolution_bitcast_fusion), calls=%async_computation.6 | async-start | bytes 2097152 | tf_op jit(solution)/shard_map/all_to_all | solution.py:94
  421.2 7.1 %all-to-all-start.4 = ((f32[4,16,128,128]{2,3,0,1:T(8,128)}), f32[4,16,128,128]{2,3,0,1:T(8,128)}, u32[]{:S(2)}, u32[]{:S(2)}) async-start(f32[4,16,128,128]{2,3,0,1:T(8,128)} %copy.151), calls=%async_computation.4 | async-start | bytes 8388608 | tf_op jit(solution)/shard_map/all_to_all | solution.py:94
  433.5 60.9 %all-to-all-done.4 = f32[4,16,128,128]{2,3,0,1:T(8,128)} async-done(((f32[4,16,128,128]{2,3,0,1:T(8,128)}), f32[4,16,128,128]{2,3,0,1:T(8,128)}, u32[]{:S(2)}, u32[]{:S(2)}) %all-to-all-start.4) | async-done | bytes 4194336 | tf_op jit(solution)/shard_map/all_to_all | solution.py:94
  494.4 5.3 %copy.176 = f32[4,16,128,128]{3,2,0,1:T(8,128)} copy(f32[4,16,128,128]{2,3,0,1:T(8,128)} %all-to-all-done.4) | data formatting | bytes 8388608 | tf_op jit(solution)/shard_map/reshape | solution.py:98
  499.7 5.6 %fusion.71 = f32[512,16,128]{2,0,1:T(8,128)S(1)} fusion(f32[512,16,128]{2,0,1:T(8,128)} %bitcast.140, f32[128,128,1]{1,0,2:T(8,128)S(1)} %copy-done.6), kind=kOutput, calls=%fused_computation.84 | convolution fusion | flops 1610612736 | bytes 8454144 | tf_op jit(solution)/shard_map/rjx,xo->rjo/dot_general | solution.py:101
  516.6 4.9 reshape.90
  521.5 5.1 maximum_bitcast_fusion
  (107 shorter events, 162.3 us)
Async XLA Ops:
  6.7 11.0 %copy-start.8 = (s32[128]{0:T(128)S(1)}, s32[128]{0:T(128)}, u32[]{:S(2)}) copy-start(s32[128]{0:T(128)} %param.10) | copy-start | bytes 1540
  6.7 61.6 %all-to-all-start.1 = ((bf16[128,128,128]{2,1,0:T(8,128)(2,1)}), bf16[128,128,128]{2,1,0:T(8,128)(2,1)}, u32[]{:S(2)}, u32[]{:S(2)}) async-start(bf16[128,128,128]{2,1,0:T(8,128)(2,1)} %bitcast.152), calls=%async_computation.1 | async-start | bytes 8388608 | tf_op jit(solution)/shard_map/all_to_all | solution.py:71
  68.2 58.2 %all-to-all-start.2 = ((bf16[128,128,128]{2,1,0:T(8,128)(2,1)}), bf16[128,128,128]{2,1,0:T(8,128)(2,1)}, u32[]{:S(2)}, u32[]{:S(2)}) async-start(bf16[128,128,128]{2,1,0:T(8,128)(2,1)} %bitcast.150), calls=%async_computation.2 | async-start | bytes 8388608 | tf_op jit(solution)/shard_map/all_to_all | solution.py:71
  126.4 58.2 %all-to-all-start.3 = ((bf16[128,128,128]{2,1,0:T(8,128)(2,1)}), bf16[128,128,128]{2,1,0:T(8,128)(2,1)}, u32[]{:S(2)}, u32[]{:S(2)}) async-start(bf16[128,128,128]{2,1,0:T(8,128)(2,1)} %bitcast.149), calls=%async_computation.3 | async-start | bytes 8388608 | tf_op jit(solution)/shard_map/all_to_all | solution.py:71
  184.7 61.3 %all-to-all-start = ((bf16[128,136,128]{2,1,0:T(8,128)(2,1)}), bf16[128,136,128]{2,1,0:T(8,128)(2,1)}, u32[]{:S(2)}, u32[]{:S(2)}) async-start(bf16[128,136,128]{2,1,0:T(8,128)(2,1)} %pad_maximum_fusion), calls=%async_computation | async-start | bytes 8912896 | tf_op jit(solution)/shard_map/all_to_all | solution.py:71
  246.0 101.1 %all-to-all-start.5 = ((bf16[128,128,128]{2,1,0:T(8,128)(2,1)}), bf16[128,128,128]{2,1,0:T(8,128)(2,1)}, u32[]{:S(2)}, u32[]{:S(2)}) async-start(bf16[128,128,128]{2,1,0:T(8,128)(2,1)} %bitcast.148), calls=%async_computation.5 | async-start | bytes 8388608 | tf_op jit(solution)/shard_map/all_to_all | solution.py:71
  271.3 3.7 copy-start.7
  276.1 116.8 %collective-permute-start = (f32[16,4,128]{2,0,1:T(8,128)S(1)}, f32[16,4,128]{2,0,1:T(8,128)S(1)}, u32[]{:S(2)}, u32[]{:S(2)}) collective-permute-start(f32[16,4,128]{2,0,1:T(8,128)S(1)} %get-tuple-element.5), channel_id=1, source_target_pairs={{0,1},{1,2},{2,3},{3,4},{4,5},{5,6},{6,7},{8,9},{9,10},{10,11},{11... | collective-permute-start | bytes 98312 | tf_op jit(solution)/shard_map/ppermute | solution.py:44
  278.1 118.3 %collective-permute-start.1 = (f32[16,4,128]{2,0,1:T(8,128)S(1)}, f32[16,4,128]{2,0,1:T(8,128)S(1)}, u32[]{:S(2)}, u32[]{:S(2)}) collective-permute-start(f32[16,4,128]{2,0,1:T(8,128)S(1)} %get-tuple-element.6), channel_id=1, source_target_pairs={{1,0},{2,1},{3,2},{4,3},{5,4},{6,5},{7,6},{9,8},{10,9},{11,10},{12... | collective-permute-start | bytes 98312 | tf_op jit(solution)/shard_map/ppermute | solution.py:46
  301.0 97.4 %collective-permute-start.2 = (f32[16,4,128]{2,0,1:T(8,128)S(1)}, f32[16,4,128]{2,0,1:T(8,128)S(1)}, u32[]{:S(2)}, u32[]{:S(2)}) collective-permute-start(f32[16,4,128]{2,0,1:T(8,128)S(1)} %get-tuple-element.7), channel_id=1, source_target_pairs={{0,1},{1,2},{2,3},{3,4},{4,5},{5,6},{6,7},{8,9},{9,10},{10,11},{11... | collective-permute-start | bytes 98312 | tf_op jit(solution)/shard_map/ppermute | solution.py:44
  363.5 17.4 %copy-start.3 = (f32[136,128,1]{1,0,2:T(8,128)S(1)}, f32[136,128,1]{1,0,2:T(8,128)}, u32[]{:S(2)}) copy-start(f32[136,128,1]{1,0,2:T(8,128)} %constant.35) | copy-start | bytes 208900
  370.3 6.2 %collective-permute-start.8 = (f32[16,4,128]{2,0,1:T(8,128)S(1)}, f32[16,4,128]{2,0,1:T(8,128)S(1)}, u32[]{:S(2)}, u32[]{:S(2)}) collective-permute-start(f32[16,4,128]{2,0,1:T(8,128)S(1)} %get-tuple-element.13), channel_id=1, source_target_pairs={{0,1},{1,2},{2,3},{3,4},{4,5},{5,6},{6,7},{8,9},{9,10},{10,11},{11... | collective-permute-start | bytes 98312 | tf_op jit(solution)/shard_map/ppermute | solution.py:44
  373.5 5.4 %collective-permute-start.9 = (f32[16,4,128]{2,0,1:T(8,128)S(1)}, f32[16,4,128]{2,0,1:T(8,128)S(1)}, u32[]{:S(2)}, u32[]{:S(2)}) collective-permute-start(f32[16,4,128]{2,0,1:T(8,128)S(1)} %get-tuple-element.14), channel_id=1, source_target_pairs={{1,0},{2,1},{3,2},{4,3},{5,4},{6,5},{7,6},{9,8},{10,9},{11,10},{12... | collective-permute-start | bytes 98312 | tf_op jit(solution)/shard_map/ppermute | solution.py:46
  376.5 25.8 %collective-permute-start.3 = (f32[16,4,128]{2,0,1:T(8,128)S(1)}, f32[16,4,128]{2,0,1:T(8,128)S(1)}, u32[]{:S(2)}, u32[]{:S(2)}) collective-permute-start(f32[16,4,128]{2,0,1:T(8,128)S(1)} %get-tuple-element.8), channel_id=1, source_target_pairs={{1,0},{2,1},{3,2},{4,3},{5,4},{6,5},{7,6},{9,8},{10,9},{11,10},{12... | collective-permute-start | bytes 98312 | tf_op jit(solution)/shard_map/ppermute | solution.py:46
  378.9 23.5 %collective-permute-start.4 = (f32[16,4,128]{2,0,1:T(8,128)}, f32[16,4,128]{2,0,1:T(8,128)S(1)}, u32[]{:S(2)}, u32[]{:S(2)}) collective-permute-start(f32[16,4,128]{2,0,1:T(8,128)} %get-tuple-element.9), channel_id=1, source_target_pairs={{0,1},{1,2},{2,3},{3,4},{4,5},{5,6},{6,7},{8,9},{9,10},{10,11},{11... | collective-permute-start | bytes 98312 | tf_op jit(solution)/shard_map/ppermute | solution.py:44
  385.4 35.8 %all-to-all-start.6 = ((f32[1,16,128,128]{2,3,0,1:T(8,128)}), f32[1,16,128,128]{2,3,0,1:T(8,128)}, u32[]{:S(2)}, u32[]{:S(2)}) async-start(f32[1,16,128,128]{2,3,0,1:T(8,128)} %convolution_bitcast_fusion), calls=%async_computation.6 | async-start | bytes 2097152 | tf_op jit(solution)/shard_map/all_to_all | solution.py:94
  392.9 9.5 %copy-start.2 = (f32[16,128,128]{2,0,1:T(8,128)S(1)}, f32[16,128,128]{2,0,1:T(8,128)}, u32[]{:S(2)}) copy-start(f32[16,128,128]{2,0,1:T(8,128)} %copy-done.1) | copy-start | bytes 3145732
  392.9 9.5 %collective-permute-start.5 = (f32[16,4,128]{2,0,1:T(8,128)S(1)}, f32[16,4,128]{2,0,1:T(8,128)S(1)}, u32[]{:S(2)}, u32[]{:S(2)}) collective-permute-start(f32[16,4,128]{2,0,1:T(8,128)S(1)} %get-tuple-element.10), channel_id=1, source_target_pairs={{1,0},{2,1},{3,2},{4,3},{5,4},{6,5},{7,6},{9,8},{10,9},{11,10},{12... | collective-permute-start | bytes 98312 | tf_op jit(solution)/shard_map/ppermute | solution.py:46
  396.4 6.1 %collective-permute-start.6 = (f32[16,4,128]{2,0,1:T(8,128)}, f32[16,4,128]{2,0,1:T(8,128)S(1)}, u32[]{:S(2)}, u32[]{:S(2)}) collective-permute-start(f32[16,4,128]{2,0,1:T(8,128)} %get-tuple-element.11), channel_id=1, source_target_pairs={{0,1},{1,2},{2,3},{3,4},{4,5},{5,6},{6,7},{8,9},{9,10},{10,11},{11... | collective-permute-start | bytes 98312 | tf_op jit(solution)/shard_map/ppermute | solution.py:44
  398.4 5.5 %collective-permute-start.7 = (f32[16,4,128]{2,0,1:T(8,128)}, f32[16,4,128]{2,0,1:T(8,128)S(1)}, u32[]{:S(2)}, u32[]{:S(2)}) collective-permute-start(f32[16,4,128]{2,0,1:T(8,128)} %get-tuple-element.12), channel_id=1, source_target_pairs={{1,0},{2,1},{3,2},{4,3},{5,4},{6,5},{7,6},{9,8},{10,9},{11,10},{12... | collective-permute-start | bytes 98312 | tf_op jit(solution)/shard_map/ppermute | solution.py:46
  421.2 8.7 %copy-start.6 = (f32[128,128,1]{1,0,2:T(8,128)S(1)}, f32[128,128,1]{1,0,2:T(8,128)}, u32[]{:S(2)}) copy-start(f32[128,128,1]{1,0,2:T(8,128)} %constant.36) | copy-start | bytes 196612
  421.2 73.2 %all-to-all-start.4 = ((f32[4,16,128,128]{2,3,0,1:T(8,128)}), f32[4,16,128,128]{2,3,0,1:T(8,128)}, u32[]{:S(2)}, u32[]{:S(2)}) async-start(f32[4,16,128,128]{2,3,0,1:T(8,128)} %copy.151), calls=%async_computation.4 | async-start | bytes 8388608 | tf_op jit(solution)/shard_map/all_to_all | solution.py:94
  428.3 3.8 copy-start.4
  499.7 5.6 %copy-start = (f32[4,16,128,128]{3,2,0,1:T(8,128)S(1)}, f32[4,16,128,128]{3,2,0,1:T(8,128)}, u32[]{:S(2)}) copy-start(f32[4,16,128,128]{3,2,0,1:T(8,128)} %copy.176) | copy-start | bytes 12582916
  (3 other events, 5.6 us)

commit v3 on v2

--- a/solution.py
+++ b/solution.py
@@ -91,17 +91,16 @@
         return jnp.einsum("iy,zix->zyx", wy, padded, precision=HIGHEST)
 
     def gather_x(along_y):
-        return lax.all_to_all(along_y, "gx", 1, 3, tiled=True)
+        return lax.all_to_all(along_y, "gx", 1, 1, tiled=True)
 
-    def along_x(slab):
-        count = slab.shape[0]
-        blocks = slab.reshape(count * height, across, width)
-        edge = jnp.zeros((count * height, 1, width), blocks.dtype)
+    def along_x(blocks):
+        count = blocks.shape[0]
+        edge = jnp.zeros((count, 1, height, width), blocks.dtype)
         padded = jnp.concatenate([edge, blocks, edge], axis=1)
-        result = jnp.einsum("rjx,xo->rjo", padded[:, 1 : across + 1], w_mid, precision=HIGHEST)
-        result = result + jnp.einsum("rjx,xo->rjo", padded[:, 0:across], w_left, precision=HIGHEST)
-        result = result + jnp.einsum("rjx,xo->rjo", padded[:, 2 : across + 2], w_right, precision=HIGHEST)
-        return result.reshape(slab.shape)
+        result = jnp.einsum("fjyx,xo->fyjo", padded[:, 1 : across + 1], w_mid, precision=HIGHEST)
+        result = result + jnp.einsum("fjyx,xo->fyjo", padded[:, 0:across], w_left, precision=HIGHEST)
+        result = result + jnp.einsum("fjyx,xo->fyjo", padded[:, 2 : across + 2], w_right, precision=HIGHEST)
+        return result.reshape(count, 1, height, across * width)
 
     w_mid = band(width, width, 0)
     w_left = band(width, width, width)
@@ -114,9 +113,9 @@
     first = gather_x(jnp.stack(smoothed, axis=0))
     last = proc(incoming)
     last = gather_x(last[None])
-    first = along_x(first)
-    last = along_x(last)
-    return jnp.concatenate([first, last], axis=0)
+    spare = jnp.zeros((1,) + first.shape[1:], first.dtype)
+    result = along_x(jnp.concatenate([first, spare], axis=0))
+    return lax.dynamic_update_slice_in_dim(result, along_x(last), fields - 1, axis=0)
 
 
 def solution(mesh):

time: 537 us -> 537 us (level)
  matrix products: 79.4 us -> 87.3 us
    dot_general x6, matrix products: 15.6 us -> 22 us  [the longest x2 8.45 us: along_x(): jnp.einsum('fjyx,xo->fyjo', padded[:, 2:across + 2], w_right, precision=H...]
    unnamed x25 -> x35, local copies, waits for them, and re-layouts: 15.2 us -> 15.3 us
where the time goes in v3:
time: 537 us; the launch traced here: 527 us
  waiting for transfers between devices  241 us (45%)
  local copies, waits for them, and re-layouts  107 us (20%)
  matrix products  87.3 us (16%)
  starting transfers between devices  82.9 us (15%)
  other arithmetic  6.84 us (1%)
    all_to_all x5, waiting for transfers between devices, send(): return lax.all_to_all(outgoing, ('gx', 'gy'), 0, 0, tiled=True)  177 us
    all_to_all x2, waiting for transfers between devices, gather_x(): return lax.all_to_all(along_y, 'gx', 1, 1, tiled=True)  62.6 us
    reshape x10, local copies, waits for them, and re-layouts, proc(): deposited = deposited.reshape(planes, height, width)  55.7 us
    all_to_all x5, starting transfers between devices, send(): return lax.all_to_all(outgoing, ('gx', 'gy'), 0, 0, tiled=True)  41.4 us
    dot_general x5, matrix products, proc(): jnp.einsum('ts,src->trc', landing, incoming, preferred_element_type=jnp.f...  20.7 us
    dot_general x5, matrix products, proc(): return jnp.einsum('iy,zix->zyx', wy, padded, precision=HIGHEST)  18.8 us
    dot_general x5, matrix products, send(): jnp.dot(pick, record, preferred_element_type=jnp.float32)  17.2 us
    ppermute x5, starting transfers between devices, halo(): lax.ppermute(head, axis, [((i + 1) % count, i) for i in range(ends)])  16 us
  transfers between devices with their start and end apart: 17, of which 6 were waited for; matrix products, arithmetic and copies ran while one was open for 31% of the time, Pallas kernels for 0%

profile of v3, /device:TPU:4, one launch (start us, length us, event | category | flops | bytes accessed | tf_op | source)
XLA Modules:
  0.0 526.7 jit_solution(1670819742669168883)
XLA Ops:
  6.7 11.0 %all-to-all-start.1 = ((bf16[128,128,128]{2,1,0:T(8,128)(2,1)}), bf16[128,128,128]{2,1,0:T(8,128)(2,1)}, u32[]{:S(2)}, u32[]{:S(2)}) async-start(bf16[128,128,128]{2,1,0:T(8,128)(2,1)} %bitcast.152), calls=%async_computation.1 | async-start | bytes 8388608 | tf_op jit(solution)/shard_map/all_to_all | solution.py:71
  24.3 43.9 %all-to-all-done.1 = bf16[128,128,128]{2,1,0:T(8,128)(2,1)} async-done(((bf16[128,128,128]{2,1,0:T(8,128)(2,1)}), bf16[128,128,128]{2,1,0:T(8,128)(2,1)}, u32[]{:S(2)}, u32[]{:S(2)}) %all-to-all-start.1) | async-done | bytes 4194336 | tf_op jit(solution)/shard_map/all_to_all | solution.py:71
  68.2 7.5 %all-to-all-start.2 = ((bf16[128,128,128]{2,1,0:T(8,128)(2,1)}), bf16[128,128,128]{2,1,0:T(8,128)(2,1)}, u32[]{:S(2)}, u32[]{:S(2)}) async-start(bf16[128,128,128]{2,1,0:T(8,128)(2,1)} %bitcast.150), calls=%async_computation.2 | async-start | bytes 8388608 | tf_op jit(solution)/shard_map/all_to_all | solution.py:71
  82.4 44.1 %all-to-all-done.2 = bf16[128,128,128]{2,1,0:T(8,128)(2,1)} async-done(((bf16[128,128,128]{2,1,0:T(8,128)(2,1)}), bf16[128,128,128]{2,1,0:T(8,128)(2,1)}, u32[]{:S(2)}, u32[]{:S(2)}) %all-to-all-start.2) | async-done | bytes 4194336 | tf_op jit(solution)/shard_map/all_to_all | solution.py:71
  126.5 7.5 %all-to-all-start.3 = ((bf16[128,128,128]{2,1,0:T(8,128)(2,1)}), bf16[128,128,128]{2,1,0:T(8,128)(2,1)}, u32[]{:S(2)}, u32[]{:S(2)}) async-start(bf16[128,128,128]{2,1,0:T(8,128)(2,1)} %bitcast.149), calls=%async_computation.3 | async-start | bytes 8388608 | tf_op jit(solution)/shard_map/all_to_all | solution.py:71
  142.3 42.4 %all-to-all-done.3 = bf16[128,128,128]{2,1,0:T(8,128)(2,1)} async-done(((bf16[128,128,128]{2,1,0:T(8,128)(2,1)}), bf16[128,128,128]{2,1,0:T(8,128)(2,1)}, u32[]{:S(2)}, u32[]{:S(2)}) %all-to-all-start.3) | async-done | bytes 4194336 | tf_op jit(solution)/shard_map/all_to_all | solution.py:71
  184.7 7.9 %all-to-all-start = ((bf16[128,136,128]{2,1,0:T(8,128)(2,1)}), bf16[128,136,128]{2,1,0:T(8,128)(2,1)}, u32[]{:S(2)}, u32[]{:S(2)}) async-start(bf16[128,136,128]{2,1,0:T(8,128)(2,1)} %pad_maximum_fusion), calls=%async_computation | async-start | bytes 8912896 | tf_op jit(solution)/shard_map/all_to_all | solution.py:71
  199.3 46.7 %all-to-all-done = bf16[128,136,128]{2,1,0:T(8,128)(2,1)} async-done(((bf16[128,136,128]{2,1,0:T(8,128)(2,1)}), bf16[128,136,128]{2,1,0:T(8,128)(2,1)}, u32[]{:S(2)}, u32[]{:S(2)}) %all-to-all-start) | async-done | bytes 4456480 | tf_op jit(solution)/shard_map/all_to_all | solution.py:71
  246.0 7.5 %all-to-all-start.5 = ((bf16[128,128,128]{2,1,0:T(8,128)(2,1)}), bf16[128,128,128]{2,1,0:T(8,128)(2,1)}, u32[]{:S(2)}, u32[]{:S(2)}) async-start(bf16[128,128,128]{2,1,0:T(8,128)(2,1)} %bitcast.148), calls=%async_computation.5 | async-start | bytes 8388608 | tf_op jit(solution)/shard_map/all_to_all | solution.py:71
  264.5 6.9 %copy.153 = f32[16,4,32,4,32]{4,3,0,2,1:T(4,128)} copy(f32[16,4,32,4,32]{4,2,0,3,1:T(8,128)} %bitcast.143) | data formatting | bytes 2097152 | tf_op jit(solution)/shard_map/reshape | solution.py:88
  289.5 6.9 %copy.154 = f32[16,4,32,4,32]{4,3,0,2,1:T(4,128)} copy(f32[16,4,32,4,32]{4,2,0,3,1:T(8,128)} %bitcast.144) | data formatting | bytes 2097152 | tf_op jit(solution)/shard_map/reshape | solution.py:88
  310.5 6.9 %copy.155 = f32[16,4,32,4,32]{4,3,0,2,1:T(4,128)} copy(f32[16,4,32,4,32]{4,2,0,3,1:T(8,128)} %bitcast.145) | data formatting | bytes 2097152 | tf_op jit(solution)/shard_map/reshape | solution.py:88
  329.3 6.9 %copy.156 = f32[16,4,32,4,32]{4,3,0,2,1:T(4,128)} copy(f32[16,4,32,4,32]{4,2,0,3,1:T(8,128)} %bitcast.146) | data formatting | bytes 2097152 | tf_op jit(solution)/shard_map/reshape | solution.py:88
  336.1 4.9 reshape.116
  347.1 4.9 fusion.11
  356.9 6.9 %copy.157 = f32[16,4,32,4,32]{4,3,0,2,1:T(4,128)} copy(f32[16,4,32,4,32]{4,2,0,3,1:T(8,128)} %bitcast.147) | data formatting | bytes 2097152 | tf_op jit(solution)/shard_map/reshape | solution.py:88
  385.7 7.4 %all-to-all-start.6 = ((f32[1,16,128,128]{2,3,0,1:T(8,128)}), f32[1,16,128,128]{2,3,0,1:T(8,128)S(1)}, u32[]{:S(2)}, u32[]{:S(2)}) async-start(f32[1,16,128,128]{2,3,0,1:T(8,128)} %convolution_bitcast_fusion), calls=%async_computation.6 | async-start | bytes 2097152 | tf_op jit(solution)/shard_map/all_to_all | solution.py:94
  421.5 7.1 %all-to-all-start.4 = ((f32[4,16,128,128]{2,3,0,1:T(8,128)}), f32[4,16,128,128]{2,3,0,1:T(8,128)}, u32[]{:S(2)}, u32[]{:S(2)}) async-start(f32[4,16,128,128]{2,3,0,1:T(8,128)} %copy.137), calls=%async_computation.4 | async-start | bytes 8388608 | tf_op jit(solution)/shard_map/all_to_all | solution.py:94
  432.6 62.5 %all-to-all-done.4 = f32[4,16,128,128]{2,3,0,1:T(8,128)} async-done(((f32[4,16,128,128]{2,3,0,1:T(8,128)}), f32[4,16,128,128]{2,3,0,1:T(8,128)}, u32[]{:S(2)}, u32[]{:S(2)}) %all-to-all-start.4) | async-done | bytes 4194336 | tf_op jit(solution)/shard_map/all_to_all | solution.py:94
  495.1 5.3 %copy.138 = f32[4,16,128,128]{3,2,1,0:T(8,128)} copy(f32[4,16,128,128]{2,3,0,1:T(8,128)} %all-to-all-done.4) | data formatting | bytes 8388608 | tf_op jit(solution)/shard_map/all_to_all | solution.py:94
  500.5 6.8 %fusion = f32[5,16,128,128]{2,3,1,0:T(8,128)S(1)} fusion(f32[128,128,1,1]{0,1,3,2:T(8,128)S(1)} %copy-done.9, f32[4,16,128,128]{3,2,1,0:T(8,128)} %copy.138), kind=kOutput, calls=%fused_computation.5 | convolution fusion | flops 1887436800 | bytes 9502720 | tf_op jit(solution)/shard_map/fjyx,xo->fyjo/dot_general | solution.py:101
  507.3 4.6 fusion.84
  511.9 7.4 %add_add_fusion = f32[5,16,128,128]{2,3,1,0:T(8,128)} fusion(f32[5,16,128,128]{2,3,1,0:T(8,128)S(1)} %fusion.84, f32[5,16,128,128]{2,3,1,0:T(8,128)S(1)} %fusion, f32[128,128,1,1]{0,1,3,2:T(8,128)S(1)} %copy-done.7, f32[4,16,128,128]{3,2,1,0:T(8,128)S(1)} %copy-done), kind=kOutput, calls=%fused_computation.9 | convolution fusion | flops 1890058240 | bytes 19988480 | tf_op jit(solution)/shard_map/fjyx,xo->fyjo/dot_general | solution.py:102
  519.3 5.9 %copy.148 = f32[5,1,128,2048]{3,2,1,0:T(8,128)} copy(f32[5,1,128,2048]{2,3,0,1:T(8,128)} %bitcast.142) | data formatting | bytes 10485760 | tf_op jit(solution)/shard_map/reshape | solution.py:103
  (116 shorter events, 155.2 us)
Async XLA Ops:
  6.7 11.0 %copy-start.13 = (s32[128]{0:T(128)S(1)}, s32[128]{0:T(128)}, u32[]{:S(2)}) copy-start(s32[128]{0:T(128)} %param.10) | copy-start | bytes 1540
  6.7 61.6 %all-to-all-start.1 = ((bf16[128,128,128]{2,1,0:T(8,128)(2,1)}), bf16[128,128,128]{2,1,0:T(8,128)(2,1)}, u32[]{:S(2)}, u32[]{:S(2)}) async-start(bf16[128,128,128]{2,1,0:T(8,128)(2,1)} %bitcast.152), calls=%async_computation.1 | async-start | bytes 8388608 | tf_op jit(solution)/shard_map/all_to_all | solution.py:71
  68.2 58.2 %all-to-all-start.2 = ((bf16[128,128,128]{2,1,0:T(8,128)(2,1)}), bf16[128,128,128]{2,1,0:T(8,128)(2,1)}, u32[]{:S(2)}, u32[]{:S(2)}) async-start(bf16[128,128,128]{2,1,0:T(8,128)(2,1)} %bitcast.150), calls=%async_computation.2 | async-start | bytes 8388608 | tf_op jit(solution)/shard_map/all_to_all | solution.py:71
  126.5 58.2 %all-to-all-start.3 = ((bf16[128,128,128]{2,1,0:T(8,128)(2,1)}), bf16[128,128,128]{2,1,0:T(8,128)(2,1)}, u32[]{:S(2)}, u32[]{:S(2)}) async-start(bf16[128,128,128]{2,1,0:T(8,128)(2,1)} %bitcast.149), calls=%async_computation.3 | async-start | bytes 8388608 | tf_op jit(solution)/shard_map/all_to_all | solution.py:71
  184.7 61.3 %all-to-all-start = ((bf16[128,136,128]{2,1,0:T(8,128)(2,1)}), bf16[128,136,128]{2,1,0:T(8,128)(2,1)}, u32[]{:S(2)}, u32[]{:S(2)}) async-start(bf16[128,136,128]{2,1,0:T(8,128)(2,1)} %pad_maximum_fusion), calls=%async_computation | async-start | bytes 8912896 | tf_op jit(solution)/shard_map/all_to_all | solution.py:71
  246.0 101.1 %all-to-all-start.5 = ((bf16[128,128,128]{2,1,0:T(8,128)(2,1)}), bf16[128,128,128]{2,1,0:T(8,128)(2,1)}, u32[]{:S(2)}, u32[]{:S(2)}) async-start(bf16[128,128,128]{2,1,0:T(8,128)(2,1)} %bitcast.148), calls=%async_computation.5 | async-start | bytes 8388608 | tf_op jit(solution)/shard_map/all_to_all | solution.py:71
  276.1 117.1 %collective-permute-start = (f32[16,4,128]{2,0,1:T(8,128)S(1)}, f32[16,4,128]{2,0,1:T(8,128)S(1)}, u32[]{:S(2)}, u32[]{:S(2)}) collective-permute-start(f32[16,4,128]{2,0,1:T(8,128)S(1)} %get-tuple-element.7), channel_id=1, source_target_pairs={{0,1},{1,2},{2,3},{3,4},{4,5},{5,6},{6,7},{8,9},{9,10},{10,11},{11... | collective-permute-start | bytes 98312 | tf_op jit(solution)/shard_map/ppermute | solution.py:44
  278.2 118.5 %collective-permute-start.1 = (f32[16,4,128]{2,0,1:T(8,128)S(1)}, f32[16,4,128]{2,0,1:T(8,128)S(1)}, u32[]{:S(2)}, u32[]{:S(2)}) collective-permute-start(f32[16,4,128]{2,0,1:T(8,128)S(1)} %get-tuple-element.8), channel_id=1, source_target_pairs={{1,0},{2,1},{3,2},{4,3},{5,4},{6,5},{7,6},{9,8},{10,9},{11,10},{12... | collective-permute-start | bytes 98312 | tf_op jit(solution)/shard_map/ppermute | solution.py:46
  301.1 97.7 %collective-permute-start.2 = (f32[16,4,128]{2,0,1:T(8,128)S(1)}, f32[16,4,128]{2,0,1:T(8,128)S(1)}, u32[]{:S(2)}, u32[]{:S(2)}) collective-permute-start(f32[16,4,128]{2,0,1:T(8,128)S(1)} %get-tuple-element.9), channel_id=1, source_target_pairs={{0,1},{1,2},{2,3},{3,4},{4,5},{5,6},{6,7},{8,9},{9,10},{10,11},{11... | collective-permute-start | bytes 98312 | tf_op jit(solution)/shard_map/ppermute | solution.py:44
  347.1 29.1 %copy-start.1 = (f32[16,128,128]{2,0,1:T(8,128)}, f32[16,128,128]{2,0,1:T(8,128)S(1)}, u32[]{:S(2)}) copy-start(f32[16,128,128]{2,0,1:T(8,128)S(1)} %fusion.82) | copy-start | bytes 3145732
  363.8 17.4 %copy-start.5 = (f32[136,128,1]{1,0,2:T(8,128)S(1)}, f32[136,128,1]{1,0,2:T(8,128)}, u32[]{:S(2)}) copy-start(f32[136,128,1]{1,0,2:T(8,128)} %constant.40) | copy-start | bytes 208900
  370.6 6.2 %collective-permute-start.8 = (f32[16,4,128]{2,0,1:T(8,128)S(1)}, f32[16,4,128]{2,0,1:T(8,128)S(1)}, u32[]{:S(2)}, u32[]{:S(2)}) collective-permute-start(f32[16,4,128]{2,0,1:T(8,128)S(1)} %get-tuple-element.5), channel_id=1, source_target_pairs={{0,1},{1,2},{2,3},{3,4},{4,5},{5,6},{6,7},{8,9},{9,10},{10,11},{11... | collective-permute-start | bytes 98312 | tf_op jit(solution)/shard_map/ppermute | solution.py:44
  373.8 5.4 %collective-permute-start.9 = (f32[16,4,128]{2,0,1:T(8,128)S(1)}, f32[16,4,128]{2,0,1:T(8,128)S(1)}, u32[]{:S(2)}, u32[]{:S(2)}) collective-permute-start(f32[16,4,128]{2,0,1:T(8,128)S(1)} %get-tuple-element.6), channel_id=1, source_target_pairs={{1,0},{2,1},{3,2},{4,3},{5,4},{6,5},{7,6},{9,8},{10,9},{11,10},{12... | collective-permute-start | bytes 98312 | tf_op jit(solution)/shard_map/ppermute | solution.py:46
  376.8 25.7 %collective-permute-start.3 = (f32[16,4,128]{2,0,1:T(8,128)S(1)}, f32[16,4,128]{2,0,1:T(8,128)S(1)}, u32[]{:S(2)}, u32[]{:S(2)}) collective-permute-start(f32[16,4,128]{2,0,1:T(8,128)S(1)} %get-tuple-element.10), channel_id=1, source_target_pairs={{1,0},{2,1},{3,2},{4,3},{5,4},{6,5},{7,6},{9,8},{10,9},{11,10},{12... | collective-permute-start | bytes 98312 | tf_op jit(solution)/shard_map/ppermute | solution.py:46
  379.2 23.4 %collective-permute-start.4 = (f32[16,4,128]{2,0,1:T(8,128)}, f32[16,4,128]{2,0,1:T(8,128)S(1)}, u32[]{:S(2)}, u32[]{:S(2)}) collective-permute-start(f32[16,4,128]{2,0,1:T(8,128)} %get-tuple-element.11), channel_id=1, source_target_pairs={{0,1},{1,2},{2,3},{3,4},{4,5},{5,6},{6,7},{8,9},{9,10},{10,11},{11... | collective-permute-start | bytes 98312 | tf_op jit(solution)/shard_map/ppermute | solution.py:44
  385.7 35.7 %all-to-all-start.6 = ((f32[1,16,128,128]{2,3,0,1:T(8,128)}), f32[1,16,128,128]{2,3,0,1:T(8,128)S(1)}, u32[]{:S(2)}, u32[]{:S(2)}) async-start(f32[1,16,128,128]{2,3,0,1:T(8,128)} %convolution_bitcast_fusion), calls=%async_computation.6 | async-start | bytes 2097152 | tf_op jit(solution)/shard_map/all_to_all | solution.py:94
  393.2 9.5 %copy-start.4 = (f32[16,128,128]{2,0,1:T(8,128)S(1)}, f32[16,128,128]{2,0,1:T(8,128)}, u32[]{:S(2)}) copy-start(f32[16,128,128]{2,0,1:T(8,128)} %copy-done.3) | copy-start | bytes 3145732
  393.2 11.1 %copy-start.2 = (f32[16,128,128]{2,0,1:T(8,128)S(1)}, f32[16,128,128]{2,0,1:T(8,128)}, u32[]{:S(2)}) copy-start(f32[16,128,128]{2,0,1:T(8,128)} %copy-done.1) | copy-start | bytes 3145732
  393.2 9.5 %collective-permute-start.5 = (f32[16,4,128]{2,0,1:T(8,128)S(1)}, f32[16,4,128]{2,0,1:T(8,128)S(1)}, u32[]{:S(2)}, u32[]{:S(2)}) collective-permute-start(f32[16,4,128]{2,0,1:T(8,128)S(1)} %get-tuple-element.12), channel_id=1, source_target_pairs={{1,0},{2,1},{3,2},{4,3},{5,4},{6,5},{7,6},{9,8},{10,9},{11,10},{12... | collective-permute-start | bytes 98312 | tf_op jit(solution)/shard_map/ppermute | solution.py:46
  396.7 6.1 %collective-permute-start.6 = (f32[16,4,128]{2,0,1:T(8,128)}, f32[16,4,128]{2,0,1:T(8,128)S(1)}, u32[]{:S(2)}, u32[]{:S(2)}) collective-permute-start(f32[16,4,128]{2,0,1:T(8,128)} %get-tuple-element.13), channel_id=1, source_target_pairs={{0,1},{1,2},{2,3},{3,4},{4,5},{5,6},{6,7},{8,9},{9,10},{10,11},{11... | collective-permute-start | bytes 98312 | tf_op jit(solution)/shard_map/ppermute | solution.py:44
  398.7 5.5 %collective-permute-start.7 = (f32[16,4,128]{2,0,1:T(8,128)}, f32[16,4,128]{2,0,1:T(8,128)S(1)}, u32[]{:S(2)}, u32[]{:S(2)}) collective-permute-start(f32[16,4,128]{2,0,1:T(8,128)} %get-tuple-element.14), channel_id=1, source_target_pairs={{1,0},{2,1},{3,2},{4,3},{5,4},{6,5},{7,6},{9,8},{10,9},{11,10},{12... | collective-permute-start | bytes 98312 | tf_op jit(solution)/shard_map/ppermute | solution.py:46
  421.5 7.5 %copy-start.12 = (f32[128,128,1]{0,1,2:T(8,128)S(1)}, f32[128,128,1]{0,1,2:T(8,128)}, u32[]{:S(2)}) copy-start(f32[128,128,1]{0,1,2:T(8,128)} %constant.44) | copy-start | bytes 196612
  421.5 73.6 %all-to-all-start.4 = ((f32[4,16,128,128]{2,3,0,1:T(8,128)}), f32[4,16,128,128]{2,3,0,1:T(8,128)}, u32[]{:S(2)}, u32[]{:S(2)}) async-start(f32[4,16,128,128]{2,3,0,1:T(8,128)} %copy.137), calls=%async_computation.4 | async-start | bytes 8388608 | tf_op jit(solution)/shard_map/all_to_all | solution.py:94
  432.5 67.9 %copy-start.9 = (f32[128,128,1,1]{0,1,3,2:T(8,128)S(1)}, f32[128,128,1,1]{0,1,3,2:T(8,128)}, u32[]{:S(2)}) copy-start(f32[128,128,1,1]{0,1,3,2:T(8,128)} %constant.42) | copy-start | bytes 196612
  (8 other events, 28.8 us)

commit v4 on v3

--- a/solution.py
+++ b/solution.py
@@ -93,6 +93,16 @@
     def gather_x(along_y):
         return lax.all_to_all(along_y, "gx", 1, 1, tiled=True)
 
+    def spread_x(along_y):
+        me_x = lax.axis_index("gx")
+        pieces = [lax.dynamic_slice_in_dim(along_y, me_x, 1, axis=0)]
+        for shift in range(1, across):
+            piece = lax.dynamic_slice_in_dim(along_y, (me_x + shift) % across, 1, axis=0)
+            pieces.append(lax.ppermute(piece, "gx", [(g, (g + shift) % across) for g in range(across)]))
+        stacked = jnp.concatenate(pieces, axis=0)
+        order = (me_x - jnp.arange(across, dtype=jnp.int32)) % across
+        return jnp.take(stacked, order, axis=0)[None]
+
     def along_x(blocks):
         count = blocks.shape[0]
         edge = jnp.zeros((count, 1, height, width), blocks.dtype)
@@ -112,7 +122,7 @@
         incoming = following
     first = gather_x(jnp.stack(smoothed, axis=0))
     last = proc(incoming)
-    last = gather_x(last[None])
+    last = spread_x(last)
     spare = jnp.zeros((1,) + first.shape[1:], first.dtype)
     result = along_x(jnp.concatenate([first, spare], axis=0))
     return lax.dynamic_update_slice_in_dim(result, along_x(last), fields - 1, axis=0)

time: 537 us -> 545 us (1.015)
  starting transfers between devices: 82.9 us -> 110 us
  waiting for transfers between devices: 241 us -> 222 us
    all_to_all x2 -> x1, waiting for transfers between devices: 62.6 us -> 0.01 us  [gather_x(): return lax.all_to_all(along_y, 'gx', 1, 1, tiled=True)]
    ppermute x0 -> x15, waiting for transfers between devices: none -> 42.2 us  [spread_x(): lax.ppermute(piece, 'gx', [(g, (g + shift) % across) for g in range(acros...]
    ppermute x0 -> x15, starting transfers between devices: none -> 33.5 us  [spread_x(): lax.ppermute(piece, 'gx', [(g, (g + shift) % across) for g in range(acros...]
    all_to_all x2 -> x1, starting transfers between devices: 14.5 us -> 7.79 us  [gather_x(): return lax.all_to_all(along_y, 'gx', 1, 1, tiled=True)]
    unnamed x35 -> x48, local copies, waits for them, and re-layouts: 15.3 us -> 14.4 us
  transfers between devices with their start and end apart: 17 -> 31, of which waited for: 6 -> 9; matrix products, arithmetic and copies ran while one was open for 31% -> 29% of each run, Pallas kernels for 0% -> 0%
where the time goes in v4:
time: 545 us; the launch traced here: 535 us
  waiting for transfers between devices  222 us (41%)
  starting transfers between devices  110 us (20%)
  local copies, waits for them, and re-layouts  109 us (20%)
  matrix products  85.2 us (16%)
  other arithmetic  7.01 us (1%)
    all_to_all x5, waiting for transfers between devices, send(): return lax.all_to_all(outgoing, ('gx', 'gy'), 0, 0, tiled=True)  177 us
    reshape x10, local copies, waits for them, and re-layouts, proc(): deposited = deposited.reshape(planes, height, width)  55.4 us
    ppermute x15, waiting for transfers between devices, spread_x(): lax.ppermute(piece, 'gx', [(g, (g + shift) % across) for g in range(acros...  42.2 us
    all_to_all x5, starting transfers between devices, send(): return lax.all_to_all(outgoing, ('gx', 'gy'), 0, 0, tiled=True)  41.4 us
    ppermute x15, starting transfers between devices, spread_x(): lax.ppermute(piece, 'gx', [(g, (g + shift) % across) for g in range(acros...  33.5 us
    dot_general x5, matrix products, proc(): jnp.einsum('ts,src->trc', landing, incoming, preferred_element_type=jnp.f...  20.4 us
    dot_general x5, matrix products, proc(): return jnp.einsum('iy,zix->zyx', wy, padded, precision=HIGHEST)  17.6 us
    dot_general x5, matrix products, send(): jnp.dot(pick, record, preferred_element_type=jnp.float32)  17.2 us
  transfers between devices with their start and end apart: 31, of which 9 were waited for; matrix products, arithmetic and copies ran while one was open for 29% of the time, Pallas kernels for 0%

profile of v4, /device:TPU:4, one launch (start us, length us, event | category | flops | bytes accessed | tf_op | source)
XLA Modules:
  0.0 535.4 jit_solution(15384634257501521211)
XLA Ops:
  6.7 11.0 %all-to-all-start.3 = ((bf16[128,128,128]{2,1,0:T(8,128)(2,1)}), bf16[128,128,128]{2,1,0:T(8,128)(2,1)}, u32[]{:S(2)}, u32[]{:S(2)}) async-start(bf16[128,128,128]{2,1,0:T(8,128)(2,1)} %bitcast.178), calls=%async_computation.3 | async-start | bytes 8388608 | tf_op jit(solution)/shard_map/all_to_all | solution.py:71
  24.3 43.9 %all-to-all-done.3 = bf16[128,128,128]{2,1,0:T(8,128)(2,1)} async-done(((bf16[128,128,128]{2,1,0:T(8,128)(2,1)}), bf16[128,128,128]{2,1,0:T(8,128)(2,1)}, u32[]{:S(2)}, u32[]{:S(2)}) %all-to-all-start.3) | async-done | bytes 4194336 | tf_op jit(solution)/shard_map/all_to_all | solution.py:71
  68.3 7.5 %all-to-all-start.2 = ((bf16[128,128,128]{2,1,0:T(8,128)(2,1)}), bf16[128,128,128]{2,1,0:T(8,128)(2,1)}, u32[]{:S(2)}, u32[]{:S(2)}) async-start(bf16[128,128,128]{2,1,0:T(8,128)(2,1)} %bitcast.176), calls=%async_computation.2 | async-start | bytes 8388608 | tf_op jit(solution)/shard_map/all_to_all | solution.py:71
  82.5 44.0 %all-to-all-done.2 = bf16[128,128,128]{2,1,0:T(8,128)(2,1)} async-done(((bf16[128,128,128]{2,1,0:T(8,128)(2,1)}), bf16[128,128,128]{2,1,0:T(8,128)(2,1)}, u32[]{:S(2)}, u32[]{:S(2)}) %all-to-all-start.2) | async-done | bytes 4194336 | tf_op jit(solution)/shard_map/all_to_all | solution.py:71
  126.5 7.5 %all-to-all-start.1 = ((bf16[128,128,128]{2,1,0:T(8,128)(2,1)}), bf16[128,128,128]{2,1,0:T(8,128)(2,1)}, u32[]{:S(2)}, u32[]{:S(2)}) async-start(bf16[128,128,128]{2,1,0:T(8,128)(2,1)} %bitcast.175), calls=%async_computation.1 | async-start | bytes 8388608 | tf_op jit(solution)/shard_map/all_to_all | solution.py:71
  142.3 42.4 %all-to-all-done.1 = bf16[128,128,128]{2,1,0:T(8,128)(2,1)} async-done(((bf16[128,128,128]{2,1,0:T(8,128)(2,1)}), bf16[128,128,128]{2,1,0:T(8,128)(2,1)}, u32[]{:S(2)}, u32[]{:S(2)}) %all-to-all-start.1) | async-done | bytes 4194336 | tf_op jit(solution)/shard_map/all_to_all | solution.py:71
  184.8 7.8 %all-to-all-start = ((bf16[128,136,128]{2,1,0:T(8,128)(2,1)}), bf16[128,136,128]{2,1,0:T(8,128)(2,1)}, u32[]{:S(2)}, u32[]{:S(2)}) async-start(bf16[128,136,128]{2,1,0:T(8,128)(2,1)} %pad_maximum_fusion), calls=%async_computation | async-start | bytes 8912896 | tf_op jit(solution)/shard_map/all_to_all | solution.py:71
  199.4 46.7 %all-to-all-done = bf16[128,136,128]{2,1,0:T(8,128)(2,1)} async-done(((bf16[128,136,128]{2,1,0:T(8,128)(2,1)}), bf16[128,136,128]{2,1,0:T(8,128)(2,1)}, u32[]{:S(2)}, u32[]{:S(2)}) %all-to-all-start) | async-done | bytes 4456480 | tf_op jit(solution)/shard_map/all_to_all | solution.py:71
  246.0 7.5 %all-to-all-start.5 = ((bf16[128,128,128]{2,1,0:T(8,128)(2,1)}), bf16[128,128,128]{2,1,0:T(8,128)(2,1)}, u32[]{:S(2)}, u32[]{:S(2)}) async-start(bf16[128,128,128]{2,1,0:T(8,128)(2,1)} %bitcast.174), calls=%async_computation.5 | async-start | bytes 8388608 | tf_op jit(solution)/shard_map/all_to_all | solution.py:71
  264.2 6.9 %copy.157 = f32[16,4,32,4,32]{4,3,0,2,1:T(4,128)} copy(f32[16,4,32,4,32]{4,2,0,3,1:T(8,128)} %bitcast.169) | data formatting | bytes 2097152 | tf_op jit(solution)/shard_map/reshape | solution.py:88
  287.8 6.9 %copy.156 = f32[16,4,32,4,32]{4,3,0,2,1:T(4,128)} copy(f32[16,4,32,4,32]{4,2,0,3,1:T(8,128)} %bitcast.170) | data formatting | bytes 2097152 | tf_op jit(solution)/shard_map/reshape | solution.py:88
  312.5 6.8 %copy.155 = f32[16,4,32,4,32]{4,3,0,2,1:T(4,128)} copy(f32[16,4,32,4,32]{4,2,0,3,1:T(8,128)} %bitcast.171) | data formatting | bytes 2097152 | tf_op jit(solution)/shard_map/reshape | solution.py:88
  319.4 4.5 reshape.180
  340.3 6.9 %copy.154 = f32[16,4,32,4,32]{4,3,0,2,1:T(4,128)} copy(f32[16,4,32,4,32]{4,2,0,3,1:T(8,128)} %bitcast.172) | data formatting | bytes 2097152 | tf_op jit(solution)/shard_map/reshape | solution.py:88
  365.8 6.9 %copy.158 = f32[16,4,32,4,32]{4,3,0,2,1:T(4,128)} copy(f32[16,4,32,4,32]{4,2,0,3,1:T(8,128)} %bitcast.173) | data formatting | bytes 2097152 | tf_op jit(solution)/shard_map/reshape | solution.py:88
  372.7 4.6 reshape.183
  402.8 7.8 %all-to-all-start.4 = ((f32[4,16,128,128]{2,3,0,1:T(8,128)}), f32[4,16,128,128]{2,3,0,1:T(8,128)}, u32[]{:S(2)}, u32[]{:S(2)}) async-start(f32[4,16,128,128]{2,3,0,1:T(8,128)} %copy.136), calls=%async_computation.4 | async-start | bytes 8388608 | tf_op jit(solution)/shard_map/all_to_all | solution.py:94
  433.5 35.5 %collective-permute-done.10 = f32[1,128,128]{1,2,0:T(8,128)S(1)} collective-permute-done((f32[1,128,128]{1,2,0:T(8,128)S(1)}, f32[1,128,128]{1,2,0:T(8,128)S(1)}, u32[]{:S(2)}, u32[]{:S(2)}) %collective-permute-start.10) | collective-permute-done | bytes 65568 | tf_op jit(solution)/shard_map/ppermute | solution.py:101
  468.9 7.4 %collective-permute-start.15 = (f32[1,128,128]{1,2,0:T(8,128)S(1)}, f32[1,128,128]{1,2,0:T(8,128)S(1)}, u32[]{:S(2)}, u32[]{:S(2)}) collective-permute-start(f32[1,128,128]{1,2,0:T(8,128)S(1)} %get-tuple-element.14), channel_id=1, source_target_pairs={{0,48},{8,56},{16,64},{24,72},{32,80},{40,88},{48,96},{56,104},{64... | collective-permute-start | bytes 196616 | tf_op jit(solution)/shard_map/ppermute | solution.py:101
  504.4 5.3 copy.137
  509.7 6.6 %fusion.93 = f32[5,16,128,128]{2,3,1,0:T(8,128)S(1)} fusion(f32[4,16,128,128]{3,2,1,0:T(8,128)} %copy.137, f32[128,128,1,1]{0,1,3,2:T(8,128)S(1)} %copy-done.7), kind=kOutput, calls=%fused_computation.145 | convolution fusion | flops 1610612736 | bytes 9502720 | tf_op jit(solution)/shard_map/fjyx,xo->fyjo/dot_general | solution.py:110
  516.4 4.7 fusion
  521.1 7.1 %add_add_fusion = f32[5,16,128,128]{2,3,1,0:T(8,128)} fusion(f32[5,16,128,128]{2,3,1,0:T(8,128)S(1)} %fusion.93, f32[5,16,128,128]{2,3,1,0:T(8,128)S(1)} %fusion, f32[128,128,1,1]{0,1,3,2:T(8,128)S(1)} %copy-done.5, f32[4,16,128,128]{3,2,1,0:T(8,128)S(1)} %copy-done), kind=kOutput, calls=%fused_computation.10 | convolution fusion | flops 1890058240 | bytes 19988480 | tf_op jit(solution)/shard_map/fjyx,xo->fyjo/dot_general | solution.py:112
  528.2 5.9 %copy.146 = f32[5,1,128,2048]{3,2,1,0:T(8,128)} copy(f32[5,1,128,2048]{2,3,0,1:T(8,128)} %bitcast.168) | data formatting | bytes 10485760 | tf_op jit(solution)/shard_map/reshape | solution.py:113
  (163 shorter events, 191.4 us)
Async XLA Ops:
  6.7 61.6 %all-to-all-start.3 = ((bf16[128,128,128]{2,1,0:T(8,128)(2,1)}), bf16[128,128,128]{2,1,0:T(8,128)(2,1)}, u32[]{:S(2)}, u32[]{:S(2)}) async-start(bf16[128,128,128]{2,1,0:T(8,128)(2,1)} %bitcast.178), calls=%async_computation.3 | async-start | bytes 8388608 | tf_op jit(solution)/shard_map/all_to_all | solution.py:71
  68.3 58.2 %all-to-all-start.2 = ((bf16[128,128,128]{2,1,0:T(8,128)(2,1)}), bf16[128,128,128]{2,1,0:T(8,128)(2,1)}, u32[]{:S(2)}, u32[]{:S(2)}) async-start(bf16[128,128,128]{2,1,0:T(8,128)(2,1)} %bitcast.176), calls=%async_computation.2 | async-start | bytes 8388608 | tf_op jit(solution)/shard_map/all_to_all | solution.py:71
  126.5 58.2 %all-to-all-start.1 = ((bf16[128,128,128]{2,1,0:T(8,128)(2,1)}), bf16[128,128,128]{2,1,0:T(8,128)(2,1)}, u32[]{:S(2)}, u32[]{:S(2)}) async-start(bf16[128,128,128]{2,1,0:T(8,128)(2,1)} %bitcast.175), calls=%async_computation.1 | async-start | bytes 8388608 | tf_op jit(solution)/shard_map/all_to_all | solution.py:71
  184.8 61.2 %all-to-all-start = ((bf16[128,136,128]{2,1,0:T(8,128)(2,1)}), bf16[128,136,128]{2,1,0:T(8,128)(2,1)}, u32[]{:S(2)}, u32[]{:S(2)}) async-start(bf16[128,136,128]{2,1,0:T(8,128)(2,1)} %pad_maximum_fusion), calls=%async_computation | async-start | bytes 8912896 | tf_op jit(solution)/shard_map/all_to_all | solution.py:71
  246.0 108.9 %all-to-all-start.5 = ((bf16[128,128,128]{2,1,0:T(8,128)(2,1)}), bf16[128,128,128]{2,1,0:T(8,128)(2,1)}, u32[]{:S(2)}, u32[]{:S(2)}) async-start(bf16[128,128,128]{2,1,0:T(8,128)(2,1)} %bitcast.174), calls=%async_computation.5 | async-start | bytes 8388608 | tf_op jit(solution)/shard_map/all_to_all | solution.py:71
  275.9 101.4 %collective-permute-start.7 = (f32[16,4,128]{2,0,1:T(8,128)S(1)}, f32[16,4,128]{2,0,1:T(8,128)S(1)}, u32[]{:S(2)}, u32[]{:S(2)}) collective-permute-start(f32[16,4,128]{2,0,1:T(8,128)S(1)} %get-tuple-element.29), channel_id=1, source_target_pairs={{1,0},{2,1},{3,2},{4,3},{5,4},{6,5},{7,6},{9,8},{10,9},{11,10},{12... | collective-permute-start | bytes 98312 | tf_op jit(solution)/shard_map/ppermute | solution.py:46
  278.1 101.2 %collective-permute-start.6 = (f32[16,4,128]{2,0,1:T(8,128)S(1)}, f32[16,4,128]{2,0,1:T(8,128)S(1)}, u32[]{:S(2)}, u32[]{:S(2)}) collective-permute-start(f32[16,4,128]{2,0,1:T(8,128)S(1)} %get-tuple-element.28), channel_id=1, source_target_pairs={{0,1},{1,2},{2,3},{3,4},{4,5},{5,6},{6,7},{8,9},{9,10},{10,11},{11... | collective-permute-start | bytes 98312 | tf_op jit(solution)/shard_map/ppermute | solution.py:44
  299.4 87.2 %collective-permute-start.5 = (f32[16,4,128]{2,0,1:T(8,128)S(1)}, f32[16,4,128]{2,0,1:T(8,128)S(1)}, u32[]{:S(2)}, u32[]{:S(2)}) collective-permute-start(f32[16,4,128]{2,0,1:T(8,128)S(1)} %get-tuple-element.27), channel_id=1, source_target_pairs={{1,0},{2,1},{3,2},{4,3},{5,4},{6,5},{7,6},{9,8},{10,9},{11,10},{12... | collective-permute-start | bytes 98312 | tf_op jit(solution)/shard_map/ppermute | solution.py:46
  302.8 86.3 %collective-permute-start.4 = (f32[16,4,128]{2,0,1:T(8,128)S(1)}, f32[16,4,128]{2,0,1:T(8,128)S(1)}, u32[]{:S(2)}, u32[]{:S(2)}) collective-permute-start(f32[16,4,128]{2,0,1:T(8,128)S(1)} %get-tuple-element.26), channel_id=1, source_target_pairs={{0,1},{1,2},{2,3},{3,4},{4,5},{5,6},{6,7},{8,9},{9,10},{10,11},{11... | collective-permute-start | bytes 98312 | tf_op jit(solution)/shard_map/ppermute | solution.py:44
  326.7 66.0 %collective-permute-start.3 = (f32[16,4,128]{2,0,1:T(8,128)}, f32[16,4,128]{2,0,1:T(8,128)S(1)}, u32[]{:S(2)}, u32[]{:S(2)}) collective-permute-start(f32[16,4,128]{2,0,1:T(8,128)} %get-tuple-element.25), channel_id=1, source_target_pairs={{1,0},{2,1},{3,2},{4,3},{5,4},{6,5},{7,6},{9,8},{10,9},{11,10},{12... | collective-permute-start | bytes 98312 | tf_op jit(solution)/shard_map/ppermute | solution.py:46
  377.3 15.5 %collective-permute-start.2 = (f32[16,4,128]{2,0,1:T(8,128)S(1)}, f32[16,4,128]{2,0,1:T(8,128)S(1)}, u32[]{:S(2)}, u32[]{:S(2)}) collective-permute-start(f32[16,4,128]{2,0,1:T(8,128)S(1)} %get-tuple-element.24), channel_id=1, source_target_pairs={{0,1},{1,2},{2,3},{3,4},{4,5},{5,6},{6,7},{8,9},{9,10},{10,11},{11... | collective-permute-start | bytes 98312 | tf_op jit(solution)/shard_map/ppermute | solution.py:44
  379.3 17.0 %collective-permute-start.1 = (f32[16,4,128]{2,0,1:T(8,128)}, f32[16,4,128]{2,0,1:T(8,128)S(1)}, u32[]{:S(2)}, u32[]{:S(2)}) collective-permute-start(f32[16,4,128]{2,0,1:T(8,128)} %get-tuple-element.23), channel_id=1, source_target_pairs={{1,0},{2,1},{3,2},{4,3},{5,4},{6,5},{7,6},{9,8},{10,9},{11,10},{12... | collective-permute-start | bytes 98312 | tf_op jit(solution)/shard_map/ppermute | solution.py:46
  386.6 9.7 %collective-permute-start = (f32[16,4,128]{2,0,1:T(8,128)S(1)}, f32[16,4,128]{2,0,1:T(8,128)S(1)}, u32[]{:S(2)}, u32[]{:S(2)}) collective-permute-start(f32[16,4,128]{2,0,1:T(8,128)S(1)} %copy-done.11), channel_id=1, source_target_pairs={{0,1},{1,2},{2,3},{3,4},{4,5},{5,6},{6,7},{8,9},{9,10},{10,11},{11... | collective-permute-start | bytes 98312 | tf_op jit(solution)/shard_map/ppermute | solution.py:44
  402.8 101.6 %all-to-all-start.4 = ((f32[4,16,128,128]{2,3,0,1:T(8,128)}), f32[4,16,128,128]{2,3,0,1:T(8,128)}, u32[]{:S(2)}, u32[]{:S(2)}) async-start(f32[4,16,128,128]{2,3,0,1:T(8,128)} %copy.136), calls=%async_computation.4 | async-start | bytes 8388608 | tf_op jit(solution)/shard_map/all_to_all | solution.py:94
  424.0 45.0 %collective-permute-start.10 = (f32[1,128,128]{1,2,0:T(8,128)S(1)}, f32[1,128,128]{1,2,0:T(8,128)S(1)}, u32[]{:S(2)}, u32[]{:S(2)}) collective-permute-start(f32[1,128,128]{1,2,0:T(8,128)S(1)} %get-tuple-element.19), channel_id=1, source_target_pairs={{0,8},{8,16},{16,24},{24,32},{32,40},{40,48},{48,56},{56,64},{64,7... | collective-permute-start | bytes 196616 | tf_op jit(solution)/shard_map/ppermute | solution.py:101
  425.8 53.9 %collective-permute-start.11 = (f32[1,128,128]{1,2,0:T(8,128)S(1)}, f32[1,128,128]{1,2,0:T(8,128)S(1)}, u32[]{:S(2)}, u32[]{:S(2)}) collective-permute-start(f32[1,128,128]{1,2,0:T(8,128)S(1)} %get-tuple-element.18), channel_id=1, source_target_pairs={{0,16},{8,24},{16,32},{24,40},{32,48},{40,56},{48,64},{56,72},{64,... | collective-permute-start | bytes 196616 | tf_op jit(solution)/shard_map/ppermute | solution.py:101
  428.4 51.2 %collective-permute-start.12 = (f32[1,128,128]{1,2,0:T(8,128)S(1)}, f32[1,128,128]{1,2,0:T(8,128)S(1)}, u32[]{:S(2)}, u32[]{:S(2)}) collective-permute-start(f32[1,128,128]{1,2,0:T(8,128)S(1)} %get-tuple-element.17), channel_id=1, source_target_pairs={{0,24},{8,32},{16,40},{24,48},{32,56},{40,64},{48,72},{56,80},{64,... | collective-permute-start | bytes 196616 | tf_op jit(solution)/shard_map/ppermute | solution.py:101
  430.8 50.3 %collective-permute-start.13 = (f32[1,128,128]{1,2,0:T(8,128)S(1)}, f32[1,128,128]{1,2,0:T(8,128)S(1)}, u32[]{:S(2)}, u32[]{:S(2)}) collective-permute-start(f32[1,128,128]{1,2,0:T(8,128)S(1)} %get-tuple-element.16), channel_id=1, source_target_pairs={{0,32},{8,40},{16,48},{24,56},{32,64},{40,72},{48,80},{56,88},{64,... | collective-permute-start | bytes 196616 | tf_op jit(solution)/shard_map/ppermute | solution.py:101
  432.3 52.8 %collective-permute-start.14 = (f32[1,128,128]{1,2,0:T(8,128)S(1)}, f32[1,128,128]{1,2,0:T(8,128)S(1)}, u32[]{:S(2)}, u32[]{:S(2)}) collective-permute-start(f32[1,128,128]{1,2,0:T(8,128)S(1)} %get-tuple-element.15), channel_id=1, source_target_pairs={{0,40},{8,48},{16,56},{24,64},{32,72},{40,80},{48,88},{56,96},{64,... | collective-permute-start | bytes 196616 | tf_op jit(solution)/shard_map/ppermute | solution.py:101
  468.9 16.4 %collective-permute-start.15 = (f32[1,128,128]{1,2,0:T(8,128)S(1)}, f32[1,128,128]{1,2,0:T(8,128)S(1)}, u32[]{:S(2)}, u32[]{:S(2)}) collective-permute-start(f32[1,128,128]{1,2,0:T(8,128)S(1)} %get-tuple-element.14), channel_id=1, source_target_pairs={{0,48},{8,56},{16,64},{24,72},{32,80},{40,88},{48,96},{56,104},{64... | collective-permute-start | bytes 196616 | tf_op jit(solution)/shard_map/ppermute | solution.py:101
  479.7 12.0 %collective-permute-start.17 = (f32[1,128,128]{1,2,0:T(8,128)S(1)}, f32[1,128,128]{1,2,0:T(8,128)S(1)}, u32[]{:S(2)}, u32[]{:S(2)}) collective-permute-start(f32[1,128,128]{1,2,0:T(8,128)S(1)} %get-tuple-element.12), channel_id=1, source_target_pairs={{0,64},{8,72},{16,80},{24,88},{32,96},{40,104},{48,112},{56,120},{... | collective-permute-start | bytes 196616 | tf_op jit(solution)/shard_map/ppermute | solution.py:101
  481.1 10.7 %collective-permute-start.18 = (f32[1,128,128]{1,2,0:T(8,128)S(1)}, f32[1,128,128]{1,2,0:T(8,128)S(1)}, u32[]{:S(2)}, u32[]{:S(2)}) collective-permute-start(f32[1,128,128]{1,2,0:T(8,128)S(1)} %get-tuple-element.11), channel_id=1, source_target_pairs={{0,72},{8,80},{16,88},{24,96},{32,104},{40,112},{48,120},{56,0},{6... | collective-permute-start | bytes 196616 | tf_op jit(solution)/shard_map/ppermute | solution.py:101
  485.1 10.2 %collective-permute-start.19 = (f32[1,128,128]{1,2,0:T(8,128)S(1)}, f32[1,128,128]{1,2,0:T(8,128)S(1)}, u32[]{:S(2)}, u32[]{:S(2)}) collective-permute-start(f32[1,128,128]{1,2,0:T(8,128)S(1)} %get-tuple-element.10), channel_id=1, source_target_pairs={{0,80},{8,88},{16,96},{24,104},{32,112},{40,120},{48,0},{56,8},{64... | collective-permute-start | bytes 196616 | tf_op jit(solution)/shard_map/ppermute | solution.py:101
  485.3 11.1 %collective-permute-start.20 = (f32[1,128,128]{1,2,0:T(8,128)S(1)}, f32[1,128,128]{1,2,0:T(8,128)S(1)}, u32[]{:S(2)}, u32[]{:S(2)}) collective-permute-start(f32[1,128,128]{1,2,0:T(8,128)S(1)} %get-tuple-element.9), channel_id=1, source_target_pairs={{0,88},{8,96},{16,104},{24,112},{32,120},{40,0},{48,8},{56,16},{64... | collective-permute-start | bytes 196616 | tf_op jit(solution)/shard_map/ppermute | solution.py:101
  (21 other events, 269.2 us)

commit v5 on v4

--- a/solution.py
+++ b/solution.py
@@ -11,6 +11,7 @@
 BY = 4
 RADIUS = 4
 HIGHEST = lax.Precision.HIGHEST
+HIGH = lax.Precision.HIGH
 
 
 def gauss_taps():
@@ -107,9 +108,9 @@
         count = blocks.shape[0]
         edge = jnp.zeros((count, 1, height, width), blocks.dtype)
         padded = jnp.concatenate([edge, blocks, edge], axis=1)
-        result = jnp.einsum("fjyx,xo->fyjo", padded[:, 1 : across + 1], w_mid, precision=HIGHEST)
-        result = result + jnp.einsum("fjyx,xo->fyjo", padded[:, 0:across], w_left, precision=HIGHEST)
-        result = result + jnp.einsum("fjyx,xo->fyjo", padded[:, 2 : across + 2], w_right, precision=HIGHEST)
+        result = jnp.einsum("fjyx,xo->fyjo", padded[:, 1 : across + 1], w_mid, precision=HIGH)
+        result = result + jnp.einsum("fjyx,xo->fyjo", padded[:, 0:across], w_left, precision=HIGH)
+        result = result + jnp.einsum("fjyx,xo->fyjo", padded[:, 2 : across + 2], w_right, precision=HIGH)
         return result.reshape(count, 1, height, across * width)
 
     w_mid = band(width, width, 0)

time: 545 us -> 537 us (0.985)
  matrix products: 85.2 us -> 77.2 us
    dot_general x4, matrix products: 13.6 us -> 7.98 us  [the longest x2 5.26 us: along_x(): jnp.einsum('fjyx,xo->fyjo', padded[:, 1:across + 1], w_mid, precision=HIGH)]
  transfers between devices with their start and end apart: 31 -> 31, of which waited for: 9 -> 9; matrix products, arithmetic and copies ran while one was open for 29% -> 30% of each run, Pallas kernels for 0% -> 0%
where the time goes in v5:
time: 537 us; the launch traced here: 528 us
  waiting for transfers between devices  222 us (41%)
  starting transfers between devices  110 us (20%)
  local copies, waits for them, and re-layouts  109 us (20%)
  matrix products  77.2 us (14%)
  other arithmetic  7.01 us (1%)
    all_to_all x5, waiting for transfers between devices, send(): return lax.all_to_all(outgoing, ('gx', 'gy'), 0, 0, tiled=True)  177 us
    reshape x10, local copies, waits for them, and re-layouts, proc(): deposited = deposited.reshape(planes, height, width)  55.4 us
    ppermute x15, waiting for transfers between devices, spread_x(): lax.ppermute(piece, 'gx', [(g, (g + shift) % across) for g in range(acros...  42.2 us
    all_to_all x5, starting transfers between devices, send(): return lax.all_to_all(outgoing, ('gx', 'gy'), 0, 0, tiled=True)  41.4 us
    ppermute x15, starting transfers between devices, spread_x(): lax.ppermute(piece, 'gx', [(g, (g + shift) % across) for g in range(acros...  33.6 us
    dot_general x5, matrix products, proc(): jnp.einsum('ts,src->trc', landing, incoming, preferred_element_type=jnp.f...  20.4 us
    dot_general x5, matrix products, proc(): return jnp.einsum('iy,zix->zyx', wy, padded, precision=HIGHEST)  17.6 us
    dot_general x5, matrix products, send(): jnp.dot(pick, record, preferred_element_type=jnp.float32)  17.2 us
  transfers between devices with their start and end apart: 31, of which 9 were waited for; matrix products, arithmetic and copies ran while one was open for 30% of the time, Pallas kernels for 0%

profile of v5, /device:TPU:4, one launch (start us, length us, event | category | flops | bytes accessed | tf_op | source)
XLA Modules:
  0.0 527.6 jit_solution(8682611472583823297)
XLA Ops:
  6.7 11.0 %all-to-all-start.3 = ((bf16[128,128,128]{2,1,0:T(8,128)(2,1)}), bf16[128,128,128]{2,1,0:T(8,128)(2,1)}, u32[]{:S(2)}, u32[]{:S(2)}) async-start(bf16[128,128,128]{2,1,0:T(8,128)(2,1)} %bitcast.178), calls=%async_computation.3 | async-start | bytes 8388608 | tf_op jit(solution)/shard_map/all_to_all | solution.py:72
  24.3 43.9 %all-to-all-done.3 = bf16[128,128,128]{2,1,0:T(8,128)(2,1)} async-done(((bf16[128,128,128]{2,1,0:T(8,128)(2,1)}), bf16[128,128,128]{2,1,0:T(8,128)(2,1)}, u32[]{:S(2)}, u32[]{:S(2)}) %all-to-all-start.3) | async-done | bytes 4194336 | tf_op jit(solution)/shard_map/all_to_all | solution.py:72
  68.3 7.5 %all-to-all-start.2 = ((bf16[128,128,128]{2,1,0:T(8,128)(2,1)}), bf16[128,128,128]{2,1,0:T(8,128)(2,1)}, u32[]{:S(2)}, u32[]{:S(2)}) async-start(bf16[128,128,128]{2,1,0:T(8,128)(2,1)} %bitcast.176), calls=%async_computation.2 | async-start | bytes 8388608 | tf_op jit(solution)/shard_map/all_to_all | solution.py:72
  82.5 44.0 %all-to-all-done.2 = bf16[128,128,128]{2,1,0:T(8,128)(2,1)} async-done(((bf16[128,128,128]{2,1,0:T(8,128)(2,1)}), bf16[128,128,128]{2,1,0:T(8,128)(2,1)}, u32[]{:S(2)}, u32[]{:S(2)}) %all-to-all-start.2) | async-done | bytes 4194336 | tf_op jit(solution)/shard_map/all_to_all | solution.py:72
  126.5 7.5 %all-to-all-start.1 = ((bf16[128,128,128]{2,1,0:T(8,128)(2,1)}), bf16[128,128,128]{2,1,0:T(8,128)(2,1)}, u32[]{:S(2)}, u32[]{:S(2)}) async-start(bf16[128,128,128]{2,1,0:T(8,128)(2,1)} %bitcast.175), calls=%async_computation.1 | async-start | bytes 8388608 | tf_op jit(solution)/shard_map/all_to_all | solution.py:72
  142.3 42.4 %all-to-all-done.1 = bf16[128,128,128]{2,1,0:T(8,128)(2,1)} async-done(((bf16[128,128,128]{2,1,0:T(8,128)(2,1)}), bf16[128,128,128]{2,1,0:T(8,128)(2,1)}, u32[]{:S(2)}, u32[]{:S(2)}) %all-to-all-start.1) | async-done | bytes 4194336 | tf_op jit(solution)/shard_map/all_to_all | solution.py:72
  184.8 7.9 %all-to-all-start = ((bf16[128,136,128]{2,1,0:T(8,128)(2,1)}), bf16[128,136,128]{2,1,0:T(8,128)(2,1)}, u32[]{:S(2)}, u32[]{:S(2)}) async-start(bf16[128,136,128]{2,1,0:T(8,128)(2,1)} %pad_maximum_fusion), calls=%async_computation | async-start | bytes 8912896 | tf_op jit(solution)/shard_map/all_to_all | solution.py:72
  199.4 46.7 %all-to-all-done = bf16[128,136,128]{2,1,0:T(8,128)(2,1)} async-done(((bf16[128,136,128]{2,1,0:T(8,128)(2,1)}), bf16[128,136,128]{2,1,0:T(8,128)(2,1)}, u32[]{:S(2)}, u32[]{:S(2)}) %all-to-all-start) | async-done | bytes 4456480 | tf_op jit(solution)/shard_map/all_to_all | solution.py:72
  246.0 7.5 %all-to-all-start.5 = ((bf16[128,128,128]{2,1,0:T(8,128)(2,1)}), bf16[128,128,128]{2,1,0:T(8,128)(2,1)}, u32[]{:S(2)}, u32[]{:S(2)}) async-start(bf16[128,128,128]{2,1,0:T(8,128)(2,1)} %bitcast.174), calls=%async_computation.5 | async-start | bytes 8388608 | tf_op jit(solution)/shard_map/all_to_all | solution.py:72
  264.3 6.9 %copy.157 = f32[16,4,32,4,32]{4,3,0,2,1:T(4,128)} copy(f32[16,4,32,4,32]{4,2,0,3,1:T(8,128)} %bitcast.169) | data formatting | bytes 2097152 | tf_op jit(solution)/shard_map/reshape | solution.py:89
  288.0 6.9 %copy.156 = f32[16,4,32,4,32]{4,3,0,2,1:T(4,128)} copy(f32[16,4,32,4,32]{4,2,0,3,1:T(8,128)} %bitcast.170) | data formatting | bytes 2097152 | tf_op jit(solution)/shard_map/reshape | solution.py:89
  312.5 6.8 %copy.155 = f32[16,4,32,4,32]{4,3,0,2,1:T(4,128)} copy(f32[16,4,32,4,32]{4,2,0,3,1:T(8,128)} %bitcast.171) | data formatting | bytes 2097152 | tf_op jit(solution)/shard_map/reshape | solution.py:89
  319.4 4.5 reshape.180
  340.6 6.9 %copy.154 = f32[16,4,32,4,32]{4,3,0,2,1:T(4,128)} copy(f32[16,4,32,4,32]{4,2,0,3,1:T(8,128)} %bitcast.172) | data formatting | bytes 2097152 | tf_op jit(solution)/shard_map/reshape | solution.py:89
  347.4 4.5 reshape.179
  366.1 6.9 %copy.158 = f32[16,4,32,4,32]{4,3,0,2,1:T(4,128)} copy(f32[16,4,32,4,32]{4,2,0,3,1:T(8,128)} %bitcast.173) | data formatting | bytes 2097152 | tf_op jit(solution)/shard_map/reshape | solution.py:89
  372.9 4.6 reshape.183
  402.8 7.8 %all-to-all-start.4 = ((f32[4,16,128,128]{2,3,0,1:T(8,128)}), f32[4,16,128,128]{2,3,0,1:T(8,128)}, u32[]{:S(2)}, u32[]{:S(2)}) async-start(f32[4,16,128,128]{2,3,0,1:T(8,128)} %copy.136), calls=%async_computation.4 | async-start | bytes 8388608 | tf_op jit(solution)/shard_map/all_to_all | solution.py:95
  433.5 35.5 %collective-permute-done.10 = f32[1,128,128]{1,2,0:T(8,128)S(1)} collective-permute-done((f32[1,128,128]{1,2,0:T(8,128)S(1)}, f32[1,128,128]{1,2,0:T(8,128)S(1)}, u32[]{:S(2)}, u32[]{:S(2)}) %collective-permute-start.10) | collective-permute-done | bytes 65568 | tf_op jit(solution)/shard_map/ppermute | solution.py:102
  469.0 7.4 %collective-permute-start.15 = (f32[1,128,128]{1,2,0:T(8,128)S(1)}, f32[1,128,128]{1,2,0:T(8,128)S(1)}, u32[]{:S(2)}, u32[]{:S(2)}) collective-permute-start(f32[1,128,128]{1,2,0:T(8,128)S(1)} %get-tuple-element.14), channel_id=1, source_target_pairs={{0,48},{8,56},{16,64},{24,72},{32,80},{40,88},{48,96},{56,104},{64... | collective-permute-start | bytes 196616 | tf_op jit(solution)/shard_map/ppermute | solution.py:102
  502.9 5.3 %copy.137 = f32[4,16,128,128]{3,2,1,0:T(8,128)} copy(f32[4,16,128,128]{2,3,0,1:T(8,128)} %all-to-all-done.4) | data formatting | bytes 8388608 | tf_op jit(solution)/shard_map/all_to_all | solution.py:95
  508.3 4.6 fusion.93
  515.1 5.2 add_add_fusion
  520.3 5.9 %copy.146 = f32[5,1,128,2048]{3,2,1,0:T(8,128)} copy(f32[5,1,128,2048]{2,3,0,1:T(8,128)} %bitcast.168) | data formatting | bytes 10485760 | tf_op jit(solution)/shard_map/reshape | solution.py:114
  (163 shorter events, 187.5 us)
Async XLA Ops:
  6.7 61.6 %all-to-all-start.3 = ((bf16[128,128,128]{2,1,0:T(8,128)(2,1)}), bf16[128,128,128]{2,1,0:T(8,128)(2,1)}, u32[]{:S(2)}, u32[]{:S(2)}) async-start(bf16[128,128,128]{2,1,0:T(8,128)(2,1)} %bitcast.178), calls=%async_computation.3 | async-start | bytes 8388608 | tf_op jit(solution)/shard_map/all_to_all | solution.py:72
  68.3 58.2 %all-to-all-start.2 = ((bf16[128,128,128]{2,1,0:T(8,128)(2,1)}), bf16[128,128,128]{2,1,0:T(8,128)(2,1)}, u32[]{:S(2)}, u32[]{:S(2)}) async-start(bf16[128,128,128]{2,1,0:T(8,128)(2,1)} %bitcast.176), calls=%async_computation.2 | async-start | bytes 8388608 | tf_op jit(solution)/shard_map/all_to_all | solution.py:72
  126.5 58.2 %all-to-all-start.1 = ((bf16[128,128,128]{2,1,0:T(8,128)(2,1)}), bf16[128,128,128]{2,1,0:T(8,128)(2,1)}, u32[]{:S(2)}, u32[]{:S(2)}) async-start(bf16[128,128,128]{2,1,0:T(8,128)(2,1)} %bitcast.175), calls=%async_computation.1 | async-start | bytes 8388608 | tf_op jit(solution)/shard_map/all_to_all | solution.py:72
  184.8 61.3 %all-to-all-start = ((bf16[128,136,128]{2,1,0:T(8,128)(2,1)}), bf16[128,136,128]{2,1,0:T(8,128)(2,1)}, u32[]{:S(2)}, u32[]{:S(2)}) async-start(bf16[128,136,128]{2,1,0:T(8,128)(2,1)} %pad_maximum_fusion), calls=%async_computation | async-start | bytes 8912896 | tf_op jit(solution)/shard_map/all_to_all | solution.py:72
  246.0 109.1 %all-to-all-start.5 = ((bf16[128,128,128]{2,1,0:T(8,128)(2,1)}), bf16[128,128,128]{2,1,0:T(8,128)(2,1)}, u32[]{:S(2)}, u32[]{:S(2)}) async-start(bf16[128,128,128]{2,1,0:T(8,128)(2,1)} %bitcast.174), calls=%async_computation.5 | async-start | bytes 8388608 | tf_op jit(solution)/shard_map/all_to_all | solution.py:72
  275.9 101.6 %collective-permute-start.7 = (f32[16,4,128]{2,0,1:T(8,128)S(1)}, f32[16,4,128]{2,0,1:T(8,128)S(1)}, u32[]{:S(2)}, u32[]{:S(2)}) collective-permute-start(f32[16,4,128]{2,0,1:T(8,128)S(1)} %get-tuple-element.29), channel_id=1, source_target_pairs={{1,0},{2,1},{3,2},{4,3},{5,4},{6,5},{7,6},{9,8},{10,9},{11,10},{12... | collective-permute-start | bytes 98312 | tf_op jit(solution)/shard_map/ppermute | solution.py:47
  278.1 101.4 %collective-permute-start.6 = (f32[16,4,128]{2,0,1:T(8,128)S(1)}, f32[16,4,128]{2,0,1:T(8,128)S(1)}, u32[]{:S(2)}, u32[]{:S(2)}) collective-permute-start(f32[16,4,128]{2,0,1:T(8,128)S(1)} %get-tuple-element.28), channel_id=1, source_target_pairs={{0,1},{1,2},{2,3},{3,4},{4,5},{5,6},{6,7},{8,9},{9,10},{10,11},{11... | collective-permute-start | bytes 98312 | tf_op jit(solution)/shard_map/ppermute | solution.py:45
  299.6 87.2 %collective-permute-start.5 = (f32[16,4,128]{2,0,1:T(8,128)S(1)}, f32[16,4,128]{2,0,1:T(8,128)S(1)}, u32[]{:S(2)}, u32[]{:S(2)}) collective-permute-start(f32[16,4,128]{2,0,1:T(8,128)S(1)} %get-tuple-element.27), channel_id=1, source_target_pairs={{1,0},{2,1},{3,2},{4,3},{5,4},{6,5},{7,6},{9,8},{10,9},{11,10},{12... | collective-permute-start | bytes 98312 | tf_op jit(solution)/shard_map/ppermute | solution.py:47
  303.1 86.0 %collective-permute-start.4 = (f32[16,4,128]{2,0,1:T(8,128)S(1)}, f32[16,4,128]{2,0,1:T(8,128)S(1)}, u32[]{:S(2)}, u32[]{:S(2)}) collective-permute-start(f32[16,4,128]{2,0,1:T(8,128)S(1)} %get-tuple-element.26), channel_id=1, source_target_pairs={{0,1},{1,2},{2,3},{3,4},{4,5},{5,6},{6,7},{8,9},{9,10},{10,11},{11... | collective-permute-start | bytes 98312 | tf_op jit(solution)/shard_map/ppermute | solution.py:45
  326.7 66.0 %collective-permute-start.3 = (f32[16,4,128]{2,0,1:T(8,128)}, f32[16,4,128]{2,0,1:T(8,128)S(1)}, u32[]{:S(2)}, u32[]{:S(2)}) collective-permute-start(f32[16,4,128]{2,0,1:T(8,128)} %get-tuple-element.25), channel_id=1, source_target_pairs={{1,0},{2,1},{3,2},{4,3},{5,4},{6,5},{7,6},{9,8},{10,9},{11,10},{12... | collective-permute-start | bytes 98312 | tf_op jit(solution)/shard_map/ppermute | solution.py:47
  377.5 15.2 %collective-permute-start.2 = (f32[16,4,128]{2,0,1:T(8,128)S(1)}, f32[16,4,128]{2,0,1:T(8,128)S(1)}, u32[]{:S(2)}, u32[]{:S(2)}) collective-permute-start(f32[16,4,128]{2,0,1:T(8,128)S(1)} %get-tuple-element.24), channel_id=1, source_target_pairs={{0,1},{1,2},{2,3},{3,4},{4,5},{5,6},{6,7},{8,9},{9,10},{10,11},{11... | collective-permute-start | bytes 98312 | tf_op jit(solution)/shard_map/ppermute | solution.py:45
  379.6 16.8 %collective-permute-start.1 = (f32[16,4,128]{2,0,1:T(8,128)}, f32[16,4,128]{2,0,1:T(8,128)S(1)}, u32[]{:S(2)}, u32[]{:S(2)}) collective-permute-start(f32[16,4,128]{2,0,1:T(8,128)} %get-tuple-element.23), channel_id=1, source_target_pairs={{1,0},{2,1},{3,2},{4,3},{5,4},{6,5},{7,6},{9,8},{10,9},{11,10},{12... | collective-permute-start | bytes 98312 | tf_op jit(solution)/shard_map/ppermute | solution.py:47
  402.8 100.2 %all-to-all-start.4 = ((f32[4,16,128,128]{2,3,0,1:T(8,128)}), f32[4,16,128,128]{2,3,0,1:T(8,128)}, u32[]{:S(2)}, u32[]{:S(2)}) async-start(f32[4,16,128,128]{2,3,0,1:T(8,128)} %copy.136), calls=%async_computation.4 | async-start | bytes 8388608 | tf_op jit(solution)/shard_map/all_to_all | solution.py:95
  424.0 45.0 %collective-permute-start.10 = (f32[1,128,128]{1,2,0:T(8,128)S(1)}, f32[1,128,128]{1,2,0:T(8,128)S(1)}, u32[]{:S(2)}, u32[]{:S(2)}) collective-permute-start(f32[1,128,128]{1,2,0:T(8,128)S(1)} %get-tuple-element.19), channel_id=1, source_target_pairs={{0,8},{8,16},{16,24},{24,32},{32,40},{40,48},{48,56},{56,64},{64,7... | collective-permute-start | bytes 196616 | tf_op jit(solution)/shard_map/ppermute | solution.py:102
  425.8 53.9 %collective-permute-start.11 = (f32[1,128,128]{1,2,0:T(8,128)S(1)}, f32[1,128,128]{1,2,0:T(8,128)S(1)}, u32[]{:S(2)}, u32[]{:S(2)}) collective-permute-start(f32[1,128,128]{1,2,0:T(8,128)S(1)} %get-tuple-element.18), channel_id=1, source_target_pairs={{0,16},{8,24},{16,32},{24,40},{32,48},{40,56},{48,64},{56,72},{64,... | collective-permute-start | bytes 196616 | tf_op jit(solution)/shard_map/ppermute | solution.py:102
  428.5 51.2 %collective-permute-start.12 = (f32[1,128,128]{1,2,0:T(8,128)S(1)}, f32[1,128,128]{1,2,0:T(8,128)S(1)}, u32[]{:S(2)}, u32[]{:S(2)}) collective-permute-start(f32[1,128,128]{1,2,0:T(8,128)S(1)} %get-tuple-element.17), channel_id=1, source_target_pairs={{0,24},{8,32},{16,40},{24,48},{32,56},{40,64},{48,72},{56,80},{64,... | collective-permute-start | bytes 196616 | tf_op jit(solution)/shard_map/ppermute | solution.py:102
  430.8 50.3 %collective-permute-start.13 = (f32[1,128,128]{1,2,0:T(8,128)S(1)}, f32[1,128,128]{1,2,0:T(8,128)S(1)}, u32[]{:S(2)}, u32[]{:S(2)}) collective-permute-start(f32[1,128,128]{1,2,0:T(8,128)S(1)} %get-tuple-element.16), channel_id=1, source_target_pairs={{0,32},{8,40},{16,48},{24,56},{32,64},{40,72},{48,80},{56,88},{64,... | collective-permute-start | bytes 196616 | tf_op jit(solution)/shard_map/ppermute | solution.py:102
  432.3 52.8 %collective-permute-start.14 = (f32[1,128,128]{1,2,0:T(8,128)S(1)}, f32[1,128,128]{1,2,0:T(8,128)S(1)}, u32[]{:S(2)}, u32[]{:S(2)}) collective-permute-start(f32[1,128,128]{1,2,0:T(8,128)S(1)} %get-tuple-element.15), channel_id=1, source_target_pairs={{0,40},{8,48},{16,56},{24,64},{32,72},{40,80},{48,88},{56,96},{64,... | collective-permute-start | bytes 196616 | tf_op jit(solution)/shard_map/ppermute | solution.py:102
  469.0 16.4 %collective-permute-start.15 = (f32[1,128,128]{1,2,0:T(8,128)S(1)}, f32[1,128,128]{1,2,0:T(8,128)S(1)}, u32[]{:S(2)}, u32[]{:S(2)}) collective-permute-start(f32[1,128,128]{1,2,0:T(8,128)S(1)} %get-tuple-element.14), channel_id=1, source_target_pairs={{0,48},{8,56},{16,64},{24,72},{32,80},{40,88},{48,96},{56,104},{64... | collective-permute-start | bytes 196616 | tf_op jit(solution)/shard_map/ppermute | solution.py:102
  479.7 9.7 %collective-permute-start.16 = (f32[1,128,128]{1,2,0:T(8,128)S(1)}, f32[1,128,128]{1,2,0:T(8,128)S(1)}, u32[]{:S(2)}, u32[]{:S(2)}) collective-permute-start(f32[1,128,128]{1,2,0:T(8,128)S(1)} %get-tuple-element.13), channel_id=1, source_target_pairs={{0,56},{8,64},{16,72},{24,80},{32,88},{40,96},{48,104},{56,112},{6... | collective-permute-start | bytes 196616 | tf_op jit(solution)/shard_map/ppermute | solution.py:102
  479.7 12.0 %collective-permute-start.17 = (f32[1,128,128]{1,2,0:T(8,128)S(1)}, f32[1,128,128]{1,2,0:T(8,128)S(1)}, u32[]{:S(2)}, u32[]{:S(2)}) collective-permute-start(f32[1,128,128]{1,2,0:T(8,128)S(1)} %get-tuple-element.12), channel_id=1, source_target_pairs={{0,64},{8,72},{16,80},{24,88},{32,96},{40,104},{48,112},{56,120},{... | collective-permute-start | bytes 196616 | tf_op jit(solution)/shard_map/ppermute | solution.py:102
  481.1 10.7 %collective-permute-start.18 = (f32[1,128,128]{1,2,0:T(8,128)S(1)}, f32[1,128,128]{1,2,0:T(8,128)S(1)}, u32[]{:S(2)}, u32[]{:S(2)}) collective-permute-start(f32[1,128,128]{1,2,0:T(8,128)S(1)} %get-tuple-element.11), channel_id=1, source_target_pairs={{0,72},{8,80},{16,88},{24,96},{32,104},{40,112},{48,120},{56,0},{6... | collective-permute-start | bytes 196616 | tf_op jit(solution)/shard_map/ppermute | solution.py:102
  485.2 10.2 %collective-permute-start.19 = (f32[1,128,128]{1,2,0:T(8,128)S(1)}, f32[1,128,128]{1,2,0:T(8,128)S(1)}, u32[]{:S(2)}, u32[]{:S(2)}) collective-permute-start(f32[1,128,128]{1,2,0:T(8,128)S(1)} %get-tuple-element.10), channel_id=1, source_target_pairs={{0,80},{8,88},{16,96},{24,104},{32,112},{40,120},{48,0},{56,8},{64... | collective-permute-start | bytes 196616 | tf_op jit(solution)/shard_map/ppermute | solution.py:102
  485.4 11.2 %collective-permute-start.20 = (f32[1,128,128]{1,2,0:T(8,128)S(1)}, f32[1,128,128]{1,2,0:T(8,128)S(1)}, u32[]{:S(2)}, u32[]{:S(2)}) collective-permute-start(f32[1,128,128]{1,2,0:T(8,128)S(1)} %get-tuple-element.9), channel_id=1, source_target_pairs={{0,88},{8,96},{16,104},{24,112},{32,120},{40,0},{48,8},{56,16},{64... | collective-permute-start | bytes 196616 | tf_op jit(solution)/shard_map/ppermute | solution.py:102
  (21 other events, 260.9 us)

commit v6 on v5

--- a/solution.py
+++ b/solution.py
@@ -89,7 +89,7 @@
         deposited = deposited.reshape(planes, height, width)
         along_z = jnp.einsum("io,iyx->oyx", wz, deposited, precision=HIGHEST)
         padded = halo(along_z, "gy", 1, RADIUS)
-        return jnp.einsum("iy,zix->zyx", wy, padded, precision=HIGHEST)
+        return jnp.einsum("iy,zix->zxy", wy, padded, precision=HIGHEST)
 
     def gather_x(along_y):
         return lax.all_to_all(along_y, "gx", 1, 1, tiled=True)
@@ -106,11 +106,11 @@
 
     def along_x(blocks):
         count = blocks.shape[0]
-        edge = jnp.zeros((count, 1, height, width), blocks.dtype)
+        edge = jnp.zeros((count, 1, width, height), blocks.dtype)
         padded = jnp.concatenate([edge, blocks, edge], axis=1)
-        result = jnp.einsum("fjyx,xo->fyjo", padded[:, 1 : across + 1], w_mid, precision=HIGH)
-        result = result + jnp.einsum("fjyx,xo->fyjo", padded[:, 0:across], w_left, precision=HIGH)
-        result = result + jnp.einsum("fjyx,xo->fyjo", padded[:, 2 : across + 2], w_right, precision=HIGH)
+        result = jnp.einsum("fjxy,xo->fyjo", padded[:, 1 : across + 1], w_mid, precision=HIGH)
+        result = result + jnp.einsum("fjxy,xo->fyjo", padded[:, 0:across], w_left, precision=HIGH)
+        result = result + jnp.einsum("fjxy,xo->fyjo", padded[:, 2 : across + 2], w_right, precision=HIGH)
         return result.reshape(count, 1, height, across * width)
 
     w_mid = band(width, width, 0)

time: 537 us -> 536 us (level)
    unnamed x48 -> x45, local copies, waits for them, and re-layouts: 14.4 us -> 14.4 us
where the time goes in v6:
time: 536 us; the launch traced here: 526 us
  waiting for transfers between devices  222 us (41%)
  starting transfers between devices  110 us (21%)
  local copies, waits for them, and re-layouts  104 us (19%)
  matrix products  81.1 us (15%)
  other arithmetic  7.01 us (1%)
    all_to_all x5, waiting for transfers between devices, send(): return lax.all_to_all(outgoing, ('gx', 'gy'), 0, 0, tiled=True)  177 us
    reshape x10, local copies, waits for them, and re-layouts, proc(): deposited = deposited.reshape(planes, height, width)  55.4 us
    ppermute x15, waiting for transfers between devices, spread_x(): lax.ppermute(piece, 'gx', [(g, (g + shift) % across) for g in range(acros...  42.1 us
    all_to_all x5, starting transfers between devices, send(): return lax.all_to_all(outgoing, ('gx', 'gy'), 0, 0, tiled=True)  41.4 us
    ppermute x15, starting transfers between devices, spread_x(): lax.ppermute(piece, 'gx', [(g, (g + shift) % across) for g in range(acros...  33.6 us
    dot_general x5, matrix products, proc(): jnp.einsum('ts,src->trc', landing, incoming, preferred_element_type=jnp.f...  20.4 us
    dot_general x5, matrix products, proc(): return jnp.einsum('iy,zix->zxy', wy, padded, precision=HIGHEST)  17.6 us
    dot_general x5, matrix products, send(): jnp.dot(pick, record, preferred_element_type=jnp.float32)  17.2 us
  transfers between devices with their start and end apart: 31, of which 9 were waited for; matrix products, arithmetic and copies ran while one was open for 30% of the time, Pallas kernels for 0%

profile of v6, /device:TPU:4, one launch (start us, length us, event | category | flops | bytes accessed | tf_op | source)
XLA Modules:
  0.0 526.2 jit_solution(8989616165766190139)
XLA Ops:
  6.7 11.0 %all-to-all-start.3 = ((bf16[128,128,128]{2,1,0:T(8,128)(2,1)}), bf16[128,128,128]{2,1,0:T(8,128)(2,1)}, u32[]{:S(2)}, u32[]{:S(2)}) async-start(bf16[128,128,128]{2,1,0:T(8,128)(2,1)} %bitcast.137), calls=%async_computation.3 | async-start | bytes 8388608 | tf_op jit(solution)/shard_map/all_to_all | solution.py:72
  24.3 43.9 %all-to-all-done.3 = bf16[128,128,128]{2,1,0:T(8,128)(2,1)} async-done(((bf16[128,128,128]{2,1,0:T(8,128)(2,1)}), bf16[128,128,128]{2,1,0:T(8,128)(2,1)}, u32[]{:S(2)}, u32[]{:S(2)}) %all-to-all-start.3) | async-done | bytes 4194336 | tf_op jit(solution)/shard_map/all_to_all | solution.py:72
  68.3 7.5 %all-to-all-start.2 = ((bf16[128,128,128]{2,1,0:T(8,128)(2,1)}), bf16[128,128,128]{2,1,0:T(8,128)(2,1)}, u32[]{:S(2)}, u32[]{:S(2)}) async-start(bf16[128,128,128]{2,1,0:T(8,128)(2,1)} %bitcast.135), calls=%async_computation.2 | async-start | bytes 8388608 | tf_op jit(solution)/shard_map/all_to_all | solution.py:72
  82.5 44.0 %all-to-all-done.2 = bf16[128,128,128]{2,1,0:T(8,128)(2,1)} async-done(((bf16[128,128,128]{2,1,0:T(8,128)(2,1)}), bf16[128,128,128]{2,1,0:T(8,128)(2,1)}, u32[]{:S(2)}, u32[]{:S(2)}) %all-to-all-start.2) | async-done | bytes 4194336 | tf_op jit(solution)/shard_map/all_to_all | solution.py:72
  126.5 7.5 %all-to-all-start.1 = ((bf16[128,128,128]{2,1,0:T(8,128)(2,1)}), bf16[128,128,128]{2,1,0:T(8,128)(2,1)}, u32[]{:S(2)}, u32[]{:S(2)}) async-start(bf16[128,128,128]{2,1,0:T(8,128)(2,1)} %bitcast.134), calls=%async_computation.1 | async-start | bytes 8388608 | tf_op jit(solution)/shard_map/all_to_all | solution.py:72
  142.3 42.4 %all-to-all-done.1 = bf16[128,128,128]{2,1,0:T(8,128)(2,1)} async-done(((bf16[128,128,128]{2,1,0:T(8,128)(2,1)}), bf16[128,128,128]{2,1,0:T(8,128)(2,1)}, u32[]{:S(2)}, u32[]{:S(2)}) %all-to-all-start.1) | async-done | bytes 4194336 | tf_op jit(solution)/shard_map/all_to_all | solution.py:72
  184.8 7.9 %all-to-all-start = ((bf16[128,136,128]{2,1,0:T(8,128)(2,1)}), bf16[128,136,128]{2,1,0:T(8,128)(2,1)}, u32[]{:S(2)}, u32[]{:S(2)}) async-start(bf16[128,136,128]{2,1,0:T(8,128)(2,1)} %pad_maximum_fusion), calls=%async_computation | async-start | bytes 8912896 | tf_op jit(solution)/shard_map/all_to_all | solution.py:72
  199.4 46.7 %all-to-all-done = bf16[128,136,128]{2,1,0:T(8,128)(2,1)} async-done(((bf16[128,136,128]{2,1,0:T(8,128)(2,1)}), bf16[128,136,128]{2,1,0:T(8,128)(2,1)}, u32[]{:S(2)}, u32[]{:S(2)}) %all-to-all-start) | async-done | bytes 4456480 | tf_op jit(solution)/shard_map/all_to_all | solution.py:72
  246.0 7.5 %all-to-all-start.5 = ((bf16[128,128,128]{2,1,0:T(8,128)(2,1)}), bf16[128,128,128]{2,1,0:T(8,128)(2,1)}, u32[]{:S(2)}, u32[]{:S(2)}) async-start(bf16[128,128,128]{2,1,0:T(8,128)(2,1)} %bitcast.133), calls=%async_computation.5 | async-start | bytes 8388608 | tf_op jit(solution)/shard_map/all_to_all | solution.py:72
  256.9 4.5 fusion.13
  264.3 6.9 %copy.130 = f32[16,4,32,4,32]{4,3,0,2,1:T(4,128)} copy(f32[16,4,32,4,32]{4,2,0,3,1:T(8,128)} %bitcast.128) | data formatting | bytes 2097152 | tf_op jit(solution)/shard_map/reshape | solution.py:89
  280.7 4.5 fusion.15
  288.0 6.9 %copy.129 = f32[16,4,32,4,32]{4,3,0,2,1:T(4,128)} copy(f32[16,4,32,4,32]{4,2,0,3,1:T(8,128)} %bitcast.129) | data formatting | bytes 2097152 | tf_op jit(solution)/shard_map/reshape | solution.py:89
  312.5 6.8 %copy.128 = f32[16,4,32,4,32]{4,3,0,2,1:T(4,128)} copy(f32[16,4,32,4,32]{4,2,0,3,1:T(8,128)} %bitcast.130) | data formatting | bytes 2097152 | tf_op jit(solution)/shard_map/reshape | solution.py:89
  319.4 4.5 reshape.180
  340.6 6.8 %copy.127 = f32[16,4,32,4,32]{4,3,0,2,1:T(4,128)} copy(f32[16,4,32,4,32]{4,2,0,3,1:T(8,128)} %bitcast.131) | data formatting | bytes 2097152 | tf_op jit(solution)/shard_map/reshape | solution.py:89
  347.4 4.5 reshape.179
  366.1 6.8 %copy.131 = f32[16,4,32,4,32]{4,3,0,2,1:T(4,128)} copy(f32[16,4,32,4,32]{4,2,0,3,1:T(8,128)} %bitcast.132) | data formatting | bytes 2097152 | tf_op jit(solution)/shard_map/reshape | solution.py:89
  372.9 4.6 reshape.183
  402.8 7.8 %all-to-all-start.4 = ((f32[4,16,128,128]{3,2,0,1:T(8,128)}), f32[4,16,128,128]{3,2,0,1:T(8,128)}, u32[]{:S(2)}, u32[]{:S(2)}) async-start(f32[4,16,128,128]{3,2,0,1:T(8,128)} %copy.115), calls=%async_computation.4 | async-start | bytes 8388608 | tf_op jit(solution)/shard_map/all_to_all | solution.py:95
  433.6 35.4 %collective-permute-done.10 = f32[1,128,128]{2,1,0:T(8,128)S(1)} collective-permute-done((f32[1,128,128]{2,1,0:T(8,128)S(1)}, f32[1,128,128]{2,1,0:T(8,128)S(1)}, u32[]{:S(2)}, u32[]{:S(2)}) %collective-permute-start.10) | collective-permute-done | bytes 65568 | tf_op jit(solution)/shard_map/ppermute | solution.py:102
  469.0 7.4 %collective-permute-start.15 = (f32[1,128,128]{2,1,0:T(8,128)S(1)}, f32[1,128,128]{2,1,0:T(8,128)S(1)}, u32[]{:S(2)}, u32[]{:S(2)}) collective-permute-start(f32[1,128,128]{2,1,0:T(8,128)S(1)} %get-tuple-element.14), channel_id=1, source_target_pairs={{0,48},{8,56},{16,64},{24,72},{32,80},{40,88},{48,96},{56,104},{64... | collective-permute-start | bytes 196616 | tf_op jit(solution)/shard_map/ppermute | solution.py:102
  511.6 7.2 %add_add_fusion = f32[5,16,128,128]{2,3,1,0:T(8,128)} fusion(f32[5,16,128,128]{2,3,1,0:T(8,128)S(1)} %fusion.83, f32[5,16,128,128]{2,3,1,0:T(8,128)S(1)} %fusion, f32[128,128,1,1]{0,1,3,2:T(8,128)S(1)} %copy-done.4, f32[4,16,128,128]{3,2,0,1:T(8,128)} %all-to-all-done.4), kind=kOutput, calls=%fused_computation.10 | convolution fusion | flops 946339840 | bytes 19988480 | tf_op jit(solution)/shard_map/fjxy,xo->fyjo/dot_general | solution.py:113
  518.9 5.9 %copy.122 = f32[5,1,128,2048]{3,2,1,0:T(8,128)} copy(f32[5,1,128,2048]{2,3,0,1:T(8,128)} %bitcast.127) | data formatting | bytes 10485760 | tf_op jit(solution)/shard_map/reshape | solution.py:114
  (159 shorter events, 185.0 us)
Async XLA Ops:
  6.7 61.6 %all-to-all-start.3 = ((bf16[128,128,128]{2,1,0:T(8,128)(2,1)}), bf16[128,128,128]{2,1,0:T(8,128)(2,1)}, u32[]{:S(2)}, u32[]{:S(2)}) async-start(bf16[128,128,128]{2,1,0:T(8,128)(2,1)} %bitcast.137), calls=%async_computation.3 | async-start | bytes 8388608 | tf_op jit(solution)/shard_map/all_to_all | solution.py:72
  68.3 58.2 %all-to-all-start.2 = ((bf16[128,128,128]{2,1,0:T(8,128)(2,1)}), bf16[128,128,128]{2,1,0:T(8,128)(2,1)}, u32[]{:S(2)}, u32[]{:S(2)}) async-start(bf16[128,128,128]{2,1,0:T(8,128)(2,1)} %bitcast.135), calls=%async_computation.2 | async-start | bytes 8388608 | tf_op jit(solution)/shard_map/all_to_all | solution.py:72
  126.5 58.2 %all-to-all-start.1 = ((bf16[128,128,128]{2,1,0:T(8,128)(2,1)}), bf16[128,128,128]{2,1,0:T(8,128)(2,1)}, u32[]{:S(2)}, u32[]{:S(2)}) async-start(bf16[128,128,128]{2,1,0:T(8,128)(2,1)} %bitcast.134), calls=%async_computation.1 | async-start | bytes 8388608 | tf_op jit(solution)/shard_map/all_to_all | solution.py:72
  184.8 61.3 %all-to-all-start = ((bf16[128,136,128]{2,1,0:T(8,128)(2,1)}), bf16[128,136,128]{2,1,0:T(8,128)(2,1)}, u32[]{:S(2)}, u32[]{:S(2)}) async-start(bf16[128,136,128]{2,1,0:T(8,128)(2,1)} %pad_maximum_fusion), calls=%async_computation | async-start | bytes 8912896 | tf_op jit(solution)/shard_map/all_to_all | solution.py:72
  246.0 109.1 %all-to-all-start.5 = ((bf16[128,128,128]{2,1,0:T(8,128)(2,1)}), bf16[128,128,128]{2,1,0:T(8,128)(2,1)}, u32[]{:S(2)}, u32[]{:S(2)}) async-start(bf16[128,128,128]{2,1,0:T(8,128)(2,1)} %bitcast.133), calls=%async_computation.5 | async-start | bytes 8388608 | tf_op jit(solution)/shard_map/all_to_all | solution.py:72
  275.9 101.6 %collective-permute-start.7 = (f32[16,4,128]{2,0,1:T(8,128)S(1)}, f32[16,4,128]{2,0,1:T(8,128)S(1)}, u32[]{:S(2)}, u32[]{:S(2)}) collective-permute-start(f32[16,4,128]{2,0,1:T(8,128)S(1)} %get-tuple-element.30), channel_id=1, source_target_pairs={{1,0},{2,1},{3,2},{4,3},{5,4},{6,5},{7,6},{9,8},{10,9},{11,10},{12... | collective-permute-start | bytes 98312 | tf_op jit(solution)/shard_map/ppermute | solution.py:47
  278.1 101.4 %collective-permute-start.6 = (f32[16,4,128]{2,0,1:T(8,128)S(1)}, f32[16,4,128]{2,0,1:T(8,128)S(1)}, u32[]{:S(2)}, u32[]{:S(2)}) collective-permute-start(f32[16,4,128]{2,0,1:T(8,128)S(1)} %get-tuple-element.29), channel_id=1, source_target_pairs={{0,1},{1,2},{2,3},{3,4},{4,5},{5,6},{6,7},{8,9},{9,10},{10,11},{11... | collective-permute-start | bytes 98312 | tf_op jit(solution)/shard_map/ppermute | solution.py:45
  299.7 87.2 %collective-permute-start.5 = (f32[16,4,128]{2,0,1:T(8,128)S(1)}, f32[16,4,128]{2,0,1:T(8,128)S(1)}, u32[]{:S(2)}, u32[]{:S(2)}) collective-permute-start(f32[16,4,128]{2,0,1:T(8,128)S(1)} %get-tuple-element.28), channel_id=1, source_target_pairs={{1,0},{2,1},{3,2},{4,3},{5,4},{6,5},{7,6},{9,8},{10,9},{11,10},{12... | collective-permute-start | bytes 98312 | tf_op jit(solution)/shard_map/ppermute | solution.py:47
  303.1 86.0 %collective-permute-start.4 = (f32[16,4,128]{2,0,1:T(8,128)S(1)}, f32[16,4,128]{2,0,1:T(8,128)S(1)}, u32[]{:S(2)}, u32[]{:S(2)}) collective-permute-start(f32[16,4,128]{2,0,1:T(8,128)S(1)} %get-tuple-element.27), channel_id=1, source_target_pairs={{0,1},{1,2},{2,3},{3,4},{4,5},{5,6},{6,7},{8,9},{9,10},{10,11},{11... | collective-permute-start | bytes 98312 | tf_op jit(solution)/shard_map/ppermute | solution.py:45
  326.7 66.0 %collective-permute-start.3 = (f32[16,4,128]{2,0,1:T(8,128)}, f32[16,4,128]{2,0,1:T(8,128)S(1)}, u32[]{:S(2)}, u32[]{:S(2)}) collective-permute-start(f32[16,4,128]{2,0,1:T(8,128)} %get-tuple-element.26), channel_id=1, source_target_pairs={{1,0},{2,1},{3,2},{4,3},{5,4},{6,5},{7,6},{9,8},{10,9},{11,10},{12... | collective-permute-start | bytes 98312 | tf_op jit(solution)/shard_map/ppermute | solution.py:47
  377.5 15.2 %collective-permute-start.2 = (f32[16,4,128]{2,0,1:T(8,128)S(1)}, f32[16,4,128]{2,0,1:T(8,128)S(1)}, u32[]{:S(2)}, u32[]{:S(2)}) collective-permute-start(f32[16,4,128]{2,0,1:T(8,128)S(1)} %get-tuple-element.25), channel_id=1, source_target_pairs={{0,1},{1,2},{2,3},{3,4},{4,5},{5,6},{6,7},{8,9},{9,10},{10,11},{11... | collective-permute-start | bytes 98312 | tf_op jit(solution)/shard_map/ppermute | solution.py:45
  379.6 16.8 %collective-permute-start.1 = (f32[16,4,128]{2,0,1:T(8,128)}, f32[16,4,128]{2,0,1:T(8,128)S(1)}, u32[]{:S(2)}, u32[]{:S(2)}) collective-permute-start(f32[16,4,128]{2,0,1:T(8,128)} %get-tuple-element.24), channel_id=1, source_target_pairs={{1,0},{2,1},{3,2},{4,3},{5,4},{6,5},{7,6},{9,8},{10,9},{11,10},{12... | collective-permute-start | bytes 98312 | tf_op jit(solution)/shard_map/ppermute | solution.py:47
  402.8 100.2 %all-to-all-start.4 = ((f32[4,16,128,128]{3,2,0,1:T(8,128)}), f32[4,16,128,128]{3,2,0,1:T(8,128)}, u32[]{:S(2)}, u32[]{:S(2)}) async-start(f32[4,16,128,128]{3,2,0,1:T(8,128)} %copy.115), calls=%async_computation.4 | async-start | bytes 8388608 | tf_op jit(solution)/shard_map/all_to_all | solution.py:95
  424.1 44.9 %collective-permute-start.10 = (f32[1,128,128]{2,1,0:T(8,128)S(1)}, f32[1,128,128]{2,1,0:T(8,128)S(1)}, u32[]{:S(2)}, u32[]{:S(2)}) collective-permute-start(f32[1,128,128]{2,1,0:T(8,128)S(1)} %get-tuple-element.19), channel_id=1, source_target_pairs={{0,8},{8,16},{16,24},{24,32},{32,40},{40,48},{48,56},{56,64},{64,7... | collective-permute-start | bytes 196616 | tf_op jit(solution)/shard_map/ppermute | solution.py:102
  425.9 53.8 %collective-permute-start.11 = (f32[1,128,128]{2,1,0:T(8,128)S(1)}, f32[1,128,128]{2,1,0:T(8,128)S(1)}, u32[]{:S(2)}, u32[]{:S(2)}) collective-permute-start(f32[1,128,128]{2,1,0:T(8,128)S(1)} %get-tuple-element.18), channel_id=1, source_target_pairs={{0,16},{8,24},{16,32},{24,40},{32,48},{40,56},{48,64},{56,72},{64,... | collective-permute-start | bytes 196616 | tf_op jit(solution)/shard_map/ppermute | solution.py:102
  428.6 51.1 %collective-permute-start.12 = (f32[1,128,128]{2,1,0:T(8,128)S(1)}, f32[1,128,128]{2,1,0:T(8,128)S(1)}, u32[]{:S(2)}, u32[]{:S(2)}) collective-permute-start(f32[1,128,128]{2,1,0:T(8,128)S(1)} %get-tuple-element.17), channel_id=1, source_target_pairs={{0,24},{8,32},{16,40},{24,48},{32,56},{40,64},{48,72},{56,80},{64,... | collective-permute-start | bytes 196616 | tf_op jit(solution)/shard_map/ppermute | solution.py:102
  431.0 50.1 %collective-permute-start.13 = (f32[1,128,128]{2,1,0:T(8,128)S(1)}, f32[1,128,128]{2,1,0:T(8,128)S(1)}, u32[]{:S(2)}, u32[]{:S(2)}) collective-permute-start(f32[1,128,128]{2,1,0:T(8,128)S(1)} %get-tuple-element.16), channel_id=1, source_target_pairs={{0,32},{8,40},{16,48},{24,56},{32,64},{40,72},{48,80},{56,88},{64,... | collective-permute-start | bytes 196616 | tf_op jit(solution)/shard_map/ppermute | solution.py:102
  432.5 52.7 %collective-permute-start.14 = (f32[1,128,128]{2,1,0:T(8,128)S(1)}, f32[1,128,128]{2,1,0:T(8,128)S(1)}, u32[]{:S(2)}, u32[]{:S(2)}) collective-permute-start(f32[1,128,128]{2,1,0:T(8,128)S(1)} %get-tuple-element.15), channel_id=1, source_target_pairs={{0,40},{8,48},{16,56},{24,64},{32,72},{40,80},{48,88},{56,96},{64,... | collective-permute-start | bytes 196616 | tf_op jit(solution)/shard_map/ppermute | solution.py:102
  469.0 16.4 %collective-permute-start.15 = (f32[1,128,128]{2,1,0:T(8,128)S(1)}, f32[1,128,128]{2,1,0:T(8,128)S(1)}, u32[]{:S(2)}, u32[]{:S(2)}) collective-permute-start(f32[1,128,128]{2,1,0:T(8,128)S(1)} %get-tuple-element.14), channel_id=1, source_target_pairs={{0,48},{8,56},{16,64},{24,72},{32,80},{40,88},{48,96},{56,104},{64... | collective-permute-start | bytes 196616 | tf_op jit(solution)/shard_map/ppermute | solution.py:102
  479.7 9.7 %collective-permute-start.16 = (f32[1,128,128]{2,1,0:T(8,128)S(1)}, f32[1,128,128]{2,1,0:T(8,128)S(1)}, u32[]{:S(2)}, u32[]{:S(2)}) collective-permute-start(f32[1,128,128]{2,1,0:T(8,128)S(1)} %get-tuple-element.13), channel_id=1, source_target_pairs={{0,56},{8,64},{16,72},{24,80},{32,88},{40,96},{48,104},{56,112},{6... | collective-permute-start | bytes 196616 | tf_op jit(solution)/shard_map/ppermute | solution.py:102
  479.7 12.0 %collective-permute-start.17 = (f32[1,128,128]{2,1,0:T(8,128)S(1)}, f32[1,128,128]{2,1,0:T(8,128)S(1)}, u32[]{:S(2)}, u32[]{:S(2)}) collective-permute-start(f32[1,128,128]{2,1,0:T(8,128)S(1)} %get-tuple-element.12), channel_id=1, source_target_pairs={{0,64},{8,72},{16,80},{24,88},{32,96},{40,104},{48,112},{56,120},{... | collective-permute-start | bytes 196616 | tf_op jit(solution)/shard_map/ppermute | solution.py:102
  481.1 10.7 %collective-permute-start.18 = (f32[1,128,128]{2,1,0:T(8,128)S(1)}, f32[1,128,128]{2,1,0:T(8,128)S(1)}, u32[]{:S(2)}, u32[]{:S(2)}) collective-permute-start(f32[1,128,128]{2,1,0:T(8,128)S(1)} %get-tuple-element.11), channel_id=1, source_target_pairs={{0,72},{8,80},{16,88},{24,96},{32,104},{40,112},{48,120},{56,0},{6... | collective-permute-start | bytes 196616 | tf_op jit(solution)/shard_map/ppermute | solution.py:102
  485.2 10.2 %collective-permute-start.19 = (f32[1,128,128]{2,1,0:T(8,128)S(1)}, f32[1,128,128]{2,1,0:T(8,128)S(1)}, u32[]{:S(2)}, u32[]{:S(2)}) collective-permute-start(f32[1,128,128]{2,1,0:T(8,128)S(1)} %get-tuple-element.10), channel_id=1, source_target_pairs={{0,80},{8,88},{16,96},{24,104},{32,112},{40,120},{48,0},{56,8},{64... | collective-permute-start | bytes 196616 | tf_op jit(solution)/shard_map/ppermute | solution.py:102
  485.4 11.2 %collective-permute-start.20 = (f32[1,128,128]{2,1,0:T(8,128)S(1)}, f32[1,128,128]{2,1,0:T(8,128)S(1)}, u32[]{:S(2)}, u32[]{:S(2)}) collective-permute-start(f32[1,128,128]{2,1,0:T(8,128)S(1)} %get-tuple-element.9), channel_id=1, source_target_pairs={{0,88},{8,96},{16,104},{24,112},{32,120},{40,0},{48,8},{56,16},{64... | collective-permute-start | bytes 196616 | tf_op jit(solution)/shard_map/ppermute | solution.py:102
  (20 other events, 264.0 us)

commit v7 on v6

--- a/solution.py
+++ b/solution.py
@@ -11,7 +11,6 @@
 BY = 4
 RADIUS = 4
 HIGHEST = lax.Precision.HIGHEST
-HIGH = lax.Precision.HIGH
 
 
 def gauss_taps():
@@ -108,9 +107,14 @@
         count = blocks.shape[0]
         edge = jnp.zeros((count, 1, width, height), blocks.dtype)
         padded = jnp.concatenate([edge, blocks, edge], axis=1)
-        result = jnp.einsum("fjxy,xo->fyjo", padded[:, 1 : across + 1], w_mid, precision=HIGH)
-        result = result + jnp.einsum("fjxy,xo->fyjo", padded[:, 0:across], w_left, precision=HIGH)
-        result = result + jnp.einsum("fjxy,xo->fyjo", padded[:, 2 : across + 2], w_right, precision=HIGH)
+        result = jnp.einsum("fjxy,xo->fyjo", padded[:, 1 : across + 1], w_mid, precision=HIGHEST)
+        reach = width - RADIUS
+        from_left = jnp.einsum("fjxy,xo->fyjo", padded[:, 0:across, reach:], w_left[reach:, :RADIUS], precision=HIGHEST)
+        from_right = jnp.einsum(
+            "fjxy,xo->fyjo", padded[:, 2 : across + 2, :RADIUS], w_right[:RADIUS, reach:], precision=HIGHEST
+        )
+        zeros = jnp.zeros(from_left.shape[:3] + (reach,), result.dtype)
+        result = result + jnp.concatenate([from_left, zeros], axis=3) + jnp.concatenate([zeros, from_right], axis=3)
         return result.reshape(count, 1, height, across * width)
 
     w_mid = band(width, width, 0)

time: 536 us -> 490 us (0.914)
  waiting for transfers between devices: 222 us -> 182 us
  matrix products: 81.1 us -> 73.7 us
    all_to_all x5, waiting for transfers between devices: 177 us -> 154 us  [send(): return lax.all_to_all(outgoing, ('gx', 'gy'), 0, 0, tiled=True)]
    ppermute x15, waiting for transfers between devices: 42.1 us -> 25.8 us  [spread_x(): lax.ppermute(piece, 'gx', [(g, (g + shift) % across) for g in range(acros...]
    dot_general x6, matrix products: 17.6 us -> 11 us  [the longest x2 9.86 us: along_x(): jnp.einsum('fjxy,xo->fyjo', padded[:, 1:across + 1], w_mid, precision=HIG...]
    unnamed x45 -> x39, local copies, waits for them, and re-layouts: 14.4 us -> 14.6 us
  transfers between devices with their start and end apart: 31 -> 31, of which waited for: 9 -> 10; matrix products, arithmetic and copies ran while one was open for 30% -> 33% of each run, Pallas kernels for 0% -> 0%
where the time goes in v7:
time: 490 us; the launch traced here: 480 us
  waiting for transfers between devices  182 us (37%)
  starting transfers between devices  112 us (23%)
  local copies, waits for them, and re-layouts  102 us (21%)
  matrix products  73.7 us (15%)
  other arithmetic  7.01 us (1%)
    all_to_all x5, waiting for transfers between devices, send(): return lax.all_to_all(outgoing, ('gx', 'gy'), 0, 0, tiled=True)  154 us
    reshape x10, local copies, waits for them, and re-layouts, proc(): deposited = deposited.reshape(planes, height, width)  54.8 us
    all_to_all x5, starting transfers between devices, send(): return lax.all_to_all(outgoing, ('gx', 'gy'), 0, 0, tiled=True)  41.8 us
    ppermute x15, starting transfers between devices, spread_x(): lax.ppermute(piece, 'gx', [(g, (g + shift) % across) for g in range(acros...  34.1 us
    ppermute x15, waiting for transfers between devices, spread_x(): lax.ppermute(piece, 'gx', [(g, (g + shift) % across) for g in range(acros...  25.8 us
    dot_general x5, matrix products, proc(): jnp.einsum('ts,src->trc', landing, incoming, preferred_element_type=jnp.f...  20.4 us
    ppermute x5, starting transfers between devices, halo(): lax.ppermute(head, axis, [((i + 1) % count, i) for i in range(ends)])  17.9 us
    dot_general x5, matrix products, proc(): return jnp.einsum('iy,zix->zxy', wy, padded, precision=HIGHEST)  17.8 us
  transfers between devices with their start and end apart: 31, of which 10 were waited for; matrix products, arithmetic and copies ran while one was open for 33% of the time, Pallas kernels for 0%

profile of v7, /device:TPU:4, one launch (start us, length us, event | category | flops | bytes accessed | tf_op | source)
XLA Modules:
  0.0 479.8 jit_solution(10746502325183417969)
XLA Ops:
  6.7 11.0 %all-to-all-start.1 = ((bf16[128,128,128]{2,1,0:T(8,128)(2,1)}), bf16[128,128,128]{2,1,0:T(8,128)(2,1)}, u32[]{:S(2)}, u32[]{:S(2)}) async-start(bf16[128,128,128]{2,1,0:T(8,128)(2,1)} %bitcast.153), calls=%async_computation.1 | async-start | bytes 8388608 | tf_op jit(solution)/shard_map/all_to_all | solution.py:71
  24.3 43.9 %all-to-all-done.1 = bf16[128,128,128]{2,1,0:T(8,128)(2,1)} async-done(((bf16[128,128,128]{2,1,0:T(8,128)(2,1)}), bf16[128,128,128]{2,1,0:T(8,128)(2,1)}, u32[]{:S(2)}, u32[]{:S(2)}) %all-to-all-start.1) | async-done | bytes 4194336 | tf_op jit(solution)/shard_map/all_to_all | solution.py:71
  68.3 7.5 %all-to-all-start.2 = ((bf16[128,128,128]{2,1,0:T(8,128)(2,1)}), bf16[128,128,128]{2,1,0:T(8,128)(2,1)}, u32[]{:S(2)}, u32[]{:S(2)}) async-start(bf16[128,128,128]{2,1,0:T(8,128)(2,1)} %bitcast.151), calls=%async_computation.2 | async-start | bytes 8388608 | tf_op jit(solution)/shard_map/all_to_all | solution.py:71
  84.1 42.4 %all-to-all-done.2 = bf16[128,128,128]{2,1,0:T(8,128)(2,1)} async-done(((bf16[128,128,128]{2,1,0:T(8,128)(2,1)}), bf16[128,128,128]{2,1,0:T(8,128)(2,1)}, u32[]{:S(2)}, u32[]{:S(2)}) %all-to-all-start.2) | async-done | bytes 4194336 | tf_op jit(solution)/shard_map/all_to_all | solution.py:71
  126.5 7.5 %all-to-all-start = ((bf16[128,136,128]{2,1,0:T(8,128)(2,1)}), bf16[128,136,128]{2,1,0:T(8,128)(2,1)}, u32[]{:S(2)}, u32[]{:S(2)}) async-start(bf16[128,136,128]{2,1,0:T(8,128)(2,1)} %pad_maximum_fusion), calls=%async_computation | async-start | bytes 8912896 | tf_op jit(solution)/shard_map/all_to_all | solution.py:71
  140.7 46.9 %all-to-all-done = bf16[128,136,128]{2,1,0:T(8,128)(2,1)} async-done(((bf16[128,136,128]{2,1,0:T(8,128)(2,1)}), bf16[128,136,128]{2,1,0:T(8,128)(2,1)}, u32[]{:S(2)}, u32[]{:S(2)}) %all-to-all-start) | async-done | bytes 4456480 | tf_op jit(solution)/shard_map/all_to_all | solution.py:71
  187.6 7.9 %all-to-all-start.3 = ((bf16[128,128,128]{2,1,0:T(8,128)(2,1)}), bf16[128,128,128]{2,1,0:T(8,128)(2,1)}, u32[]{:S(2)}, u32[]{:S(2)}) async-start(bf16[128,128,128]{2,1,0:T(8,128)(2,1)} %bitcast.150), calls=%async_computation.3 | async-start | bytes 8388608 | tf_op jit(solution)/shard_map/all_to_all | solution.py:71
  213.2 6.9 %copy.127 = f32[16,4,32,4,32]{4,3,0,2,1:T(4,128)} copy(f32[16,4,32,4,32]{4,2,0,3,1:T(8,128)} %bitcast.144) | data formatting | bytes 2097152 | tf_op jit(solution)/shard_map/reshape | solution.py:88
  224.8 21.2 %all-to-all-done.3 = bf16[128,128,128]{2,1,0:T(8,128)(2,1)} async-done(((bf16[128,128,128]{2,1,0:T(8,128)(2,1)}), bf16[128,128,128]{2,1,0:T(8,128)(2,1)}, u32[]{:S(2)}, u32[]{:S(2)}) %all-to-all-start.3) | async-done | bytes 4194336 | tf_op jit(solution)/shard_map/all_to_all | solution.py:71
  246.0 7.9 %all-to-all-start.5 = ((bf16[128,128,128]{2,1,0:T(8,128)(2,1)}), bf16[128,128,128]{2,1,0:T(8,128)(2,1)}, u32[]{:S(2)}, u32[]{:S(2)}) async-start(bf16[128,128,128]{2,1,0:T(8,128)(2,1)} %bitcast.149), calls=%async_computation.5 | async-start | bytes 8388608 | tf_op jit(solution)/shard_map/all_to_all | solution.py:71
  259.5 4.5 fusion.14
  266.9 6.8 %copy.128 = f32[16,4,32,4,32]{4,3,0,2,1:T(4,128)} copy(f32[16,4,32,4,32]{4,2,0,3,1:T(8,128)} %bitcast.145) | data formatting | bytes 2097152 | tf_op jit(solution)/shard_map/reshape | solution.py:88
  284.2 4.5 fusion.12
  291.6 7.0 %copy.129 = f32[16,4,32,4,32]{4,3,0,2,1:T(4,128)} copy(f32[16,4,32,4,32]{4,2,0,3,1:T(8,128)} %bitcast.146) | data formatting | bytes 2097152 | tf_op jit(solution)/shard_map/reshape | solution.py:88
  298.5 4.5 reshape.179
  307.4 4.5 fusion.10
  316.9 7.0 %copy.130 = f32[16,4,32,4,32]{4,3,0,2,1:T(4,128)} copy(f32[16,4,32,4,32]{4,2,0,3,1:T(8,128)} %bitcast.147) | data formatting | bytes 2097152 | tf_op jit(solution)/shard_map/reshape | solution.py:88
  323.9 4.5 reshape.180
  358.9 7.5 %all-to-all-start.4 = ((f32[4,16,128,128]{3,2,0,1:T(8,128)}), f32[4,16,128,128]{3,2,0,1:T(8,128)}, u32[]{:S(2)}, u32[]{:S(2)}) async-start(f32[4,16,128,128]{3,2,0,1:T(8,128)} %copy.115), calls=%async_computation.4 | async-start | bytes 8388608 | tf_op jit(solution)/shard_map/all_to_all | solution.py:94
  373.7 7.0 %copy.131 = f32[16,4,32,4,32]{4,3,0,2,1:T(4,128)} copy(f32[16,4,32,4,32]{4,2,0,3,1:T(8,128)} %bitcast.148) | data formatting | bytes 2097152 | tf_op jit(solution)/shard_map/reshape | solution.py:88
  406.0 19.0 %collective-permute-done.10 = f32[1,128,128]{2,1,0:T(8,128)S(1)} collective-permute-done((f32[1,128,128]{2,1,0:T(8,128)S(1)}, f32[1,128,128]{2,1,0:T(8,128)S(1)}, u32[]{:S(2)}, u32[]{:S(2)}) %collective-permute-start.10) | collective-permute-done | bytes 65568 | tf_op jit(solution)/shard_map/ppermute | solution.py:101
  425.1 7.7 %collective-permute-start.15 = (f32[1,128,128]{2,1,0:T(8,128)S(1)}, f32[1,128,128]{2,1,0:T(8,128)S(1)}, u32[]{:S(2)}, u32[]{:S(2)}) collective-permute-start(f32[1,128,128]{2,1,0:T(8,128)S(1)} %get-tuple-element.14), channel_id=1, source_target_pairs={{0,48},{8,56},{16,64},{24,72},{32,80},{40,88},{48,96},{56,104},{64... | collective-permute-start | bytes 196616 | tf_op jit(solution)/shard_map/ppermute | solution.py:101
  463.6 8.8 %fusion = f32[5,128,16,128]{1,3,2,0:T(8,128)} fusion(f32[5,128,16,4]{1,3,2,0:T(4,128)S(1)} %convolution_bitcast_fusion.5, f32[5,128,16,4]{1,3,2,0:T(4,128)S(1)} %convolution_bitcast_fusion.6, f32[128,128,1,1]{0,1,3,2:T(8,128)S(1)} %copy-done.2, f32[4,16,128,128]{3,2,0,1:T(8,128)} %all-to-all-done.4), kind=kOutput, calls=%fused_computation.9 | convolution fusion | flops 1613234176 | bytes 9830400 | tf_op jit(solution)/shard_map/fjxy,xo->fyjo/dot_general | solution.py:110
  472.4 5.9 %copy.122 = f32[5,1,128,2048]{3,2,1,0:T(8,128)} copy(f32[5,1,128,2048]{2,3,0,1:T(8,128)} %bitcast.143) | data formatting | bytes 10485760 | tf_op jit(solution)/shard_map/reshape | solution.py:118
  (155 shorter events, 175.3 us)
Async XLA Ops:
  6.7 61.6 %all-to-all-start.1 = ((bf16[128,128,128]{2,1,0:T(8,128)(2,1)}), bf16[128,128,128]{2,1,0:T(8,128)(2,1)}, u32[]{:S(2)}, u32[]{:S(2)}) async-start(bf16[128,128,128]{2,1,0:T(8,128)(2,1)} %bitcast.153), calls=%async_computation.1 | async-start | bytes 8388608 | tf_op jit(solution)/shard_map/all_to_all | solution.py:71
  68.3 58.2 %all-to-all-start.2 = ((bf16[128,128,128]{2,1,0:T(8,128)(2,1)}), bf16[128,128,128]{2,1,0:T(8,128)(2,1)}, u32[]{:S(2)}, u32[]{:S(2)}) async-start(bf16[128,128,128]{2,1,0:T(8,128)(2,1)} %bitcast.151), calls=%async_computation.2 | async-start | bytes 8388608 | tf_op jit(solution)/shard_map/all_to_all | solution.py:71
  126.5 61.0 %all-to-all-start = ((bf16[128,136,128]{2,1,0:T(8,128)(2,1)}), bf16[128,136,128]{2,1,0:T(8,128)(2,1)}, u32[]{:S(2)}, u32[]{:S(2)}) async-start(bf16[128,136,128]{2,1,0:T(8,128)(2,1)} %pad_maximum_fusion), calls=%async_computation | async-start | bytes 8912896 | tf_op jit(solution)/shard_map/all_to_all | solution.py:71
  187.6 58.5 %all-to-all-start.3 = ((bf16[128,128,128]{2,1,0:T(8,128)(2,1)}), bf16[128,128,128]{2,1,0:T(8,128)(2,1)}, u32[]{:S(2)}, u32[]{:S(2)}) async-start(bf16[128,128,128]{2,1,0:T(8,128)(2,1)} %bitcast.150), calls=%async_computation.3 | async-start | bytes 8388608 | tf_op jit(solution)/shard_map/all_to_all | solution.py:71
  246.0 112.9 %all-to-all-start.5 = ((bf16[128,128,128]{2,1,0:T(8,128)(2,1)}), bf16[128,128,128]{2,1,0:T(8,128)(2,1)}, u32[]{:S(2)}, u32[]{:S(2)}) async-start(bf16[128,128,128]{2,1,0:T(8,128)(2,1)} %bitcast.149), calls=%async_computation.5 | async-start | bytes 8388608 | tf_op jit(solution)/shard_map/all_to_all | solution.py:71
  254.0 76.7 %collective-permute-start = (f32[16,4,128]{2,0,1:T(8,128)S(1)}, f32[16,4,128]{2,0,1:T(8,128)S(1)}, u32[]{:S(2)}, u32[]{:S(2)}) collective-permute-start(f32[16,4,128]{2,0,1:T(8,128)S(1)} %get-tuple-element.23), channel_id=1, source_target_pairs={{0,1},{1,2},{2,3},{3,4},{4,5},{5,6},{6,7},{8,9},{9,10},{10,11},{11... | collective-permute-start | bytes 98312 | tf_op jit(solution)/shard_map/ppermute | solution.py:44
  256.0 78.3 %collective-permute-start.1 = (f32[16,4,128]{2,0,1:T(8,128)S(1)}, f32[16,4,128]{2,0,1:T(8,128)S(1)}, u32[]{:S(2)}, u32[]{:S(2)}) collective-permute-start(f32[16,4,128]{2,0,1:T(8,128)S(1)} %get-tuple-element.24), channel_id=1, source_target_pairs={{1,0},{2,1},{3,2},{4,3},{5,4},{6,5},{7,6},{9,8},{10,9},{11,10},{12... | collective-permute-start | bytes 98312 | tf_op jit(solution)/shard_map/ppermute | solution.py:46
  278.5 58.0 %collective-permute-start.2 = (f32[16,4,128]{2,0,1:T(8,128)S(1)}, f32[16,4,128]{2,0,1:T(8,128)S(1)}, u32[]{:S(2)}, u32[]{:S(2)}) collective-permute-start(f32[16,4,128]{2,0,1:T(8,128)S(1)} %get-tuple-element.25), channel_id=1, source_target_pairs={{0,1},{1,2},{2,3},{3,4},{4,5},{5,6},{6,7},{8,9},{9,10},{10,11},{11... | collective-permute-start | bytes 98312 | tf_op jit(solution)/shard_map/ppermute | solution.py:44
  280.4 60.2 %collective-permute-start.3 = (f32[16,4,128]{2,0,1:T(8,128)S(1)}, f32[16,4,128]{2,0,1:T(8,128)S(1)}, u32[]{:S(2)}, u32[]{:S(2)}) collective-permute-start(f32[16,4,128]{2,0,1:T(8,128)S(1)} %get-tuple-element.26), channel_id=1, source_target_pairs={{1,0},{2,1},{3,2},{4,3},{5,4},{6,5},{7,6},{9,8},{10,9},{11,10},{12... | collective-permute-start | bytes 98312 | tf_op jit(solution)/shard_map/ppermute | solution.py:46
  305.3 35.4 %collective-permute-start.4 = (f32[16,4,128]{2,0,1:T(8,128)S(1)}, f32[16,4,128]{2,0,1:T(8,128)S(1)}, u32[]{:S(2)}, u32[]{:S(2)}) collective-permute-start(f32[16,4,128]{2,0,1:T(8,128)S(1)} %get-tuple-element.27), channel_id=1, source_target_pairs={{0,1},{1,2},{2,3},{3,4},{4,5},{5,6},{6,7},{8,9},{9,10},{10,11},{11... | collective-permute-start | bytes 98312 | tf_op jit(solution)/shard_map/ppermute | solution.py:44
  330.7 10.0 %collective-permute-start.5 = (f32[16,4,128]{2,0,1:T(8,128)S(1)}, f32[16,4,128]{2,0,1:T(8,128)S(1)}, u32[]{:S(2)}, u32[]{:S(2)}) collective-permute-start(f32[16,4,128]{2,0,1:T(8,128)S(1)} %get-tuple-element.28), channel_id=1, source_target_pairs={{1,0},{2,1},{3,2},{4,3},{5,4},{6,5},{7,6},{9,8},{10,9},{11,10},{12... | collective-permute-start | bytes 98312 | tf_op jit(solution)/shard_map/ppermute | solution.py:46
  358.9 100.1 %all-to-all-start.4 = ((f32[4,16,128,128]{3,2,0,1:T(8,128)}), f32[4,16,128,128]{3,2,0,1:T(8,128)}, u32[]{:S(2)}, u32[]{:S(2)}) async-start(f32[4,16,128,128]{3,2,0,1:T(8,128)} %copy.115), calls=%async_computation.4 | async-start | bytes 8388608 | tf_op jit(solution)/shard_map/all_to_all | solution.py:94
  396.3 28.7 %collective-permute-start.10 = (f32[1,128,128]{2,1,0:T(8,128)S(1)}, f32[1,128,128]{2,1,0:T(8,128)S(1)}, u32[]{:S(2)}, u32[]{:S(2)}) collective-permute-start(f32[1,128,128]{2,1,0:T(8,128)S(1)} %get-tuple-element.19), channel_id=1, source_target_pairs={{0,8},{8,16},{16,24},{24,32},{32,40},{40,48},{48,56},{56,64},{64,7... | collective-permute-start | bytes 196616 | tf_op jit(solution)/shard_map/ppermute | solution.py:101
  398.3 37.8 %collective-permute-start.11 = (f32[1,128,128]{2,1,0:T(8,128)S(1)}, f32[1,128,128]{2,1,0:T(8,128)S(1)}, u32[]{:S(2)}, u32[]{:S(2)}) collective-permute-start(f32[1,128,128]{2,1,0:T(8,128)S(1)} %get-tuple-element.18), channel_id=1, source_target_pairs={{0,16},{8,24},{16,32},{24,40},{32,48},{40,56},{48,64},{56,72},{64,... | collective-permute-start | bytes 196616 | tf_op jit(solution)/shard_map/ppermute | solution.py:101
  401.0 35.1 %collective-permute-start.12 = (f32[1,128,128]{2,1,0:T(8,128)S(1)}, f32[1,128,128]{2,1,0:T(8,128)S(1)}, u32[]{:S(2)}, u32[]{:S(2)}) collective-permute-start(f32[1,128,128]{2,1,0:T(8,128)S(1)} %get-tuple-element.17), channel_id=1, source_target_pairs={{0,24},{8,32},{16,40},{24,48},{32,56},{40,64},{48,72},{56,80},{64,... | collective-permute-start | bytes 196616 | tf_op jit(solution)/shard_map/ppermute | solution.py:101
  403.4 33.9 %collective-permute-start.13 = (f32[1,128,128]{2,1,0:T(8,128)S(1)}, f32[1,128,128]{2,1,0:T(8,128)S(1)}, u32[]{:S(2)}, u32[]{:S(2)}) collective-permute-start(f32[1,128,128]{2,1,0:T(8,128)S(1)} %get-tuple-element.16), channel_id=1, source_target_pairs={{0,32},{8,40},{16,48},{24,56},{32,64},{40,72},{48,80},{56,88},{64,... | collective-permute-start | bytes 196616 | tf_op jit(solution)/shard_map/ppermute | solution.py:101
  404.8 36.4 %collective-permute-start.14 = (f32[1,128,128]{2,1,0:T(8,128)S(1)}, f32[1,128,128]{2,1,0:T(8,128)S(1)}, u32[]{:S(2)}, u32[]{:S(2)}) collective-permute-start(f32[1,128,128]{2,1,0:T(8,128)S(1)} %get-tuple-element.15), channel_id=1, source_target_pairs={{0,40},{8,48},{16,56},{24,64},{32,72},{40,80},{48,88},{56,96},{64,... | collective-permute-start | bytes 196616 | tf_op jit(solution)/shard_map/ppermute | solution.py:101
  425.1 17.4 %collective-permute-start.15 = (f32[1,128,128]{2,1,0:T(8,128)S(1)}, f32[1,128,128]{2,1,0:T(8,128)S(1)}, u32[]{:S(2)}, u32[]{:S(2)}) collective-permute-start(f32[1,128,128]{2,1,0:T(8,128)S(1)} %get-tuple-element.14), channel_id=1, source_target_pairs={{0,48},{8,56},{16,64},{24,72},{32,80},{40,88},{48,96},{56,104},{64... | collective-permute-start | bytes 196616 | tf_op jit(solution)/shard_map/ppermute | solution.py:101
  436.1 9.6 %collective-permute-start.16 = (f32[1,128,128]{2,1,0:T(8,128)S(1)}, f32[1,128,128]{2,1,0:T(8,128)S(1)}, u32[]{:S(2)}, u32[]{:S(2)}) collective-permute-start(f32[1,128,128]{2,1,0:T(8,128)S(1)} %get-tuple-element.13), channel_id=1, source_target_pairs={{0,56},{8,64},{16,72},{24,80},{32,88},{40,96},{48,104},{56,112},{6... | collective-permute-start | bytes 196616 | tf_op jit(solution)/shard_map/ppermute | solution.py:101
  436.1 12.6 %collective-permute-start.17 = (f32[1,128,128]{2,1,0:T(8,128)S(1)}, f32[1,128,128]{2,1,0:T(8,128)S(1)}, u32[]{:S(2)}, u32[]{:S(2)}) collective-permute-start(f32[1,128,128]{2,1,0:T(8,128)S(1)} %get-tuple-element.12), channel_id=1, source_target_pairs={{0,64},{8,72},{16,80},{24,88},{32,96},{40,104},{48,112},{56,120},{... | collective-permute-start | bytes 196616 | tf_op jit(solution)/shard_map/ppermute | solution.py:101
  437.3 11.6 %collective-permute-start.18 = (f32[1,128,128]{2,1,0:T(8,128)S(1)}, f32[1,128,128]{2,1,0:T(8,128)S(1)}, u32[]{:S(2)}, u32[]{:S(2)}) collective-permute-start(f32[1,128,128]{2,1,0:T(8,128)S(1)} %get-tuple-element.11), channel_id=1, source_target_pairs={{0,72},{8,80},{16,88},{24,96},{32,104},{40,112},{48,120},{56,0},{6... | collective-permute-start | bytes 196616 | tf_op jit(solution)/shard_map/ppermute | solution.py:101
  441.3 10.4 %collective-permute-start.19 = (f32[1,128,128]{2,1,0:T(8,128)S(1)}, f32[1,128,128]{2,1,0:T(8,128)S(1)}, u32[]{:S(2)}, u32[]{:S(2)}) collective-permute-start(f32[1,128,128]{2,1,0:T(8,128)S(1)} %get-tuple-element.10), channel_id=1, source_target_pairs={{0,80},{8,88},{16,96},{24,104},{32,112},{40,120},{48,0},{56,8},{64... | collective-permute-start | bytes 196616 | tf_op jit(solution)/shard_map/ppermute | solution.py:101
  442.4 10.5 %collective-permute-start.20 = (f32[1,128,128]{2,1,0:T(8,128)S(1)}, f32[1,128,128]{2,1,0:T(8,128)S(1)}, u32[]{:S(2)}, u32[]{:S(2)}) collective-permute-start(f32[1,128,128]{2,1,0:T(8,128)S(1)} %get-tuple-element.9), channel_id=1, source_target_pairs={{0,88},{8,96},{16,104},{24,112},{32,120},{40,0},{48,8},{56,16},{64... | collective-permute-start | bytes 196616 | tf_op jit(solution)/shard_map/ppermute | solution.py:101
  445.7 7.3 %collective-permute-start.21 = (f32[1,128,128]{2,1,0:T(8,128)S(1)}, f32[1,128,128]{2,1,0:T(8,128)S(1)}, u32[]{:S(2)}, u32[]{:S(2)}) collective-permute-start(f32[1,128,128]{2,1,0:T(8,128)S(1)} %get-tuple-element.8), channel_id=1, source_target_pairs={{0,96},{8,104},{16,112},{24,120},{32,0},{40,8},{48,16},{56,24},{64... | collective-permute-start | bytes 196616 | tf_op jit(solution)/shard_map/ppermute | solution.py:101
  (17 other events, 249.3 us)

commit v8 on v7

--- a/solution.py
+++ b/solution.py
@@ -125,12 +125,13 @@
         following = send(f + 1)
         smoothed.append(proc(incoming))
         incoming = following
+    early = spread_x(smoothed.pop())
     first = gather_x(jnp.stack(smoothed, axis=0))
     last = proc(incoming)
     last = spread_x(last)
-    spare = jnp.zeros((1,) + first.shape[1:], first.dtype)
+    spare = jnp.zeros((2,) + first.shape[1:], first.dtype)
     result = along_x(jnp.concatenate([first, spare], axis=0))
-    return lax.dynamic_update_slice_in_dim(result, along_x(last), fields - 1, axis=0)
+    return lax.dynamic_update_slice_in_dim(result, along_x(jnp.concatenate([early, last], axis=0)), fields - 2, axis=0)
 
 
 def solution(mesh):

time: 490 us -> 577 us (1.18)
  the two profiles are of different devices: /device:TPU:4 before, /device:TPU:8 now
where the time goes in v8:
time: 577 us; the launch traced here: 567 us
  waiting for transfers between devices  211 us (37%)
  local copies, waits for them, and re-layouts  138 us (24%)
  starting transfers between devices  134 us (23%)
  matrix products  73 us (13%)
  other arithmetic  9.3 us (2%)
    all_to_all x5, waiting for transfers between devices, send(): return lax.all_to_all(outgoing, ('gx', 'gy'), 0, 0, tiled=True)  181 us
    ppermute x30, starting transfers between devices, spread_x(): lax.ppermute(piece, 'gx', [(g, (g + shift) % across) for g in range(acros...  62.2 us
    reshape x10, local copies, waits for them, and re-layouts, proc(): deposited = deposited.reshape(planes, height, width)  55 us
    unnamed x55, local copies, waits for them, and re-layouts  40.2 us
    all_to_all x5, starting transfers between devices, send(): return lax.all_to_all(outgoing, ('gx', 'gy'), 0, 0, tiled=True)  37.1 us
    ppermute x30, waiting for transfers between devices, spread_x(): lax.ppermute(piece, 'gx', [(g, (g + shift) % across) for g in range(acros...  29.5 us
    dot_general x5, matrix products, proc(): jnp.einsum('ts,src->trc', landing, incoming, preferred_element_type=jnp.f...  20.4 us
    ppermute x5, starting transfers between devices, halo(): lax.ppermute(tail, axis, [(i, (i + 1) % count) for i in range(ends)])  18.8 us
  transfers between devices with their start and end apart: 46, of which 6 were waited for; matrix products, arithmetic and copies ran while one was open for 35% of the time, Pallas kernels for 0%

profile of v8, /device:TPU:8, one launch (start us, length us, event | category | flops | bytes accessed | tf_op | source)
XLA Modules:
  0.0 567.1 jit_solution(11292700902733612912)
XLA Ops:
  6.7 10.9 %all-to-all-start.5 = ((bf16[128,128,128]{2,1,0:T(8,128)(2,1)}), bf16[128,128,128]{2,1,0:T(8,128)(2,1)}, u32[]{:S(2)}, u32[]{:S(2)}) async-start(bf16[128,128,128]{2,1,0:T(8,128)(2,1)} %bitcast.134), calls=%async_computation.5 | async-start | bytes 8388608 | tf_op jit(solution)/shard_map/all_to_all | solution.py:71
  24.3 45.0 %all-to-all-done.5 = bf16[128,128,128]{2,1,0:T(8,128)(2,1)} async-done(((bf16[128,128,128]{2,1,0:T(8,128)(2,1)}), bf16[128,128,128]{2,1,0:T(8,128)(2,1)}, u32[]{:S(2)}, u32[]{:S(2)}) %all-to-all-start.5) | async-done | bytes 4194336 | tf_op jit(solution)/shard_map/all_to_all | solution.py:71
  69.3 6.4 %all-to-all-start.4 = ((bf16[128,128,128]{2,1,0:T(8,128)(2,1)}), bf16[128,128,128]{2,1,0:T(8,128)(2,1)}, u32[]{:S(2)}, u32[]{:S(2)}) async-start(bf16[128,128,128]{2,1,0:T(8,128)(2,1)} %bitcast.132), calls=%async_computation.4 | async-start | bytes 8388608 | tf_op jit(solution)/shard_map/all_to_all | solution.py:71
  82.4 45.1 %all-to-all-done.4 = bf16[128,128,128]{2,1,0:T(8,128)(2,1)} async-done(((bf16[128,128,128]{2,1,0:T(8,128)(2,1)}), bf16[128,128,128]{2,1,0:T(8,128)(2,1)}, u32[]{:S(2)}, u32[]{:S(2)}) %all-to-all-start.4) | async-done | bytes 4194336 | tf_op jit(solution)/shard_map/all_to_all | solution.py:71
  127.5 6.5 %all-to-all-start.1 = ((bf16[128,128,128]{2,1,0:T(8,128)(2,1)}), bf16[128,128,128]{2,1,0:T(8,128)(2,1)}, u32[]{:S(2)}, u32[]{:S(2)}) async-start(bf16[128,128,128]{2,1,0:T(8,128)(2,1)} %bitcast.131), calls=%async_computation.1 | async-start | bytes 8388608 | tf_op jit(solution)/shard_map/all_to_all | solution.py:71
  142.3 43.5 %all-to-all-done.1 = bf16[128,128,128]{2,1,0:T(8,128)(2,1)} async-done(((bf16[128,128,128]{2,1,0:T(8,128)(2,1)}), bf16[128,128,128]{2,1,0:T(8,128)(2,1)}, u32[]{:S(2)}, u32[]{:S(2)}) %all-to-all-start.1) | async-done | bytes 4194336 | tf_op jit(solution)/shard_map/all_to_all | solution.py:71
  185.8 6.8 %all-to-all-start = ((bf16[128,136,128]{2,1,0:T(8,128)(2,1)}), bf16[128,136,128]{2,1,0:T(8,128)(2,1)}, u32[]{:S(2)}, u32[]{:S(2)}) async-start(bf16[128,136,128]{2,1,0:T(8,128)(2,1)} %pad_maximum_fusion), calls=%async_computation | async-start | bytes 8912896 | tf_op jit(solution)/shard_map/all_to_all | solution.py:71
  199.2 47.8 %all-to-all-done = bf16[128,136,128]{2,1,0:T(8,128)(2,1)} async-done(((bf16[128,136,128]{2,1,0:T(8,128)(2,1)}), bf16[128,136,128]{2,1,0:T(8,128)(2,1)}, u32[]{:S(2)}, u32[]{:S(2)}) %all-to-all-start) | async-done | bytes 4456480 | tf_op jit(solution)/shard_map/all_to_all | solution.py:71
  247.0 6.5 %all-to-all-start.2 = ((bf16[128,128,128]{2,1,0:T(8,128)(2,1)}), bf16[128,128,128]{2,1,0:T(8,128)(2,1)}, u32[]{:S(2)}, u32[]{:S(2)}) async-start(bf16[128,128,128]{2,1,0:T(8,128)(2,1)} %bitcast.130), calls=%async_computation.2 | async-start | bytes 8388608 | tf_op jit(solution)/shard_map/all_to_all | solution.py:71
  257.7 4.5 fusion.8
  265.0 6.9 %copy.131 = f32[16,4,32,4,32]{4,3,0,2,1:T(4,128)} copy(f32[16,4,32,4,32]{4,2,0,3,1:T(8,128)} %bitcast.125) | data formatting | bytes 2097152 | tf_op jit(solution)/shard_map/reshape | solution.py:88
  281.0 4.5 fusion.10
  288.4 6.9 %copy.130 = f32[16,4,32,4,32]{4,3,0,2,1:T(4,128)} copy(f32[16,4,32,4,32]{4,2,0,3,1:T(8,128)} %bitcast.126) | data formatting | bytes 2097152 | tf_op jit(solution)/shard_map/reshape | solution.py:88
  313.8 6.9 %copy.127 = f32[16,4,32,4,32]{4,3,0,2,1:T(4,128)} copy(f32[16,4,32,4,32]{4,2,0,3,1:T(8,128)} %bitcast.127) | data formatting | bytes 2097152 | tf_op jit(solution)/shard_map/reshape | solution.py:88
  337.3 6.9 %copy.128 = f32[16,4,32,4,32]{4,3,0,2,1:T(4,128)} copy(f32[16,4,32,4,32]{4,2,0,3,1:T(8,128)} %bitcast.128) | data formatting | bytes 2097152 | tf_op jit(solution)/shard_map/reshape | solution.py:88
  344.1 4.5 reshape.121
  360.5 6.9 %copy.129 = f32[16,4,32,4,32]{4,3,0,2,1:T(4,128)} copy(f32[16,4,32,4,32]{4,2,0,3,1:T(8,128)} %bitcast.129) | data formatting | bytes 2097152 | tf_op jit(solution)/shard_map/reshape | solution.py:88
  367.3 4.9 reshape.122
  418.3 8.6 %all-to-all-start.3 = ((f32[3,16,128,128]{3,2,0,1:T(8,128)}), f32[3,16,128,128]{3,2,0,1:T(8,128)S(1)}, u32[]{:S(2)}, u32[]{:S(2)}) async-start(f32[3,16,128,128]{3,2,0,1:T(8,128)} %copy.110), calls=%async_computation.3 | async-start | bytes 6291456 | tf_op jit(solution)/shard_map/all_to_all | solution.py:94
  448.0 28.3 %collective-permute-done.30 = f32[1,128,128]{2,1,0:T(8,128)S(1)} collective-permute-done((f32[1,128,128]{2,1,0:T(8,128)}, f32[1,128,128]{2,1,0:T(8,128)S(1)}, u32[]{:S(2)}, u32[]{:S(2)}) %collective-permute-start.30) | collective-permute-done | bytes 65568 | tf_op jit(solution)/shard_map/ppermute | solution.py:101
  482.4 6.7 %collective-permute-start.38 = (f32[1,128,128]{2,1,0:T(8,128)}, f32[1,128,128]{2,1,0:T(8,128)S(1)}, u32[]{:S(2)}, u32[]{:S(2)}) collective-permute-start(f32[1,128,128]{2,1,0:T(8,128)} %get-tuple-element.25), channel_id=1, source_target_pairs={{0,112},{8,120},{16,0},{24,8},{32,16},{40,24},{48,32},{56,40},{64,... | collective-permute-start | bytes 196616 | tf_op jit(solution)/shard_map/ppermute | solution.py:101
  529.7 4.7 collective-permute-start.21
  553.7 5.4 fusion
  559.1 6.0 %copy.122 = f32[5,1,128,2048]{3,2,1,0:T(8,128)} copy(f32[5,1,128,2048]{2,3,0,1:T(8,128)} %bitcast.124) | data formatting | bytes 10485760 | tf_op jit(solution)/shard_map/reshape | solution.py:118
  (205 shorter events, 233.8 us)
Async XLA Ops:
  6.7 62.6 %all-to-all-start.5 = ((bf16[128,128,128]{2,1,0:T(8,128)(2,1)}), bf16[128,128,128]{2,1,0:T(8,128)(2,1)}, u32[]{:S(2)}, u32[]{:S(2)}) async-start(bf16[128,128,128]{2,1,0:T(8,128)(2,1)} %bitcast.134), calls=%async_computation.5 | async-start | bytes 8388608 | tf_op jit(solution)/shard_map/all_to_all | solution.py:71
  69.3 58.2 %all-to-all-start.4 = ((bf16[128,128,128]{2,1,0:T(8,128)(2,1)}), bf16[128,128,128]{2,1,0:T(8,128)(2,1)}, u32[]{:S(2)}, u32[]{:S(2)}) async-start(bf16[128,128,128]{2,1,0:T(8,128)(2,1)} %bitcast.132), calls=%async_computation.4 | async-start | bytes 8388608 | tf_op jit(solution)/shard_map/all_to_all | solution.py:71
  127.5 58.3 %all-to-all-start.1 = ((bf16[128,128,128]{2,1,0:T(8,128)(2,1)}), bf16[128,128,128]{2,1,0:T(8,128)(2,1)}, u32[]{:S(2)}, u32[]{:S(2)}) async-start(bf16[128,128,128]{2,1,0:T(8,128)(2,1)} %bitcast.131), calls=%async_computation.1 | async-start | bytes 8388608 | tf_op jit(solution)/shard_map/all_to_all | solution.py:71
  185.8 61.2 %all-to-all-start = ((bf16[128,136,128]{2,1,0:T(8,128)(2,1)}), bf16[128,136,128]{2,1,0:T(8,128)(2,1)}, u32[]{:S(2)}, u32[]{:S(2)}) async-start(bf16[128,136,128]{2,1,0:T(8,128)(2,1)} %pad_maximum_fusion), calls=%async_computation | async-start | bytes 8912896 | tf_op jit(solution)/shard_map/all_to_all | solution.py:71
  247.0 103.9 %all-to-all-start.2 = ((bf16[128,128,128]{2,1,0:T(8,128)(2,1)}), bf16[128,128,128]{2,1,0:T(8,128)(2,1)}, u32[]{:S(2)}, u32[]{:S(2)}) async-start(bf16[128,128,128]{2,1,0:T(8,128)(2,1)} %bitcast.130), calls=%async_computation.2 | async-start | bytes 8388608 | tf_op jit(solution)/shard_map/all_to_all | solution.py:71
  277.3 97.3 %collective-permute-start.23 = (f32[16,4,128]{2,0,1:T(8,128)}, f32[16,4,128]{2,0,1:T(8,128)S(1)}, u32[]{:S(2)}, u32[]{:S(2)}) collective-permute-start(f32[16,4,128]{2,0,1:T(8,128)} %get-tuple-element.40), channel_id=1, source_target_pairs={{0,1},{1,2},{2,3},{3,4},{4,5},{5,6},{6,7},{8,9},{9,10},{10,11},{11... | collective-permute-start | bytes 98312 | tf_op jit(solution)/shard_map/ppermute | solution.py:44
  279.3 96.6 %collective-permute-start.24 = (f32[16,4,128]{2,0,1:T(8,128)S(1)}, f32[16,4,128]{2,0,1:T(8,128)S(1)}, u32[]{:S(2)}, u32[]{:S(2)}) collective-permute-start(f32[16,4,128]{2,0,1:T(8,128)S(1)} %get-tuple-element.41), channel_id=1, source_target_pairs={{1,0},{2,1},{3,2},{4,3},{5,4},{6,5},{7,6},{9,8},{10,9},{11,10},{12... | collective-permute-start | bytes 98312 | tf_op jit(solution)/shard_map/ppermute | solution.py:46
  300.6 83.2 %collective-permute-start.6 = (f32[16,4,128]{2,0,1:T(8,128)}, f32[16,4,128]{2,0,1:T(8,128)S(1)}, u32[]{:S(2)}, u32[]{:S(2)}) collective-permute-start(f32[16,4,128]{2,0,1:T(8,128)} %get-tuple-element.22), channel_id=1, source_target_pairs={{0,1},{1,2},{2,3},{3,4},{4,5},{5,6},{6,7},{8,9},{9,10},{10,11},{11... | collective-permute-start | bytes 98312 | tf_op jit(solution)/shard_map/ppermute | solution.py:44
  304.7 80.5 %collective-permute-start.7 = (f32[16,4,128]{2,0,1:T(8,128)}, f32[16,4,128]{2,0,1:T(8,128)S(1)}, u32[]{:S(2)}, u32[]{:S(2)}) collective-permute-start(f32[16,4,128]{2,0,1:T(8,128)} %get-tuple-element.23), channel_id=1, source_target_pairs={{1,0},{2,1},{3,2},{4,3},{5,4},{6,5},{7,6},{9,8},{10,9},{11,10},{12... | collective-permute-start | bytes 98312 | tf_op jit(solution)/shard_map/ppermute | solution.py:46
  325.4 68.8 %collective-permute-start = (f32[16,4,128]{2,0,1:T(8,128)S(1)}, f32[16,4,128]{2,0,1:T(8,128)S(1)}, u32[]{:S(2)}, u32[]{:S(2)}) collective-permute-start(f32[16,4,128]{2,0,1:T(8,128)S(1)} %get-tuple-element.42), channel_id=1, source_target_pairs={{0,1},{1,2},{2,3},{3,4},{4,5},{5,6},{6,7},{8,9},{9,10},{10,11},{11... | collective-permute-start | bytes 98312 | tf_op jit(solution)/shard_map/ppermute | solution.py:44
  375.9 25.1 %collective-permute-start.2 = (f32[16,4,128]{2,0,1:T(8,128)S(1)}, f32[16,4,128]{2,0,1:T(8,128)S(1)}, u32[]{:S(2)}, u32[]{:S(2)}) collective-permute-start(f32[16,4,128]{2,0,1:T(8,128)S(1)} %get-tuple-element.44), channel_id=1, source_target_pairs={{0,1},{1,2},{2,3},{3,4},{4,5},{5,6},{6,7},{8,9},{9,10},{10,11},{11... | collective-permute-start | bytes 98312 | tf_op jit(solution)/shard_map/ppermute | solution.py:44
  385.2 24.0 %collective-permute-start.4 = (f32[16,4,128]{2,0,1:T(8,128)S(1)}, f32[16,4,128]{2,0,1:T(8,128)S(1)}, u32[]{:S(2)}, u32[]{:S(2)}) collective-permute-start(f32[16,4,128]{2,0,1:T(8,128)S(1)} %get-tuple-element.46), channel_id=1, source_target_pairs={{0,1},{1,2},{2,3},{3,4},{4,5},{5,6},{6,7},{8,9},{9,10},{10,11},{11... | collective-permute-start | bytes 98312 | tf_op jit(solution)/shard_map/ppermute | solution.py:44
  395.5 31.4 %collective-permute-start.25 = (f32[1,128,128]{2,1,0:T(8,128)}, f32[1,128,128]{2,1,0:T(8,128)}, u32[]{:S(2)}, u32[]{:S(2)}) collective-permute-start(f32[1,128,128]{2,1,0:T(8,128)} %get-tuple-element.38), channel_id=1, source_target_pairs={{0,8},{8,16},{16,24},{24,32},{32,40},{40,48},{48,56},{56,64},{64,7... | collective-permute-start | bytes 196616 | tf_op jit(solution)/shard_map/ppermute | solution.py:101
  401.0 30.4 %collective-permute-start.26 = (f32[1,128,128]{2,1,0:T(8,128)}, f32[1,128,128]{2,1,0:T(8,128)}, u32[]{:S(2)}, u32[]{:S(2)}) collective-permute-start(f32[1,128,128]{2,1,0:T(8,128)} %get-tuple-element.37), channel_id=1, source_target_pairs={{0,16},{8,24},{16,32},{24,40},{32,48},{40,56},{48,64},{56,72},{64,... | collective-permute-start | bytes 196616 | tf_op jit(solution)/shard_map/ppermute | solution.py:101
  403.2 33.2 %collective-permute-start.27 = (f32[1,128,128]{2,1,0:T(8,128)}, f32[1,128,128]{2,1,0:T(8,128)}, u32[]{:S(2)}, u32[]{:S(2)}) collective-permute-start(f32[1,128,128]{2,1,0:T(8,128)} %get-tuple-element.36), channel_id=1, source_target_pairs={{0,24},{8,32},{16,40},{24,48},{32,56},{40,64},{48,72},{56,80},{64,... | collective-permute-start | bytes 196616 | tf_op jit(solution)/shard_map/ppermute | solution.py:101
  409.2 29.6 %collective-permute-start.28 = (f32[1,128,128]{2,1,0:T(8,128)}, f32[1,128,128]{2,1,0:T(8,128)}, u32[]{:S(2)}, u32[]{:S(2)}) collective-permute-start(f32[1,128,128]{2,1,0:T(8,128)} %get-tuple-element.35), channel_id=1, source_target_pairs={{0,32},{8,40},{16,48},{24,56},{32,64},{40,72},{48,80},{56,88},{64,... | collective-permute-start | bytes 196616 | tf_op jit(solution)/shard_map/ppermute | solution.py:101
  411.0 31.9 %collective-permute-start.29 = (f32[1,128,128]{2,1,0:T(8,128)}, f32[1,128,128]{2,1,0:T(8,128)}, u32[]{:S(2)}, u32[]{:S(2)}) collective-permute-start(f32[1,128,128]{2,1,0:T(8,128)} %get-tuple-element.34), channel_id=1, source_target_pairs={{0,40},{8,48},{16,56},{24,64},{32,72},{40,80},{48,88},{56,96},{64,... | collective-permute-start | bytes 196616 | tf_op jit(solution)/shard_map/ppermute | solution.py:101
  418.3 133.5 %all-to-all-start.3 = ((f32[3,16,128,128]{3,2,0,1:T(8,128)}), f32[3,16,128,128]{3,2,0,1:T(8,128)S(1)}, u32[]{:S(2)}, u32[]{:S(2)}) async-start(f32[3,16,128,128]{3,2,0,1:T(8,128)} %copy.110), calls=%async_computation.3 | async-start | bytes 6291456 | tf_op jit(solution)/shard_map/all_to_all | solution.py:94
  426.9 49.4 %collective-permute-start.30 = (f32[1,128,128]{2,1,0:T(8,128)}, f32[1,128,128]{2,1,0:T(8,128)S(1)}, u32[]{:S(2)}, u32[]{:S(2)}) collective-permute-start(f32[1,128,128]{2,1,0:T(8,128)} %get-tuple-element.33), channel_id=1, source_target_pairs={{0,48},{8,56},{16,64},{24,72},{32,80},{40,88},{48,96},{56,104},{64... | collective-permute-start | bytes 196616 | tf_op jit(solution)/shard_map/ppermute | solution.py:101
  431.4 48.7 %collective-permute-start.31 = (f32[1,128,128]{2,1,0:T(8,128)}, f32[1,128,128]{2,1,0:T(8,128)S(1)}, u32[]{:S(2)}, u32[]{:S(2)}) collective-permute-start(f32[1,128,128]{2,1,0:T(8,128)} %get-tuple-element.32), channel_id=1, source_target_pairs={{0,56},{8,64},{16,72},{24,80},{32,88},{40,96},{48,104},{56,112},{6... | collective-permute-start | bytes 196616 | tf_op jit(solution)/shard_map/ppermute | solution.py:101
  436.5 45.4 %collective-permute-start.32 = (f32[1,128,128]{2,1,0:T(8,128)}, f32[1,128,128]{2,1,0:T(8,128)S(1)}, u32[]{:S(2)}, u32[]{:S(2)}) collective-permute-start(f32[1,128,128]{2,1,0:T(8,128)} %get-tuple-element.31), channel_id=1, source_target_pairs={{0,64},{8,72},{16,80},{24,88},{32,96},{40,104},{48,112},{56,120},{... | collective-permute-start | bytes 196616 | tf_op jit(solution)/shard_map/ppermute | solution.py:101
  438.8 43.7 %collective-permute-start.33 = (f32[1,128,128]{2,1,0:T(8,128)}, f32[1,128,128]{2,1,0:T(8,128)S(1)}, u32[]{:S(2)}, u32[]{:S(2)}) collective-permute-start(f32[1,128,128]{2,1,0:T(8,128)} %get-tuple-element.30), channel_id=1, source_target_pairs={{0,72},{8,80},{16,88},{24,96},{32,104},{40,112},{48,120},{56,0},{6... | collective-permute-start | bytes 196616 | tf_op jit(solution)/shard_map/ppermute | solution.py:101
  442.9 46.8 %collective-permute-start.34 = (f32[1,128,128]{2,1,0:T(8,128)}, f32[1,128,128]{2,1,0:T(8,128)S(1)}, u32[]{:S(2)}, u32[]{:S(2)}) collective-permute-start(f32[1,128,128]{2,1,0:T(8,128)} %get-tuple-element.29), channel_id=1, source_target_pairs={{0,80},{8,88},{16,96},{24,104},{32,112},{40,120},{48,0},{56,8},{64... | collective-permute-start | bytes 196616 | tf_op jit(solution)/shard_map/ppermute | solution.py:101
  497.3 23.0 %collective-permute-start.12 = (f32[1,128,128]{2,1,0:T(8,128)}, f32[1,128,128]{2,1,0:T(8,128)}, u32[]{:S(2)}, u32[]{:S(2)}) collective-permute-start(f32[1,128,128]{2,1,0:T(8,128)} %get-tuple-element.16), channel_id=1, source_target_pairs={{0,40},{8,48},{16,56},{24,64},{32,72},{40,80},{48,88},{56,96},{64,... | collective-permute-start | bytes 196616 | tf_op jit(solution)/shard_map/ppermute | solution.py:101
  (33 other events, 486.6 us)

commit v9 on v7

--- a/solution.py
+++ b/solution.py
@@ -109,10 +109,12 @@
         padded = jnp.concatenate([edge, blocks, edge], axis=1)
         result = jnp.einsum("fjxy,xo->fyjo", padded[:, 1 : across + 1], w_mid, precision=HIGHEST)
         reach = width - RADIUS
-        from_left = jnp.einsum("fjxy,xo->fyjo", padded[:, 0:across, reach:], w_left[reach:, :RADIUS], precision=HIGHEST)
-        from_right = jnp.einsum(
-            "fjxy,xo->fyjo", padded[:, 2 : across + 2, :RADIUS], w_right[:RADIUS, reach:], precision=HIGHEST
-        )
+        from_left = jnp.sum(
+            padded[:, 0:across, reach:, :, None] * w_left[reach:, :RADIUS][:, None, :], axis=2
+        ).transpose(0, 2, 1, 3)
+        from_right = jnp.sum(
+            padded[:, 2 : across + 2, :RADIUS, :, None] * w_right[:RADIUS, reach:][:, None, :], axis=2
+        ).transpose(0, 2, 1, 3)
         zeros = jnp.zeros(from_left.shape[:3] + (reach,), result.dtype)
         result = result + jnp.concatenate([from_left, zeros], axis=3) + jnp.concatenate([zeros, from_right], axis=3)
         return result.reshape(count, 1, height, across * width)

time: 490 us -> 529 us (1.080)
  waiting for transfers between devices: 182 us -> 221 us
    all_to_all x5, waiting for transfers between devices: 154 us -> 177 us  [send(): return lax.all_to_all(outgoing, ('gx', 'gy'), 0, 0, tiled=True)]
    ppermute x15, waiting for transfers between devices: 25.8 us -> 42.4 us  [spread_x(): lax.ppermute(piece, 'gx', [(g, (g + shift) % across) for g in range(acros...]
    unnamed x39 -> x37, local copies, waits for them, and re-layouts: 14.6 us -> 14.7 us
  transfers between devices with their start and end apart: 31 -> 31, of which waited for: 10 -> 9; matrix products, arithmetic and copies ran while one was open for 33% -> 29% of each run, Pallas kernels for 0% -> 0%
where the time goes in v9:
time: 529 us; the launch traced here: 519 us
  waiting for transfers between devices  221 us (42%)
  starting transfers between devices  111 us (21%)
  local copies, waits for them, and re-layouts  105 us (20%)
  matrix products  72.4 us (14%)
  other arithmetic  7.39 us (1%)
    all_to_all x5, waiting for transfers between devices, send(): return lax.all_to_all(outgoing, ('gx', 'gy'), 0, 0, tiled=True)  177 us
    reshape x10, local copies, waits for them, and re-layouts, proc(): deposited = deposited.reshape(planes, height, width)  55.4 us
    ppermute x15, waiting for transfers between devices, spread_x(): lax.ppermute(piece, 'gx', [(g, (g + shift) % across) for g in range(acros...  42.4 us
    all_to_all x5, starting transfers between devices, send(): return lax.all_to_all(outgoing, ('gx', 'gy'), 0, 0, tiled=True)  41.4 us
    ppermute x15, starting transfers between devices, spread_x(): lax.ppermute(piece, 'gx', [(g, (g + shift) % across) for g in range(acros...  33.6 us
    dot_general x5, matrix products, proc(): jnp.einsum('ts,src->trc', landing, incoming, preferred_element_type=jnp.f...  20.4 us
    ppermute x5, starting transfers between devices, halo(): lax.ppermute(head, axis, [((i + 1) % count, i) for i in range(ends)])  18.3 us
    dot_general x5, matrix products, proc(): return jnp.einsum('iy,zix->zxy', wy, padded, precision=HIGHEST)  17.6 us
  transfers between devices with their start and end apart: 31, of which 9 were waited for; matrix products, arithmetic and copies ran while one was open for 29% of the time, Pallas kernels for 0%

profile of v9, /device:TPU:4, one launch (start us, length us, event | category | flops | bytes accessed | tf_op | source)
XLA Modules:
  0.0 518.6 jit_solution(17040535620023498281)
XLA Ops:
  6.7 11.0 %all-to-all-start.5 = ((bf16[128,128,128]{2,1,0:T(8,128)(2,1)}), bf16[128,128,128]{2,1,0:T(8,128)(2,1)}, u32[]{:S(2)}, u32[]{:S(2)}) async-start(bf16[128,128,128]{2,1,0:T(8,128)(2,1)} %bitcast.139), calls=%async_computation.5 | async-start | bytes 8388608 | tf_op jit(solution)/shard_map/all_to_all | solution.py:71
  24.3 43.9 %all-to-all-done.5 = bf16[128,128,128]{2,1,0:T(8,128)(2,1)} async-done(((bf16[128,128,128]{2,1,0:T(8,128)(2,1)}), bf16[128,128,128]{2,1,0:T(8,128)(2,1)}, u32[]{:S(2)}, u32[]{:S(2)}) %all-to-all-start.5) | async-done | bytes 4194336 | tf_op jit(solution)/shard_map/all_to_all | solution.py:71
  68.2 7.5 %all-to-all-start.1 = ((bf16[128,128,128]{2,1,0:T(8,128)(2,1)}), bf16[128,128,128]{2,1,0:T(8,128)(2,1)}, u32[]{:S(2)}, u32[]{:S(2)}) async-start(bf16[128,128,128]{2,1,0:T(8,128)(2,1)} %bitcast.137), calls=%async_computation.1 | async-start | bytes 8388608 | tf_op jit(solution)/shard_map/all_to_all | solution.py:71
  82.4 44.1 %all-to-all-done.1 = bf16[128,128,128]{2,1,0:T(8,128)(2,1)} async-done(((bf16[128,128,128]{2,1,0:T(8,128)(2,1)}), bf16[128,128,128]{2,1,0:T(8,128)(2,1)}, u32[]{:S(2)}, u32[]{:S(2)}) %all-to-all-start.1) | async-done | bytes 4194336 | tf_op jit(solution)/shard_map/all_to_all | solution.py:71
  126.5 7.5 %all-to-all-start.2 = ((bf16[128,128,128]{2,1,0:T(8,128)(2,1)}), bf16[128,128,128]{2,1,0:T(8,128)(2,1)}, u32[]{:S(2)}, u32[]{:S(2)}) async-start(bf16[128,128,128]{2,1,0:T(8,128)(2,1)} %bitcast.136), calls=%async_computation.2 | async-start | bytes 8388608 | tf_op jit(solution)/shard_map/all_to_all | solution.py:71
  142.3 42.4 %all-to-all-done.2 = bf16[128,128,128]{2,1,0:T(8,128)(2,1)} async-done(((bf16[128,128,128]{2,1,0:T(8,128)(2,1)}), bf16[128,128,128]{2,1,0:T(8,128)(2,1)}, u32[]{:S(2)}, u32[]{:S(2)}) %all-to-all-start.2) | async-done | bytes 4194336 | tf_op jit(solution)/shard_map/all_to_all | solution.py:71
  184.7 7.9 %all-to-all-start = ((bf16[128,136,128]{2,1,0:T(8,128)(2,1)}), bf16[128,136,128]{2,1,0:T(8,128)(2,1)}, u32[]{:S(2)}, u32[]{:S(2)}) async-start(bf16[128,136,128]{2,1,0:T(8,128)(2,1)} %pad_maximum_fusion), calls=%async_computation | async-start | bytes 8912896 | tf_op jit(solution)/shard_map/all_to_all | solution.py:71
  199.3 46.7 %all-to-all-done = bf16[128,136,128]{2,1,0:T(8,128)(2,1)} async-done(((bf16[128,136,128]{2,1,0:T(8,128)(2,1)}), bf16[128,136,128]{2,1,0:T(8,128)(2,1)}, u32[]{:S(2)}, u32[]{:S(2)}) %all-to-all-start) | async-done | bytes 4456480 | tf_op jit(solution)/shard_map/all_to_all | solution.py:71
  246.0 7.5 %all-to-all-start.3 = ((bf16[128,128,128]{2,1,0:T(8,128)(2,1)}), bf16[128,128,128]{2,1,0:T(8,128)(2,1)}, u32[]{:S(2)}, u32[]{:S(2)}) async-start(bf16[128,128,128]{2,1,0:T(8,128)(2,1)} %bitcast.135), calls=%async_computation.3 | async-start | bytes 8388608 | tf_op jit(solution)/shard_map/all_to_all | solution.py:71
  256.9 4.5 fusion.8
  264.2 6.9 %copy.137 = f32[16,4,32,4,32]{4,3,0,2,1:T(4,128)} copy(f32[16,4,32,4,32]{4,2,0,3,1:T(8,128)} %bitcast.130) | data formatting | bytes 2097152 | tf_op jit(solution)/shard_map/reshape | solution.py:88
  271.1 4.5 reshape.189
  283.7 6.9 %copy.133 = f32[16,4,32,4,32]{4,3,0,2,1:T(4,128)} copy(f32[16,4,32,4,32]{4,2,0,3,1:T(8,128)} %bitcast.131) | data formatting | bytes 2097152 | tf_op jit(solution)/shard_map/reshape | solution.py:88
  300.9 4.5 fusion.14
  308.4 6.9 %copy.134 = f32[16,4,32,4,32]{4,3,0,2,1:T(4,128)} copy(f32[16,4,32,4,32]{4,2,0,3,1:T(8,128)} %bitcast.132) | data formatting | bytes 2097152 | tf_op jit(solution)/shard_map/reshape | solution.py:88
  333.2 6.9 %copy.135 = f32[16,4,32,4,32]{4,3,0,2,1:T(4,128)} copy(f32[16,4,32,4,32]{4,2,0,3,1:T(8,128)} %bitcast.133) | data formatting | bytes 2097152 | tf_op jit(solution)/shard_map/reshape | solution.py:88
  340.0 4.5 reshape.187
  359.2 6.9 %copy.136 = f32[16,4,32,4,32]{4,3,0,2,1:T(4,128)} copy(f32[16,4,32,4,32]{4,2,0,3,1:T(8,128)} %bitcast.134) | data formatting | bytes 2097152 | tf_op jit(solution)/shard_map/reshape | solution.py:88
  366.1 4.6 reshape.188
  399.6 7.8 %all-to-all-start.4 = ((f32[4,16,128,128]{3,2,0,1:T(8,128)}), f32[4,16,128,128]{3,2,0,1:T(8,128)}, u32[]{:S(2)}, u32[]{:S(2)}) async-start(f32[4,16,128,128]{3,2,0,1:T(8,128)} %copy.115), calls=%async_computation.4 | async-start | bytes 8388608 | tf_op jit(solution)/shard_map/all_to_all | solution.py:94
  429.3 35.7 %collective-permute-done.10 = f32[1,128,128]{2,1,0:T(8,128)S(1)} collective-permute-done((f32[1,128,128]{2,1,0:T(8,128)S(1)}, f32[1,128,128]{2,1,0:T(8,128)S(1)}, u32[]{:S(2)}, u32[]{:S(2)}) %collective-permute-start.10) | collective-permute-done | bytes 65568 | tf_op jit(solution)/shard_map/ppermute | solution.py:101
  465.0 6.1 %collective-permute-start.15 = (f32[1,128,128]{2,1,0:T(8,128)S(1)}, f32[1,128,128]{2,1,0:T(8,128)S(1)}, u32[]{:S(2)}, u32[]{:S(2)}) collective-permute-start(f32[1,128,128]{2,1,0:T(8,128)S(1)} %get-tuple-element.18), channel_id=1, source_target_pairs={{0,48},{8,56},{16,64},{24,72},{32,80},{40,88},{48,96},{56,104},{64... | collective-permute-start | bytes 196616 | tf_op jit(solution)/shard_map/ppermute | solution.py:101
  502.5 8.8 %fusion = f32[5,128,16,128]{1,3,2,0:T(8,128)} fusion(f32[5,128,16,4]{1,3,2,0:T(4,128)S(1)} %get-tuple-element.35, f32[5,128,16,4]{1,3,2,0:T(4,128)S(1)} %get-tuple-element.36, f32[128,128,1,1]{0,1,3,2:T(8,128)S(1)} %copy-done.3, f32[4,16,128,128]{3,2,0,1:T(8,128)} %all-to-all-done.4), kind=kOutput, calls=%fused_computation.9 | convolution fusion | flops 1613234176 | bytes 9830400 | tf_op jit(solution)/shard_map/fjxy,xo->fyjo/dot_general | solution.py:110
  511.3 5.9 %copy.130 = f32[5,1,128,2048]{3,2,1,0:T(8,128)} copy(f32[5,1,128,2048]{2,3,0,1:T(8,128)} %bitcast.129) | data formatting | bytes 10485760 | tf_op jit(solution)/shard_map/reshape | solution.py:120
  (161 shorter events, 176.7 us)
Async XLA Ops:
  6.7 61.6 %all-to-all-start.5 = ((bf16[128,128,128]{2,1,0:T(8,128)(2,1)}), bf16[128,128,128]{2,1,0:T(8,128)(2,1)}, u32[]{:S(2)}, u32[]{:S(2)}) async-start(bf16[128,128,128]{2,1,0:T(8,128)(2,1)} %bitcast.139), calls=%async_computation.5 | async-start | bytes 8388608 | tf_op jit(solution)/shard_map/all_to_all | solution.py:71
  68.2 58.2 %all-to-all-start.1 = ((bf16[128,128,128]{2,1,0:T(8,128)(2,1)}), bf16[128,128,128]{2,1,0:T(8,128)(2,1)}, u32[]{:S(2)}, u32[]{:S(2)}) async-start(bf16[128,128,128]{2,1,0:T(8,128)(2,1)} %bitcast.137), calls=%async_computation.1 | async-start | bytes 8388608 | tf_op jit(solution)/shard_map/all_to_all | solution.py:71
  126.5 58.2 %all-to-all-start.2 = ((bf16[128,128,128]{2,1,0:T(8,128)(2,1)}), bf16[128,128,128]{2,1,0:T(8,128)(2,1)}, u32[]{:S(2)}, u32[]{:S(2)}) async-start(bf16[128,128,128]{2,1,0:T(8,128)(2,1)} %bitcast.136), calls=%async_computation.2 | async-start | bytes 8388608 | tf_op jit(solution)/shard_map/all_to_all | solution.py:71
  184.7 61.3 %all-to-all-start = ((bf16[128,136,128]{2,1,0:T(8,128)(2,1)}), bf16[128,136,128]{2,1,0:T(8,128)(2,1)}, u32[]{:S(2)}, u32[]{:S(2)}) async-start(bf16[128,136,128]{2,1,0:T(8,128)(2,1)} %pad_maximum_fusion), calls=%async_computation | async-start | bytes 8912896 | tf_op jit(solution)/shard_map/all_to_all | solution.py:71
  246.0 103.3 %all-to-all-start.3 = ((bf16[128,128,128]{2,1,0:T(8,128)(2,1)}), bf16[128,128,128]{2,1,0:T(8,128)(2,1)}, u32[]{:S(2)}, u32[]{:S(2)}) async-start(bf16[128,128,128]{2,1,0:T(8,128)(2,1)} %bitcast.135), calls=%async_computation.3 | async-start | bytes 8388608 | tf_op jit(solution)/shard_map/all_to_all | solution.py:71
  295.3 77.5 %collective-permute-start = (f32[16,4,128]{2,0,1:T(8,128)S(1)}, f32[16,4,128]{2,0,1:T(8,128)S(1)}, u32[]{:S(2)}, u32[]{:S(2)}) collective-permute-start(f32[16,4,128]{2,0,1:T(8,128)S(1)} %get-tuple-element.27), channel_id=1, source_target_pairs={{0,1},{1,2},{2,3},{3,4},{4,5},{5,6},{6,7},{8,9},{9,10},{10,11},{11... | collective-permute-start | bytes 98312 | tf_op jit(solution)/shard_map/ppermute | solution.py:44
  297.4 79.2 %collective-permute-start.1 = (f32[16,4,128]{2,0,1:T(8,128)S(1)}, f32[16,4,128]{2,0,1:T(8,128)S(1)}, u32[]{:S(2)}, u32[]{:S(2)}) collective-permute-start(f32[16,4,128]{2,0,1:T(8,128)S(1)} %get-tuple-element.28), channel_id=1, source_target_pairs={{1,0},{2,1},{3,2},{4,3},{5,4},{6,5},{7,6},{9,8},{10,9},{11,10},{12... | collective-permute-start | bytes 98312 | tf_op jit(solution)/shard_map/ppermute | solution.py:46
  320.0 62.1 %collective-permute-start.2 = (f32[16,4,128]{2,0,1:T(8,128)S(1)}, f32[16,4,128]{2,0,1:T(8,128)S(1)}, u32[]{:S(2)}, u32[]{:S(2)}) collective-permute-start(f32[16,4,128]{2,0,1:T(8,128)S(1)} %get-tuple-element.29), channel_id=1, source_target_pairs={{0,1},{1,2},{2,3},{3,4},{4,5},{5,6},{6,7},{8,9},{9,10},{10,11},{11... | collective-permute-start | bytes 98312 | tf_op jit(solution)/shard_map/ppermute | solution.py:44
  322.0 64.0 %collective-permute-start.3 = (f32[16,4,128]{2,0,1:T(8,128)S(1)}, f32[16,4,128]{2,0,1:T(8,128)S(1)}, u32[]{:S(2)}, u32[]{:S(2)}) collective-permute-start(f32[16,4,128]{2,0,1:T(8,128)S(1)} %get-tuple-element.30), channel_id=1, source_target_pairs={{1,0},{2,1},{3,2},{4,3},{5,4},{6,5},{7,6},{9,8},{10,9},{11,10},{12... | collective-permute-start | bytes 98312 | tf_op jit(solution)/shard_map/ppermute | solution.py:46
  347.4 42.1 %collective-permute-start.4 = (f32[16,4,128]{2,0,1:T(8,128)}, f32[16,4,128]{2,0,1:T(8,128)S(1)}, u32[]{:S(2)}, u32[]{:S(2)}) collective-permute-start(f32[16,4,128]{2,0,1:T(8,128)} %get-tuple-element.31), channel_id=1, source_target_pairs={{0,1},{1,2},{2,3},{3,4},{4,5},{5,6},{6,7},{8,9},{9,10},{10,11},{11... | collective-permute-start | bytes 98312 | tf_op jit(solution)/shard_map/ppermute | solution.py:44
  372.9 16.7 %collective-permute-start.5 = (f32[16,4,128]{2,0,1:T(8,128)S(1)}, f32[16,4,128]{2,0,1:T(8,128)S(1)}, u32[]{:S(2)}, u32[]{:S(2)}) collective-permute-start(f32[16,4,128]{2,0,1:T(8,128)S(1)} %get-tuple-element.32), channel_id=1, source_target_pairs={{1,0},{2,1},{3,2},{4,3},{5,4},{6,5},{7,6},{9,8},{10,9},{11,10},{12... | collective-permute-start | bytes 98312 | tf_op jit(solution)/shard_map/ppermute | solution.py:46
  376.5 16.6 %collective-permute-start.6 = (f32[16,4,128]{2,0,1:T(8,128)S(1)}, f32[16,4,128]{2,0,1:T(8,128)S(1)}, u32[]{:S(2)}, u32[]{:S(2)}) collective-permute-start(f32[16,4,128]{2,0,1:T(8,128)S(1)} %get-tuple-element.33), channel_id=1, source_target_pairs={{0,1},{1,2},{2,3},{3,4},{4,5},{5,6},{6,7},{8,9},{9,10},{10,11},{11... | collective-permute-start | bytes 98312 | tf_op jit(solution)/shard_map/ppermute | solution.py:44
  382.1 11.1 %collective-permute-start.7 = (f32[16,4,128]{2,0,1:T(8,128)S(1)}, f32[16,4,128]{2,0,1:T(8,128)S(1)}, u32[]{:S(2)}, u32[]{:S(2)}) collective-permute-start(f32[16,4,128]{2,0,1:T(8,128)S(1)} %get-tuple-element.34), channel_id=1, source_target_pairs={{1,0},{2,1},{3,2},{4,3},{5,4},{6,5},{7,6},{9,8},{10,9},{11,10},{12... | collective-permute-start | bytes 98312 | tf_op jit(solution)/shard_map/ppermute | solution.py:46
  399.6 98.5 %all-to-all-start.4 = ((f32[4,16,128,128]{3,2,0,1:T(8,128)}), f32[4,16,128,128]{3,2,0,1:T(8,128)}, u32[]{:S(2)}, u32[]{:S(2)}) async-start(f32[4,16,128,128]{3,2,0,1:T(8,128)} %copy.115), calls=%async_computation.4 | async-start | bytes 8388608 | tf_op jit(solution)/shard_map/all_to_all | solution.py:94
  419.4 45.6 %collective-permute-start.10 = (f32[1,128,128]{2,1,0:T(8,128)S(1)}, f32[1,128,128]{2,1,0:T(8,128)S(1)}, u32[]{:S(2)}, u32[]{:S(2)}) collective-permute-start(f32[1,128,128]{2,1,0:T(8,128)S(1)} %get-tuple-element.23), channel_id=1, source_target_pairs={{0,8},{8,16},{16,24},{24,32},{32,40},{40,48},{48,56},{56,64},{64,7... | collective-permute-start | bytes 196616 | tf_op jit(solution)/shard_map/ppermute | solution.py:101
  421.5 52.8 %collective-permute-start.11 = (f32[1,128,128]{2,1,0:T(8,128)S(1)}, f32[1,128,128]{2,1,0:T(8,128)S(1)}, u32[]{:S(2)}, u32[]{:S(2)}) collective-permute-start(f32[1,128,128]{2,1,0:T(8,128)S(1)} %get-tuple-element.22), channel_id=1, source_target_pairs={{0,16},{8,24},{16,32},{24,40},{32,48},{40,56},{48,64},{56,72},{64,... | collective-permute-start | bytes 196616 | tf_op jit(solution)/shard_map/ppermute | solution.py:101
  424.3 50.1 %collective-permute-start.12 = (f32[1,128,128]{2,1,0:T(8,128)S(1)}, f32[1,128,128]{2,1,0:T(8,128)S(1)}, u32[]{:S(2)}, u32[]{:S(2)}) collective-permute-start(f32[1,128,128]{2,1,0:T(8,128)S(1)} %get-tuple-element.21), channel_id=1, source_target_pairs={{0,24},{8,32},{16,40},{24,48},{32,56},{40,64},{48,72},{56,80},{64,... | collective-permute-start | bytes 196616 | tf_op jit(solution)/shard_map/ppermute | solution.py:101
  426.6 49.0 %collective-permute-start.13 = (f32[1,128,128]{2,1,0:T(8,128)S(1)}, f32[1,128,128]{2,1,0:T(8,128)S(1)}, u32[]{:S(2)}, u32[]{:S(2)}) collective-permute-start(f32[1,128,128]{2,1,0:T(8,128)S(1)} %get-tuple-element.20), channel_id=1, source_target_pairs={{0,32},{8,40},{16,48},{24,56},{32,64},{40,72},{48,80},{56,88},{64,... | collective-permute-start | bytes 196616 | tf_op jit(solution)/shard_map/ppermute | solution.py:101
  428.1 51.4 %collective-permute-start.14 = (f32[1,128,128]{2,1,0:T(8,128)S(1)}, f32[1,128,128]{2,1,0:T(8,128)S(1)}, u32[]{:S(2)}, u32[]{:S(2)}) collective-permute-start(f32[1,128,128]{2,1,0:T(8,128)S(1)} %get-tuple-element.19), channel_id=1, source_target_pairs={{0,40},{8,48},{16,56},{24,64},{32,72},{40,80},{48,88},{56,96},{64,... | collective-permute-start | bytes 196616 | tf_op jit(solution)/shard_map/ppermute | solution.py:101
  465.0 15.8 %collective-permute-start.15 = (f32[1,128,128]{2,1,0:T(8,128)S(1)}, f32[1,128,128]{2,1,0:T(8,128)S(1)}, u32[]{:S(2)}, u32[]{:S(2)}) collective-permute-start(f32[1,128,128]{2,1,0:T(8,128)S(1)} %get-tuple-element.18), channel_id=1, source_target_pairs={{0,48},{8,56},{16,64},{24,72},{32,80},{40,88},{48,96},{56,104},{64... | collective-permute-start | bytes 196616 | tf_op jit(solution)/shard_map/ppermute | solution.py:101
  474.4 10.7 %collective-permute-start.16 = (f32[1,128,128]{2,1,0:T(8,128)S(1)}, f32[1,128,128]{2,1,0:T(8,128)S(1)}, u32[]{:S(2)}, u32[]{:S(2)}) collective-permute-start(f32[1,128,128]{2,1,0:T(8,128)S(1)} %get-tuple-element.17), channel_id=1, source_target_pairs={{0,56},{8,64},{16,72},{24,80},{32,88},{40,96},{48,104},{56,112},{6... | collective-permute-start | bytes 196616 | tf_op jit(solution)/shard_map/ppermute | solution.py:101
  474.4 12.7 %collective-permute-start.17 = (f32[1,128,128]{2,1,0:T(8,128)S(1)}, f32[1,128,128]{2,1,0:T(8,128)S(1)}, u32[]{:S(2)}, u32[]{:S(2)}) collective-permute-start(f32[1,128,128]{2,1,0:T(8,128)S(1)} %get-tuple-element.16), channel_id=1, source_target_pairs={{0,64},{8,72},{16,80},{24,88},{32,96},{40,104},{48,112},{56,120},{... | collective-permute-start | bytes 196616 | tf_op jit(solution)/shard_map/ppermute | solution.py:101
  475.6 11.6 %collective-permute-start.18 = (f32[1,128,128]{2,1,0:T(8,128)S(1)}, f32[1,128,128]{2,1,0:T(8,128)S(1)}, u32[]{:S(2)}, u32[]{:S(2)}) collective-permute-start(f32[1,128,128]{2,1,0:T(8,128)S(1)} %get-tuple-element.15), channel_id=1, source_target_pairs={{0,72},{8,80},{16,88},{24,96},{32,104},{40,112},{48,120},{56,0},{6... | collective-permute-start | bytes 196616 | tf_op jit(solution)/shard_map/ppermute | solution.py:101
  480.8 11.4 %collective-permute-start.20 = (f32[1,128,128]{2,1,0:T(8,128)S(1)}, f32[1,128,128]{2,1,0:T(8,128)S(1)}, u32[]{:S(2)}, u32[]{:S(2)}) collective-permute-start(f32[1,128,128]{2,1,0:T(8,128)S(1)} %get-tuple-element.13), channel_id=1, source_target_pairs={{0,88},{8,96},{16,104},{24,112},{32,120},{40,0},{48,8},{56,16},{64... | collective-permute-start | bytes 196616 | tf_op jit(solution)/shard_map/ppermute | solution.py:101
  (16 other events, 316.2 us)
